TPU v7x, 256 devices: a whole 4x4x8 slice. The times are simulated.
256 devices in a mesh: day: 8 (over x, core), row: 32 (over y, z).
Axes of the slice: x: 4, y: 4, z: 8, core: 2. Of those that a mesh axis runs over, the one named last changes fastest.
Arguments:
- features: bfloat16 [8, 768, 16, 128, 128], P('day', 'row'), may hold values from -6 to 6
- blocks: int32 [8, 768, 16], P('day', 'row'), may hold values from 0 to 255, as said below
- labels: int32 [8, 768, 128], P('day', 'row'), may hold values from 0 to 15
- coef: float32 [8, 16, 32768], P('day', None, 'row'), may hold values from -0.125 to 0.125
- direction: float32 [8, 16, 32768], P('day', None, 'row'), may hold values from -0.125 to 0.125
- prior: float32 [32768], P('row'), may hold values from 100 to 3000
Outputs:
- gradient: float32 [8, 16, 32768], P('day', None, 'row')
- hess_dir: float32 [8, 16, 32768], P('day', None, 'row')
Inputs may be any that keep to these rules, and one draw needn't show every extreme that they name: `blocks`: within one row tile the 16 block numbers are distinct.
All inputs are finite; a program needn't handle non-finite values.
Results may differ from a plain program's by a relative error of at most 0.0003.
Values may be sent and summed in bfloat16 or wider, within the bound.
No kernel may reach another device: no remote copies, remote signals or barrier semaphores. Data moves between devices by JAX's collectives and lax.ppermute only.
A program may use at most 64 MiB of HBM per device.

v0:
```python
import jax
import jax.numpy as jnp
from jax import lax
from jax.sharding import Mesh
from jax.sharding import PartitionSpec as P

ROW = ("row_0", "row_1")


def copy_for_each(value, axis):
    copies = jnp.broadcast_to(value, (lax.axis_size(axis), *value.shape))
    return lax.all_to_all(copies, axis, split_axis=0, concat_axis=0, tiled=True)


def laid_out(parts, dim):
    shape = list(parts.shape[1:])
    shape[dim] *= parts.shape[0]
    return jnp.moveaxis(parts, 0, dim).reshape(shape)


def collect(value, axis, dim):
    parts = copy_for_each(value, axis)
    return laid_out(parts, dim)


def extended(cells, sides, width):
    for axis, dim in sides:
        count = lax.axis_size(axis)
        ends = count - 1
        head = lax.slice_in_dim(cells, 0, width, axis=dim)
        tail = lax.slice_in_dim(cells, cells.shape[dim] - width, cells.shape[dim], axis=dim)
        cells = jnp.concatenate(
            [
                lax.ppermute(tail, axis, [(i, (i + 1) % count) for i in range(ends)]),
                cells,
                lax.ppermute(head, axis, [((i + 1) % count, i) for i in range(ends)]),
            ],
            axis=dim,
        )
    return cells


def scatter_axes(value, axes, dim):
    if not axes:
        return value
    nearer = lax.psum_scatter(value, axes[0], scatter_dimension=dim, tiled=True)
    return scatter_axes(nearer, axes[1:], dim)


def on_device(features, blocks, labels, coef, direction, prior):
    arms = coef.shape[1]
    width = features.shape[-1]
    coef_pair = jnp.concatenate([coef[0], direction[0]], axis=0).astype(jnp.bfloat16)
    coef_table = collect(coef_pair, ROW, 1)
    nfeat = coef_table.shape[1]
    both = jnp.concatenate([coef, direction], axis=1)
    neighbours = extended(both, (("day", 0),), 1)
    blks = blocks[0]
    selected = coef_table.reshape(2 * arms, nfeat // width, width)[:, blks]
    feats = features[0]
    logits_dir = jnp.einsum("tari,ktai->tkr", feats, selected, preferred_element_type=jnp.float32)
    logits = logits_dir[:, :arms]
    lin_dir = logits_dir[:, arms:]
    expo = jnp.exp(logits)
    probs = expo / jnp.sum(expo, axis=1, keepdims=True)
    onehot = (labels[0][:, None, :] == jnp.arange(arms, dtype=jnp.int32)[None, :, None]).astype(
        jnp.float32
    )
    resid = probs - onehot
    hrow = probs * lin_dir - probs * jnp.sum(probs * lin_dir, axis=1, keepdims=True)
    both_low = jnp.concatenate([resid, hrow], axis=1).astype(jnp.bfloat16)
    contrib = jnp.einsum("tari,tkr->ktai", feats, both_low, preferred_element_type=jnp.float32)
    partial_terms = jnp.zeros((2 * arms, nfeat // width, width), jnp.float32)
    partial_terms = partial_terms.at[:, blks.reshape(-1)].add(contrib.reshape(2 * arms, -1, width))
    partial_terms = partial_terms.reshape(2 * arms, nfeat)
    owned = scatter_axes(partial_terms, ROW, 1)
    day_index = lax.axis_index("day")
    ndays = lax.axis_size("day")
    links = (day_index > 0).astype(jnp.float32) + (day_index < ndays - 1).astype(jnp.float32)
    coupling = links * neighbours[1] - neighbours[0] - neighbours[2]
    result = owned + prior[None, :] * coupling
    return (result[None, :arms], result[None, arms:])


def solution(mesh):
    finer = Mesh(mesh.devices.reshape(mesh.shape["day"], 4, 8), ("day", "row_0", "row_1"))
    return jax.shard_map(
        on_device,
        mesh=finer,
        in_specs=(
            P("day", ROW, None, None, None),
            P("day", ROW, None),
            P("day", ROW, None),
            P("day", None, ROW),
            P("day", None, ROW),
            P(ROW),
        ),
        out_specs=(P("day", None, ROW), P("day", None, ROW)),
        check_vma=False,
    )
```

profile of v0, /device:TPU:2, one launch (start us, length us, event | category | flops | bytes accessed | tf_op | source)
XLA Modules:
  0.0 259.7 jit_solution(9348575013162641782)
XLA Ops:
  7.2 0.0 copy-start
  7.2 0.9 constant_dynamic-update-slice_fusion.1
  8.1 0.9 constant_dynamic-update-slice_fusion
  9.0 1.6 broadcast_in_dim.9
  10.7 11.5 %all-to-all-start = ((bf16[32,32,1024]{2,1,0:T(8,128)(2,1)}), bf16[32,32,1024]{2,1,0:T(8,128)(2,1)S(1)}, u32[]{:S(2)}, u32[]{:S(2)}) async-start(bf16[32,32,1024]{2,1,0:T(8,128)(2,1)} %broadcast_in_dim.9), calls=%async_computation | async-start | bytes 4194304 | tf_op jit(solution)/shard_map/all_to_all | solution.py:12
  22.2 0.0 reduce-scatter.3.cloned.1.call-start
  22.2 0.0 copy-done
  22.2 0.1 copy.12
  22.3 0.1 copy.14
  22.4 0.1 reshape.78
  22.4 0.1 reshape_squeeze.3
  22.6 49.6 %all-to-all-done = bf16[32,32,1024]{2,1,0:T(8,128)(2,1)S(1)} async-done(((bf16[32,32,1024]{2,1,0:T(8,128)(2,1)}), bf16[32,32,1024]{2,1,0:T(8,128)(2,1)S(1)}, u32[]{:S(2)}, u32[]{:S(2)}) %all-to-all-start) | async-done | bytes 2097184 | tf_op jit(solution)/shard_map/all_to_all | solution.py:12
  72.2 2.5 copy.13
  74.7 4.2 %reshape_reshape.3 = bf16[32,256,128]{2,1,0:T(8,128)(2,1)} reshape(bf16[32,32,1024]{2,1,0:T(8,128)(2,1)} %copy.13) | data formatting | bytes 4194304 | tf_op jit(solution)/shard_map/reshape;reshape | solution.py:59
  78.9 2.9 %copy.15 = bf16[32,256,128]{2,0,1:T(8,128)(2,1)S(1)} copy(bf16[32,256,128]{2,1,0:T(8,128)(2,1)} %reshape_reshape.3) | data formatting | bytes 4194304 | tf_op jit(solution)/shard_map/reshape;reshape | solution.py:59
  81.8 3.2 %gather_fusion = bf16[384,32,128]{2,1,0:T(8,128)(2,1)} fusion(bf16[32,256,128]{2,0,1:T(8,128)(2,1)S(1)} %copy.15, s32[1024]{0:T(1024)S(1)} %pad_clamp_fusion), kind=kCustom, calls=%fused_computation | custom fusion | bytes 6292992 | tf_op jit(solution)/shard_map/gather | solution.py:59
  85.0 0.0 copy-start.2
  85.0 9.7 %fusion.6 = f32[24,32,128]{2,1,0:T(8,128)S(1)} fusion(bf16[32,24,16,128]{3,0,2,1:T(8,128)(2,1)} %bitcast.48, bf16[1,24,16,128,128]{4,3,2,1,0:T(8,128)(2,1)} %param.6), kind=kOutput, calls=%fused_computation.9 | convolution fusion | flops 402653184 | bytes 16121856 | tf_op jit(solution)/shard_map/tari,ktai->tkr/dot_general | solution.py:61
  94.7 0.0 copy-done.2
  94.7 0.8 subtract_convert_fusion
  95.5 0.1 fusion.12
  95.5 9.0 %fusion.2 = f32[24,32,16,128]{3,1,2,0:T(8,128)} fusion(bf16[1,24,16,128,128]{4,3,2,1,0:T(8,128)(2,1)} %param.6, bf16[24,16,128]{2,1,0:T(8,128)(2,1)S(1)} %fusion.12, bf16[24,16,128]{2,1,0:T(8,128)(2,1)S(1)} %get-tuple-element.8), kind=kOutput, calls=%fused_computation.4 | convolution fusion | flops 403046400 | bytes 19070976 | tf_op jit(solution)/shard_map/tari,tkr->ktai/dot_general | solution.py:72
  104.5 2.6 broadcast_in_dim.8
  107.1 51.2 %scatter_fusion = f32[32,256,128]{2,0,1:T(8,128)} fusion(f32[32,256,128]{2,0,1:T(8,128)} %broadcast_in_dim.8, s32[384]{0:T(512)S(1)} %fusion.18, f32[384,32,128]{2,1,0:T(8,128)} %bitcast.47), kind=kCustom, calls=%fused_computation.1 | custom fusion | flops 1572864 | bytes 18875904 | tf_op jit(solution)/shard_map/scatter-add | solution.py:74
  158.3 4.4 %copy_bitcast_fusion = f32[32,32768]{1,0:T(8,128)} fusion(f32[32,256,128]{2,0,1:T(8,128)} %scatter_fusion), kind=kLoop, calls=%fused_computation.8 | loop fusion | bytes 8388608 | tf_op jit(solution)/shard_map/reshape | solution.py:75
  162.7 0.0 copy-start.1
  162.7 0.0 reduce-scatter.3.cloned.1.call-update
  162.7 0.0 reduce-scatter.5.cloned.1.call-start
  162.8 47.1 %reduce-scatter.3.cloned.1.call-done = f32[32,8192]{1,0:T(8,128)} async-done(((f32[32,32768]{1,0:T(8,128)}), f32[32,8192]{1,0:T(8,128)}) %reduce-scatter.3.cloned.1.call-update) | async-done | bytes 1048592 | tf_op jit(solution)/shard_map/reduce_scatter | solution.py:46
  209.9 0.0 reduce-scatter.5.cloned.1.call-update
  209.9 1.9 collective-permute-start
  211.8 3.6 %collective-permute-start.1 = (f32[1,32,1024]{2,1,0:T(8,128)S(1)}, f32[1,32,1024]{2,1,0:T(8,128)S(1)}, u32[]{:S(2)}, u32[]{:S(2)}) collective-permute-start(f32[1,32,1024]{2,1,0:T(8,128)S(1)} %get-tuple-element.4), channel_id=1, source_target_pairs={{32,0},{64,32},{96,64},{128,96},{160,128},{192,160},{224,192},{33,... | collective-permute-start | bytes 393224 | tf_op jit(solution)/shard_map/ppermute | solution.py:36
  215.5 0.7 collective-permute-done
  216.2 1.8 collective-permute-done.1
  218.0 33.2 %reduce-scatter.5.cloned.1.call-done = f32[32,1024]{1,0:T(8,128)} async-done(((f32[32,8192]{1,0:T(8,128)}), f32[32,1024]{1,0:T(8,128)}) %reduce-scatter.5.cloned.1.call-update) | async-done | bytes 131088 | tf_op jit(solution)/shard_map/reduce_scatter | solution.py:46
  251.2 0.0 copy-done.1
  251.2 0.9 fusion.17
  252.2 0.7 slice_bitcast_fusion
  (4 shorter events, 0.0 us)
Async XLA Ops:
  7.2 15.0 %copy-start = (s32[1,24,16]{1,2,0:T(8,128)S(1)}, s32[1,24,16]{1,2,0:T(8,128)}, u32[]{:S(2)}) copy-start(s32[1,24,16]{1,2,0:T(8,128)} %param.7) | copy-start | bytes 4612
  10.7 61.5 %all-to-all-start = ((bf16[32,32,1024]{2,1,0:T(8,128)(2,1)}), bf16[32,32,1024]{2,1,0:T(8,128)(2,1)S(1)}, u32[]{:S(2)}, u32[]{:S(2)}) async-start(bf16[32,32,1024]{2,1,0:T(8,128)(2,1)} %broadcast_in_dim.9), calls=%async_computation | async-start | bytes 4194304 | tf_op jit(solution)/shard_map/all_to_all | solution.py:12
  22.2 187.7 %reduce-scatter.3.cloned.1.call-start = ((), (), s32[]{:S(2)}) async-start(), calls=%async_computation.3 | async-start | bytes 5242880 | tf_op jit(solution)/shard_map/reduce_scatter | solution.py:46
  85.0 9.7 %copy-start.2 = (s32[1,24,128]{2,1,0:T(8,128)S(1)}, s32[1,24,128]{2,1,0:T(8,128)}, u32[]{:S(2)}) copy-start(s32[1,24,128]{2,1,0:T(8,128)} %param.8) | copy-start | bytes 36868
  162.7 88.5 %copy-start.1 = (f32[1024]{0:T(1024)S(1)}, f32[1024]{0:T(1024)}, u32[]{:S(2)}) copy-start(f32[1024]{0:T(1024)} %param.11) | copy-start | bytes 12292
  162.7 88.5 %reduce-scatter.5.cloned.1.call-start = ((), (), s32[]{:S(2)}) async-start(), calls=%async_computation.4 | async-start | bytes 1179648 | tf_op jit(solution)/shard_map/reduce_scatter | solution.py:46
  209.9 6.3 %collective-permute-start = (f32[1,32,1024]{2,1,0:T(8,128)S(1)}, f32[1,32,1024]{2,1,0:T(8,128)S(1)}, u32[]{:S(2)}, u32[]{:S(2)}) collective-permute-start(f32[1,32,1024]{2,1,0:T(8,128)S(1)} %get-tuple-element.4), channel_id=1, source_target_pairs={{0,32},{32,64},{64,96},{96,128},{128,160},{160,192},{192,224},{1,3... | collective-permute-start | bytes 393224 | tf_op jit(solution)/shard_map/ppermute | solution.py:34
  211.8 6.1 %collective-permute-start.1 = (f32[1,32,1024]{2,1,0:T(8,128)S(1)}, f32[1,32,1024]{2,1,0:T(8,128)S(1)}, u32[]{:S(2)}, u32[]{:S(2)}) collective-permute-start(f32[1,32,1024]{2,1,0:T(8,128)S(1)} %get-tuple-element.4), channel_id=1, source_target_pairs={{32,0},{64,32},{96,64},{128,96},{160,128},{192,160},{224,192},{33,... | collective-permute-start | bytes 393224 | tf_op jit(solution)/shard_map/ppermute | solution.py:36
Sparse Core Ops, SparseCore 0:
  162.9 46.9 reduce-scatter.2
  212.4 38.7 reduce-scatter.4
where the time goes:
time: 261 us; the launch traced here: 260 us
  waiting for transfers between devices  132 us (51%)
  other arithmetic  54.9 us (21%)
  local copies, waits for them, and re-layouts  22.3 us (9%)
  matrix products  18.7 us (7%)
  starting transfers between devices  17.1 us (7%)
  between operations  14.1 us (5%)
    reduce_scatter x2, waiting for transfers between devices, scatter_axes(): nearer = lax.psum_scatter(value, axes[0], scatter_dimension=dim, tiled=True)  80.3 us
    scatter-add x1, other arithmetic, on_device(): partial_terms.at[:, blks.reshape(-1)]  51.2 us
    all_to_all x1, waiting for transfers between devices, copy_for_each(): return lax.all_to_all(copies, axis, split_axis=0, concat_axis=0, tiled=True)  49.6 us
    all_to_all x1, starting transfers between devices, copy_for_each(): return lax.all_to_all(copies, axis, split_axis=0, concat_axis=0, tiled=True)  11.5 us
    dot_general x1, matrix products, on_device(): jnp.einsum('tari,ktai->tkr', feats, selected, preferred_element_type=jnp....  9.68 us
    dot_general x1, matrix products, on_device(): jnp.einsum('tari,tkr->ktai', feats, both_low, preferred_element_type=jnp....  9.01 us
    another operation x2, local copies, waits for them, and re-layouts, on_device(): selected = coef_table.reshape(2 * arms, nfeat // width, width)[:, blks]  7.12 us
  transfers between devices with their start and end apart: 5, of which 5 were waited for; matrix products, arithmetic and copies ran while one was open for 0% of the time, Pallas kernels for 0%

commit v1 on v0

--- a/solution.py
+++ b/solution.py
@@ -5,22 +5,6 @@
 from jax.sharding import PartitionSpec as P
 
 ROW = ("row_0", "row_1")
-
-
-def copy_for_each(value, axis):
-    copies = jnp.broadcast_to(value, (lax.axis_size(axis), *value.shape))
-    return lax.all_to_all(copies, axis, split_axis=0, concat_axis=0, tiled=True)
-
-
-def laid_out(parts, dim):
-    shape = list(parts.shape[1:])
-    shape[dim] *= parts.shape[0]
-    return jnp.moveaxis(parts, 0, dim).reshape(shape)
-
-
-def collect(value, axis, dim):
-    parts = copy_for_each(value, axis)
-    return laid_out(parts, dim)
 
 
 def extended(cells, sides, width):
@@ -40,23 +24,17 @@
     return cells
 
 
-def scatter_axes(value, axes, dim):
-    if not axes:
-        return value
-    nearer = lax.psum_scatter(value, axes[0], scatter_dimension=dim, tiled=True)
-    return scatter_axes(nearer, axes[1:], dim)
-
-
 def on_device(features, blocks, labels, coef, direction, prior):
     arms = coef.shape[1]
     width = features.shape[-1]
     coef_pair = jnp.concatenate([coef[0], direction[0]], axis=0).astype(jnp.bfloat16)
-    coef_table = collect(coef_pair, ROW, 1)
+    coef_table = lax.all_gather(coef_pair, ROW, axis=1, tiled=True)
     nfeat = coef_table.shape[1]
+    nblk = nfeat // width
     both = jnp.concatenate([coef, direction], axis=1)
     neighbours = extended(both, (("day", 0),), 1)
     blks = blocks[0]
-    selected = coef_table.reshape(2 * arms, nfeat // width, width)[:, blks]
+    selected = coef_table.reshape(2 * arms, nblk, width)[:, blks]
     feats = features[0]
     logits_dir = jnp.einsum("tari,ktai->tkr", feats, selected, preferred_element_type=jnp.float32)
     logits = logits_dir[:, :arms]
@@ -69,11 +47,20 @@
     resid = probs - onehot
     hrow = probs * lin_dir - probs * jnp.sum(probs * lin_dir, axis=1, keepdims=True)
     both_low = jnp.concatenate([resid, hrow], axis=1).astype(jnp.bfloat16)
-    contrib = jnp.einsum("tari,tkr->ktai", feats, both_low, preferred_element_type=jnp.float32)
-    partial_terms = jnp.zeros((2 * arms, nfeat // width, width), jnp.float32)
-    partial_terms = partial_terms.at[:, blks.reshape(-1)].add(contrib.reshape(2 * arms, -1, width))
+    contrib = jnp.einsum("tari,tkr->taki", feats, both_low, preferred_element_type=jnp.float32)
+    contrib = contrib.reshape(-1, 2 * arms, width)
+    top = lax.reduce_precision(contrib, exponent_bits=8, mantissa_bits=7)
+    hi = top.astype(jnp.bfloat16)
+    lo = (contrib - top).astype(jnp.bfloat16)
+    place = (blks.reshape(-1)[:, None] == jnp.arange(nblk, dtype=jnp.int32)[None, :]).astype(
+        jnp.bfloat16
+    )
+    parts = jnp.einsum(
+        "pb,pjki->jkbi", place, jnp.stack([hi, lo], axis=1), preferred_element_type=jnp.float32
+    )
+    partial_terms = parts[0] + parts[1]
     partial_terms = partial_terms.reshape(2 * arms, nfeat)
-    owned = scatter_axes(partial_terms, ROW, 1)
+    owned = lax.psum_scatter(partial_terms, ROW, scatter_dimension=1, tiled=True)
     day_index = lax.axis_index("day")
     ndays = lax.axis_size("day")
     links = (day_index > 0).astype(jnp.float32) + (day_index < ndays - 1).astype(jnp.float32)

time: 261 us -> 375 us (1.44)
  waiting for transfers between devices: 132 us -> 296 us
  other arithmetic: 54.9 us -> 12 us
  starting transfers between devices: 17.1 us -> 5.64 us
    reduce_scatter x2 -> x1, waiting for transfers between devices: 80.3 us -> 212 us  [on_device(): lax.psum_scatter(partial_terms, ROW, scatter_dimension=1, tiled=True)]
    all_gather x0 -> x1, waiting for transfers between devices: none -> 80.7 us  [on_device(): coef_table = lax.all_gather(coef_pair, ROW, axis=1, tiled=True)]
    scatter-add x1 -> x0, other arithmetic: 51.2 us -> none  [on_device(): partial_terms.at[:, blks.reshape(-1)]]
    all_to_all x1 -> x0, waiting for transfers between devices: 49.6 us -> none  [copy_for_each(): return lax.all_to_all(copies, axis, split_axis=0, concat_axis=0, tiled=True)]
    all_to_all x1 -> x0, starting transfers between devices: 11.5 us -> none  [copy_for_each(): return lax.all_to_all(copies, axis, split_axis=0, concat_axis=0, tiled=True)]
    unnamed x7 -> x6, local copies, waits for them, and re-layouts: 0.08 us -> 7.37 us
    another operation x3 -> x0, local copies, waits for them, and re-layouts: 7.2 us -> none  [the longest x2 7.12 us: on_device(): selected = coef_table.reshape(2 * arms, nfeat // width, width)[:, blks]]
    add x0 -> x1, local copies, waits for them, and re-layouts: none -> 5.57 us  [on_device(): partial_terms = parts[0] + parts[1]]
  transfers between devices with their start and end apart: 5 -> 4, of which waited for: 5 -> 4; matrix products, arithmetic and copies ran while one was open for 0% -> 0% of each run, Pallas kernels for 0% -> 0%
where the time goes in v1:
time: 375 us; the launch traced here: 374 us
  waiting for transfers between devices  296 us (79%)
  local copies, waits for them, and re-layouts  25.5 us (7%)
  matrix products  21.1 us (6%)
  between operations  14.1 us (4%)
  other arithmetic  12 us (3%)
  starting transfers between devices  5.64 us (2%)
    reduce_scatter x1, waiting for transfers between devices, on_device(): lax.psum_scatter(partial_terms, ROW, scatter_dimension=1, tiled=True)  212 us
    all_gather x1, waiting for transfers between devices, on_device(): coef_table = lax.all_gather(coef_pair, ROW, axis=1, tiled=True)  80.7 us
    dot_general x1, matrix products, on_device(): jnp.einsum('tari,ktai->tkr', feats, selected, preferred_element_type=jnp....  9.67 us
    dot_general x1, matrix products, on_device(): jnp.einsum('tari,tkr->taki', feats, both_low, preferred_element_type=jnp....  9.02 us
  transfers between devices with their start and end apart: 4, of which 4 were waited for; matrix products, arithmetic and copies ran while one was open for 0% of the time, Pallas kernels for 0%

profile of v1, /device:TPU:2, one launch (start us, length us, event | category | flops | bytes accessed | tf_op | source)
XLA Modules:
  0.0 374.1 jit_solution(4076354408150905320)
XLA Ops:
  7.2 0.0 all-gather.2.cloned.1.call-start
  7.2 0.9 constant_dynamic-update-slice_fusion.1
  8.1 0.9 constant_dynamic-update-slice_fusion
  9.1 0.6 pad_maximum_fusion
  9.7 0.0 all-gather.2.cloned.1.call-update
  9.7 0.0 reduce-scatter.2.cloned.1.call-start
  9.8 0.8 copy.20
  10.5 0.7 compare_select_fusion
  11.2 0.1 copy.16
  11.3 0.1 reshape.84
  11.4 0.1 eq.34
  11.5 80.7 %all-gather.2.cloned.1.call-done = bf16[32,32768]{1,0:T(8,128)(2,1)} async-done(((bf16[32,1024]{1,0:T(8,128)(2,1)}), bf16[32,32768]{1,0:T(8,128)(2,1)}) %all-gather.2.cloned.1.call-update) | async-done | bytes 2097168 | tf_op jit(solution)/shard_map/all_gather | solution.py:31
  92.2 2.0 copy_bitcast_fusion.1
  94.2 3.2 gather_fusion
  97.4 0.0 copy-start.1
  97.4 9.7 %fusion.14 = f32[24,32,128]{2,1,0:T(8,128)S(1)} fusion(bf16[32,24,16,128]{3,0,2,1:T(8,128)(2,1)} %bitcast.59, bf16[1,24,16,128,128]{4,3,2,1,0:T(8,128)(2,1)} %param.6), kind=kOutput, calls=%fused_computation.18 | convolution fusion | flops 402653184 | bytes 16121856 | tf_op jit(solution)/shard_map/tari,ktai->tkr/dot_general | solution.py:39
  107.0 0.0 copy-done.1
  107.0 0.8 subtract_convert_fusion
  107.8 0.1 fusion.20
  107.9 9.0 %fusion.2 = f32[24,32,16,128]{3,1,2,0:T(8,128)} fusion(bf16[1,24,16,128,128]{4,3,2,1,0:T(8,128)(2,1)} %param.6, bf16[24,16,128]{2,1,0:T(8,128)(2,1)S(1)} %fusion.20, bf16[24,16,128]{2,1,0:T(8,128)(2,1)S(1)} %get-tuple-element.10), kind=kOutput, calls=%fused_computation.3 | convolution fusion | flops 403046400 | bytes 19070976 | tf_op jit(solution)/shard_map/tari,tkr->taki/dot_general | solution.py:50
  116.9 6.6 %copy.18 = f32[384,1,32,128]{0,3,2,1:T(8,128)} copy(f32[384,1,32,128]{3,2,0,1:T(8,128)} %bitcast.56) | data formatting | bytes 12582912 | tf_op jit(solution)/shard_map/reshape | solution.py:51
  123.5 4.3 %reduce-precision_convert_fusion = (bf16[384,1,32,128]{0,3,2,1:T(8,128)(2,1)S(1)}, bf16[384,1,32,128]{0,3,2,1:T(8,128)(2,1)S(1)}) fusion(f32[384,1,32,128]{0,3,2,1:T(8,128)} %copy.18), kind=kLoop, calls=%fused_computation.8 | loop fusion | flops 6291456 | bytes 12582912 | tf_op jit(solution)/shard_map/convert_element_type | solution.py:53
  127.7 2.5 fusion.11
  130.2 2.8 slice_add_fusion
  132.9 5.6 %copy.21 = f32[1,32,256,128]{3,2,1,0:T(8,128)} copy(f32[1,32,256,128]{2,3,1,0:T(8,128)} %slice_add_fusion) | data formatting | bytes 8388608 | tf_op jit(solution)/shard_map/add | solution.py:61
  138.5 6.6 %copy.29 = f32[4,8,256,128]{3,1,2,0:T(8,128)} copy(f32[4,8,256,128]{3,2,1,0:T(8,128)} %bitcast.58) | data formatting | bytes 8388608
  145.1 0.0 copy-start
  145.1 0.0 reduce-scatter.2.cloned.1.call-update
  145.1 1.9 collective-permute-start
  147.1 3.6 collective-permute-start.1
  150.7 0.7 collective-permute-done
  151.4 1.8 collective-permute-done.1
  153.2 212.5 %reduce-scatter.2.cloned.1.call-done = f32[32,1024]{1,0:T(8,128)} async-done(((f32[32,32768]{1,0:T(8,128)}), f32[32,1024]{1,0:T(8,128)}) %reduce-scatter.2.cloned.1.call-update) | async-done | bytes 131088 | tf_op jit(solution)/shard_map/reduce_scatter | solution.py:63
  365.7 0.0 copy-done
  365.7 0.9 fusion.28
  366.6 0.7 slice_bitcast_fusion
  (1 shorter events, 0.0 us)
Async XLA Ops:
  7.2 85.1 %all-gather.2.cloned.1.call-start = ((), (), s32[]{:S(2)}) async-start(), calls=%async_computation.1 | async-start | bytes 2162688 | tf_op jit(solution)/shard_map/all_gather | solution.py:31
  9.7 355.9 %reduce-scatter.2.cloned.1.call-start = ((), (), s32[]{:S(2)}) async-start(), calls=%async_computation.2 | async-start | bytes 4325376 | tf_op jit(solution)/shard_map/reduce_scatter | solution.py:63
  97.4 9.7 %copy-start.1 = (s32[1,24,128]{2,1,0:T(8,128)S(1)}, s32[1,24,128]{2,1,0:T(8,128)}, u32[]{:S(2)}) copy-start(s32[1,24,128]{2,1,0:T(8,128)} %param.8) | copy-start | bytes 36868
  145.1 220.6 %copy-start = (f32[1024]{0:T(1024)S(1)}, f32[1024]{0:T(1024)}, u32[]{:S(2)}) copy-start(f32[1024]{0:T(1024)} %param.11) | copy-start | bytes 12292
  145.1 6.3 %collective-permute-start = (f32[1,32,1024]{2,1,0:T(8,128)S(1)}, f32[1,32,1024]{2,1,0:T(8,128)S(1)}, u32[]{:S(2)}, u32[]{:S(2)}) collective-permute-start(f32[1,32,1024]{2,1,0:T(8,128)S(1)} %get-tuple-element.6), channel_id=1, source_target_pairs={{0,32},{32,64},{64,96},{96,128},{128,160},{160,192},{192,224},{1,3... | collective-permute-start | bytes 393224 | tf_op jit(solution)/shard_map/ppermute | solution.py:18
  147.1 6.1 %collective-permute-start.1 = (f32[1,32,1024]{2,1,0:T(8,128)S(1)}, f32[1,32,1024]{2,1,0:T(8,128)S(1)}, u32[]{:S(2)}, u32[]{:S(2)}) collective-permute-start(f32[1,32,1024]{2,1,0:T(8,128)S(1)} %get-tuple-element.6), channel_id=1, source_target_pairs={{32,0},{64,32},{96,64},{128,96},{160,128},{192,160},{224,192},{33,... | collective-permute-start | bytes 393224 | tf_op jit(solution)/shard_map/ppermute | solution.py:20
Sparse Core Ops, SparseCore 0:
  11.1 81.0 all-gather.1
  145.3 220.3 reduce-scatter.1

commit v2 on v1

--- a/solution.py
+++ b/solution.py
@@ -5,6 +5,11 @@
 from jax.sharding import PartitionSpec as P
 
 ROW = ("row_0", "row_1")
+
+
+def copy_for_each(value, axis):
+    copies = jnp.broadcast_to(value, (lax.axis_size(axis), *value.shape))
+    return lax.all_to_all(copies, axis, split_axis=0, concat_axis=0, tiled=True)
 
 
 def extended(cells, sides, width):
@@ -24,19 +29,28 @@
     return cells
 
 
+def scatter_axes(value, axes, dim):
+    if not axes:
+        return value
+    nearer = lax.psum_scatter(value, axes[0], scatter_dimension=dim, tiled=True)
+    return scatter_axes(nearer, axes[1:], dim)
+
+
 def on_device(features, blocks, labels, coef, direction, prior):
     arms = coef.shape[1]
     width = features.shape[-1]
     coef_pair = jnp.concatenate([coef[0], direction[0]], axis=0).astype(jnp.bfloat16)
-    coef_table = lax.all_gather(coef_pair, ROW, axis=1, tiled=True)
-    nfeat = coef_table.shape[1]
-    nblk = nfeat // width
+    local_blk = coef_pair.shape[1] // width
+    by_block = coef_pair.reshape(2 * arms, local_blk, width).transpose(1, 0, 2)
+    parts = copy_for_each(by_block, ROW)
+    coef_table = parts.reshape(-1, 2 * arms, width)
+    nblk = coef_table.shape[0]
     both = jnp.concatenate([coef, direction], axis=1)
     neighbours = extended(both, (("day", 0),), 1)
     blks = blocks[0]
-    selected = coef_table.reshape(2 * arms, nblk, width)[:, blks]
+    selected = coef_table[blks]
     feats = features[0]
-    logits_dir = jnp.einsum("tari,ktai->tkr", feats, selected, preferred_element_type=jnp.float32)
+    logits_dir = jnp.einsum("tari,taki->tkr", feats, selected, preferred_element_type=jnp.float32)
     logits = logits_dir[:, :arms]
     lin_dir = logits_dir[:, arms:]
     expo = jnp.exp(logits)
@@ -48,19 +62,19 @@
     hrow = probs * lin_dir - probs * jnp.sum(probs * lin_dir, axis=1, keepdims=True)
     both_low = jnp.concatenate([resid, hrow], axis=1).astype(jnp.bfloat16)
     contrib = jnp.einsum("tari,tkr->taki", feats, both_low, preferred_element_type=jnp.float32)
-    contrib = contrib.reshape(-1, 2 * arms, width)
+    contrib = contrib.reshape(-1, 2 * arms * width)
     top = lax.reduce_precision(contrib, exponent_bits=8, mantissa_bits=7)
     hi = top.astype(jnp.bfloat16)
     lo = (contrib - top).astype(jnp.bfloat16)
-    place = (blks.reshape(-1)[:, None] == jnp.arange(nblk, dtype=jnp.int32)[None, :]).astype(
+    place = (jnp.arange(nblk, dtype=jnp.int32)[:, None] == blks.reshape(-1)[None, :]).astype(
         jnp.bfloat16
     )
-    parts = jnp.einsum(
-        "pb,pjki->jkbi", place, jnp.stack([hi, lo], axis=1), preferred_element_type=jnp.float32
+    split = jnp.einsum(
+        "bp,jpc->jbc", place, jnp.stack([hi, lo], axis=0), preferred_element_type=jnp.float32
     )
-    partial_terms = parts[0] + parts[1]
-    partial_terms = partial_terms.reshape(2 * arms, nfeat)
-    owned = lax.psum_scatter(partial_terms, ROW, scatter_dimension=1, tiled=True)
+    partial_terms = (split[0] + split[1]).reshape(nblk, 2 * arms, width)
+    owned = scatter_axes(partial_terms, ROW, 0)
+    owned = owned.transpose(1, 0, 2).reshape(2 * arms, -1)
     day_index = lax.axis_index("day")
     ndays = lax.axis_size("day")
     links = (day_index > 0).astype(jnp.float32) + (day_index < ndays - 1).astype(jnp.float32)

time: 375 us -> 221 us (0.59)
  waiting for transfers between devices: 296 us -> 132 us
  starting transfers between devices: 5.64 us -> 17.1 us
    reduce_scatter x1 -> x2, waiting for transfers between devices: 212 us -> 80.3 us  [scatter_axes(): nearer = lax.psum_scatter(value, axes[0], scatter_dimension=dim, tiled=True)]
    all_gather x1 -> x0, waiting for transfers between devices: 80.7 us -> none  [on_device(): coef_table = lax.all_gather(coef_pair, ROW, axis=1, tiled=True)]
    all_to_all x0 -> x1, waiting for transfers between devices: none -> 49.7 us  [copy_for_each(): return lax.all_to_all(copies, axis, split_axis=0, concat_axis=0, tiled=True)]
    all_to_all x0 -> x1, starting transfers between devices: none -> 11.5 us  [copy_for_each(): return lax.all_to_all(copies, axis, split_axis=0, concat_axis=0, tiled=True)]
    unnamed x6 -> x9, local copies, waits for them, and re-layouts: 7.37 us -> 0.1 us
    reshape x2, local copies, waits for them, and re-layouts: 8.52 us -> 13.7 us  [on_device(): contrib = contrib.reshape(-1, 2 * arms * width)]
  transfers between devices with their start and end apart: 4 -> 5, of which waited for: 4 -> 5; matrix products, arithmetic and copies ran while one was open for 0% -> 0% of each run, Pallas kernels for 0% -> 0%
where the time goes in v2:
time: 221 us; the launch traced here: 220 us
  waiting for transfers between devices  132 us (60%)
  local copies, waits for them, and re-layouts  25.2 us (11%)
  matrix products  21.1 us (10%)
  starting transfers between devices  17.1 us (8%)
  between operations  14.2 us (6%)
  other arithmetic  9.9 us (4%)
    reduce_scatter x2, waiting for transfers between devices, scatter_axes(): nearer = lax.psum_scatter(value, axes[0], scatter_dimension=dim, tiled=True)  80.3 us
    all_to_all x1, waiting for transfers between devices, copy_for_each(): return lax.all_to_all(copies, axis, split_axis=0, concat_axis=0, tiled=True)  49.7 us
    reshape x2, local copies, waits for them, and re-layouts, on_device(): contrib = contrib.reshape(-1, 2 * arms * width)  13.7 us
    all_to_all x1, starting transfers between devices, copy_for_each(): return lax.all_to_all(copies, axis, split_axis=0, concat_axis=0, tiled=True)  11.5 us
    dot_general x1, matrix products, on_device(): jnp.einsum('tari,taki->tkr', feats, selected, preferred_element_type=jnp....  9.67 us
    dot_general x1, matrix products, on_device(): jnp.einsum('tari,tkr->taki', feats, both_low, preferred_element_type=jnp....  8.99 us
    add x1, local copies, waits for them, and re-layouts, on_device(): partial_terms = (split[0] + split[1]).reshape(nblk, 2 * arms, width)  5.49 us
  transfers between devices with their start and end apart: 5, of which 5 were waited for; matrix products, arithmetic and copies ran while one was open for 0% of the time, Pallas kernels for 0%

profile of v2, /device:TPU:2, one launch (start us, length us, event | category | flops | bytes accessed | tf_op | source)
XLA Modules:
  0.0 219.9 jit_solution(3601473675023156870)
XLA Ops:
  7.2 0.0 copy-start
  7.2 0.9 constant_dynamic-update-slice_fusion.1
  8.1 0.9 constant_dynamic-update-slice_fusion
  9.1 1.8 broadcast_in_dim.6
  10.9 11.5 %all-to-all-start = ((bf16[32,8,32,128]{3,2,1,0:T(8,128)(2,1)}), bf16[32,8,32,128]{3,2,1,0:T(8,128)(2,1)S(1)}, u32[]{:S(2)}, u32[]{:S(2)}) async-start(bf16[32,8,32,128]{3,2,1,0:T(8,128)(2,1)} %broadcast_in_dim.6), calls=%async_computation | async-start | bytes 4194304 | tf_op jit(solution)/shard_map/all_to_all | solution.py:12
  22.4 0.0 reduce-scatter.3.cloned.1.call-start
  22.5 0.0 copy-done
  22.5 0.1 copy.28
  22.6 0.1 copy.25
  22.6 0.1 reshape.95
  22.7 0.1 eq.35
  22.8 49.7 %all-to-all-done = bf16[32,8,32,128]{3,2,1,0:T(8,128)(2,1)S(1)} async-done(((bf16[32,8,32,128]{3,2,1,0:T(8,128)(2,1)}), bf16[32,8,32,128]{3,2,1,0:T(8,128)(2,1)S(1)}, u32[]{:S(2)}, u32[]{:S(2)}) %all-to-all-start) | async-done | bytes 2097184 | tf_op jit(solution)/shard_map/all_to_all | solution.py:12
  72.5 3.2 %gather_fusion = bf16[384,32,128]{2,1,0:T(8,128)(2,1)} fusion(bf16[256,32,128]{2,1,0:T(8,128)(2,1)S(1)} %bitcast.60, s32[1024]{0:T(1024)S(1)} %pad_clamp_fusion), kind=kCustom, calls=%fused_computation | custom fusion | bytes 6292992 | tf_op jit(solution)/shard_map/gather | solution.py:51
  75.6 0.0 copy-start.2
  75.6 9.7 %fusion.13 = f32[24,32,128]{2,1,0:T(8,128)S(1)} fusion(bf16[24,16,32,128]{3,2,1,0:T(8,128)(2,1)} %bitcast.61, bf16[1,24,16,128,128]{4,3,2,1,0:T(8,128)(2,1)} %param.6), kind=kOutput, calls=%fused_computation.16 | convolution fusion | flops 402653184 | bytes 16121856 | tf_op jit(solution)/shard_map/tari,taki->tkr/dot_general | solution.py:53
  85.3 0.0 copy-done.2
  85.3 0.8 subtract_convert_fusion
  86.1 0.1 fusion.19
  86.1 9.0 %fusion.10 = f32[24,16,32,128]{3,2,1,0:T(8,128)} fusion(bf16[1,24,16,128,128]{4,3,2,1,0:T(8,128)(2,1)} %param.6, bf16[24,16,128]{2,1,0:T(8,128)(2,1)S(1)} %fusion.19, bf16[24,16,128]{2,1,0:T(8,128)(2,1)S(1)} %get-tuple-element.10), kind=kOutput, calls=%fused_computation.15 | convolution fusion | flops 403046400 | bytes 19070976 | tf_op jit(solution)/shard_map/tari,tkr->taki/dot_general | solution.py:64
  95.1 7.2 %reshape.91 = f32[1,384,4096]{2,1,0:T(8,128)} reshape(f32[24,16,32,128]{3,2,1,0:T(8,128)} %fusion.10) | data formatting | bytes 12582912 | tf_op jit(solution)/shard_map/reshape | solution.py:65
  102.3 6.6 %copy.26 = f32[1,384,4096]{1,2,0:T(8,128)} copy(f32[1,384,4096]{2,1,0:T(8,128)} %reshape.91) | data formatting | bytes 12582912 | tf_op jit(solution)/shard_map/reshape | solution.py:65
  108.9 3.8 %reduce-precision_convert_fusion = (bf16[1,384,4096]{1,2,0:T(8,128)(2,1)S(1)}, bf16[1,384,4096]{1,2,0:T(8,128)(2,1)S(1)}) fusion(f32[1,384,4096]{1,2,0:T(8,128)} %copy.26), kind=kLoop, calls=%fused_computation.8 | loop fusion | flops 6291456 | bytes 12582912 | tf_op jit(solution)/shard_map/convert_element_type | solution.py:67
  112.6 2.4 %convolution_bitcast_fusion = f32[2,256,4096]{1,2,0:T(8,128)S(1)} fusion(bf16[1,384,4096]{1,2,0:T(8,128)(2,1)S(1)} %get-tuple-element.3, bf16[1,384,4096]{1,2,0:T(8,128)(2,1)S(1)} %get-tuple-element.2, s32[384]{0:T(512)S(1)} %eq.35), kind=kOutput, calls=%fused_computation.9 | convolution fusion | flops 1613856768 | bytes 14681600 | tf_op jit(solution)/shard_map/bp,jpc->jbc/dot_general | solution.py:72
  115.0 2.5 %slice_add_fusion = f32[1,256,4096]{1,2,0:T(8,128)} fusion(f32[2,256,4096]{1,2,0:T(8,128)S(1)} %convolution_bitcast_fusion), kind=kLoop, calls=%fused_computation.14 | loop fusion | flops 1048576 | bytes 12582912 | tf_op jit(solution)/shard_map/add | solution.py:75
  117.5 5.5 %copy.29 = f32[256,32,128]{2,1,0:T(8,128)} copy(f32[256,32,128]{0,2,1:T(8,128)} %bitcast.59) | data formatting | bytes 8388608 | tf_op jit(solution)/shard_map/add | solution.py:75
  123.0 0.0 copy-start.1
  123.0 0.0 reduce-scatter.3.cloned.1.call-update
  123.0 0.0 reduce-scatter.5.cloned.1.call-start
  123.1 47.1 %reduce-scatter.3.cloned.1.call-done = f32[64,32,128]{2,1,0:T(8,128)} async-done(((f32[256,32,128]{2,1,0:T(8,128)}), f32[64,32,128]{2,1,0:T(8,128)}) %reduce-scatter.3.cloned.1.call-update) | async-done | bytes 1048592 | tf_op jit(solution)/shard_map/reduce_scatter | solution.py:35
  170.2 0.0 reduce-scatter.5.cloned.1.call-update
  170.2 1.9 collective-permute-start
  172.1 3.6 %collective-permute-start.1 = (f32[1,32,1024]{2,1,0:T(8,128)S(1)}, f32[1,32,1024]{2,1,0:T(8,128)S(1)}, u32[]{:S(2)}, u32[]{:S(2)}) collective-permute-start(f32[1,32,1024]{2,1,0:T(8,128)S(1)} %get-tuple-element.6), channel_id=1, source_target_pairs={{32,0},{64,32},{96,64},{128,96},{160,128},{192,160},{224,192},{33,... | collective-permute-start | bytes 393224 | tf_op jit(solution)/shard_map/ppermute | solution.py:25
  175.8 0.7 collective-permute-done
  176.5 1.8 collective-permute-done.1
  178.3 33.2 %reduce-scatter.5.cloned.1.call-done = f32[8,32,128]{2,1,0:T(8,128)} async-done(((f32[64,32,128]{2,1,0:T(8,128)}), f32[8,32,128]{2,1,0:T(8,128)}) %reduce-scatter.5.cloned.1.call-update) | async-done | bytes 131088 | tf_op jit(solution)/shard_map/reduce_scatter | solution.py:35
  211.5 0.0 copy-done.1
  211.5 0.9 bitcast_add_fusion
  212.4 0.7 slice_bitcast_fusion
  (6 shorter events, 0.0 us)
Async XLA Ops:
  7.2 15.3 %copy-start = (s32[1,24,16]{1,2,0:T(8,128)S(1)}, s32[1,24,16]{1,2,0:T(8,128)}, u32[]{:S(2)}) copy-start(s32[1,24,16]{1,2,0:T(8,128)} %param.7) | copy-start | bytes 4612
  10.9 61.5 %all-to-all-start = ((bf16[32,8,32,128]{3,2,1,0:T(8,128)(2,1)}), bf16[32,8,32,128]{3,2,1,0:T(8,128)(2,1)S(1)}, u32[]{:S(2)}, u32[]{:S(2)}) async-start(bf16[32,8,32,128]{3,2,1,0:T(8,128)(2,1)} %broadcast_in_dim.6), calls=%async_computation | async-start | bytes 4194304 | tf_op jit(solution)/shard_map/all_to_all | solution.py:12
  22.4 147.8 %reduce-scatter.3.cloned.1.call-start = ((), (), s32[]{:S(2)}) async-start(), calls=%async_computation.3 | async-start | bytes 5242880 | tf_op jit(solution)/shard_map/reduce_scatter | solution.py:35
  75.6 9.7 %copy-start.2 = (s32[1,24,128]{2,1,0:T(8,128)S(1)}, s32[1,24,128]{2,1,0:T(8,128)}, u32[]{:S(2)}) copy-start(s32[1,24,128]{2,1,0:T(8,128)} %param.8) | copy-start | bytes 36868
  123.0 88.5 %copy-start.1 = (f32[1024]{0:T(1024)S(1)}, f32[1024]{0:T(1024)}, u32[]{:S(2)}) copy-start(f32[1024]{0:T(1024)} %param.11) | copy-start | bytes 12292
  123.0 88.4 %reduce-scatter.5.cloned.1.call-start = ((), (), s32[]{:S(2)}) async-start(), calls=%async_computation.4 | async-start | bytes 1179648 | tf_op jit(solution)/shard_map/reduce_scatter | solution.py:35
  170.2 6.3 %collective-permute-start = (f32[1,32,1024]{2,1,0:T(8,128)S(1)}, f32[1,32,1024]{2,1,0:T(8,128)S(1)}, u32[]{:S(2)}, u32[]{:S(2)}) collective-permute-start(f32[1,32,1024]{2,1,0:T(8,128)S(1)} %get-tuple-element.6), channel_id=1, source_target_pairs={{0,32},{32,64},{64,96},{96,128},{128,160},{160,192},{192,224},{1,3... | collective-permute-start | bytes 393224 | tf_op jit(solution)/shard_map/ppermute | solution.py:23
  172.1 6.1 %collective-permute-start.1 = (f32[1,32,1024]{2,1,0:T(8,128)S(1)}, f32[1,32,1024]{2,1,0:T(8,128)S(1)}, u32[]{:S(2)}, u32[]{:S(2)}) collective-permute-start(f32[1,32,1024]{2,1,0:T(8,128)S(1)} %get-tuple-element.6), channel_id=1, source_target_pairs={{32,0},{64,32},{96,64},{128,96},{160,128},{192,160},{224,192},{33,... | collective-permute-start | bytes 393224 | tf_op jit(solution)/shard_map/ppermute | solution.py:25
Sparse Core Ops, SparseCore 0:
  123.2 46.9 reduce-scatter.2
  172.7 38.6 reduce-scatter.4

commit v3 on v2

--- a/solution.py
+++ b/solution.py
@@ -42,8 +42,8 @@
     coef_pair = jnp.concatenate([coef[0], direction[0]], axis=0).astype(jnp.bfloat16)
     local_blk = coef_pair.shape[1] // width
     by_block = coef_pair.reshape(2 * arms, local_blk, width).transpose(1, 0, 2)
-    parts = copy_for_each(by_block, ROW)
-    coef_table = parts.reshape(-1, 2 * arms, width)
+    coef_table = lax.all_gather(by_block, "row_1", axis=0, tiled=True)
+    coef_table = lax.all_gather(coef_table, "row_0", axis=0, tiled=True)
     nblk = coef_table.shape[0]
     both = jnp.concatenate([coef, direction], axis=1)
     neighbours = extended(both, (("day", 0),), 1)
@@ -66,14 +66,16 @@
     top = lax.reduce_precision(contrib, exponent_bits=8, mantissa_bits=7)
     hi = top.astype(jnp.bfloat16)
     lo = (contrib - top).astype(jnp.bfloat16)
-    place = (jnp.arange(nblk, dtype=jnp.int32)[:, None] == blks.reshape(-1)[None, :]).astype(
-        jnp.bfloat16
-    )
+    outer = lax.axis_size("row_0")
+    inner = lax.axis_size("row_1")
+    order = jnp.arange(nblk, dtype=jnp.int32).reshape(outer, inner, -1).transpose(1, 0, 2)
+    place = (order.reshape(-1)[:, None] == blks.reshape(-1)[None, :]).astype(jnp.bfloat16)
     split = jnp.einsum(
         "bp,jpc->jbc", place, jnp.stack([hi, lo], axis=0), preferred_element_type=jnp.float32
     )
     partial_terms = (split[0] + split[1]).reshape(nblk, 2 * arms, width)
-    owned = scatter_axes(partial_terms, ROW, 0)
+    owned = lax.psum_scatter(partial_terms, "row_1", scatter_dimension=0, tiled=True)
+    owned = lax.psum_scatter(owned, "row_0", scatter_dimension=0, tiled=True)
     owned = owned.transpose(1, 0, 2).reshape(2 * arms, -1)
     day_index = lax.axis_index("day")
     ndays = lax.axis_size("day")

time: 221 us -> 211 us (0.955)
  blocking collectives: 0 us -> 30.9 us
  waiting for transfers between devices: 132 us -> 107 us
  starting transfers between devices: 17.1 us -> 5.68 us
  matrix products: 21.1 us -> 18.5 us
    all_to_all x1 -> x0, waiting for transfers between devices: 49.7 us -> none  [copy_for_each(): return lax.all_to_all(copies, axis, split_axis=0, concat_axis=0, tiled=True)]
    all_gather x0 -> x1, waiting for transfers between devices: none -> 31.2 us  [on_device(): coef_table = lax.all_gather(coef_table, 'row_0', axis=0, tiled=True)]
    all_gather x0 -> x1, blocking collectives: none -> 30.9 us  [on_device(): coef_table = lax.all_gather(by_block, 'row_1', axis=0, tiled=True)]
    all_to_all x1 -> x0, starting transfers between devices: 11.5 us -> none  [copy_for_each(): return lax.all_to_all(copies, axis, split_axis=0, concat_axis=0, tiled=True)]
    reduce_scatter x2, waiting for transfers between devices: 80.3 us -> 72.8 us  [the longest x1 55.5 us: on_device(): lax.psum_scatter(partial_terms, 'row_1', scatter_dimension=0, tiled=True)]
    dot_general x1, matrix products: 9.67 us -> 7.04 us  [on_device(): jnp.einsum('tari,taki->tkr', feats, selected, preferred_element_type=jnp....]
  transfers between devices with their start and end apart: 5 -> 5, of which waited for: 5 -> 5; matrix products, arithmetic and copies ran while one was open for 0% -> 1% of each run, Pallas kernels for 0% -> 0%
where the time goes in v3:
time: 211 us; the launch traced here: 210 us
  waiting for transfers between devices  107 us (51%)
  blocking collectives  30.9 us (15%)
  local copies, waits for them, and re-layouts  23.8 us (11%)
  matrix products  18.5 us (9%)
  between operations  13.9 us (7%)
  other arithmetic  10.6 us (5%)
  starting transfers between devices  5.68 us (3%)
    reduce_scatter x1, waiting for transfers between devices, on_device(): lax.psum_scatter(partial_terms, 'row_1', scatter_dimension=0, tiled=True)  55.5 us
    all_gather x1, waiting for transfers between devices, on_device(): coef_table = lax.all_gather(coef_table, 'row_0', axis=0, tiled=True)  31.2 us
    all_gather x1, blocking collectives, on_device(): coef_table = lax.all_gather(by_block, 'row_1', axis=0, tiled=True)  30.9 us
    reduce_scatter x1, waiting for transfers between devices, on_device(): owned = lax.psum_scatter(owned, 'row_0', scatter_dimension=0, tiled=True)  17.3 us
    reshape x2, local copies, waits for them, and re-layouts, on_device(): contrib = contrib.reshape(-1, 2 * arms * width)  13.7 us
    dot_general x1, matrix products, on_device(): jnp.einsum('tari,tkr->taki', feats, both_low, preferred_element_type=jnp....  8.99 us
    dot_general x1, matrix products, on_device(): jnp.einsum('tari,taki->tkr', feats, selected, preferred_element_type=jnp....  7.04 us
    add x1, local copies, waits for them, and re-layouts, on_device(): partial_terms = (split[0] + split[1]).reshape(nblk, 2 * arms, width)  5.49 us
  transfers between devices with their start and end apart: 5, of which 5 were waited for; matrix products, arithmetic and copies ran while one was open for 1% of the time, Pallas kernels for 0%

profile of v3, /device:TPU:2, one launch (start us, length us, event | category | flops | bytes accessed | tf_op | source)
XLA Modules:
  0.0 209.9 jit_solution(5084960627540762023)
XLA Ops:
  7.2 0.0 all-gather.2.cloned.1.call-start
  7.2 0.9 constant_dynamic-update-slice_fusion.1
  8.1 0.9 constant_dynamic-update-slice_fusion
  9.1 30.9 %all_gather.6 = bf16[64,32,128]{2,1,0:T(8,128)(2,1)} all-gather(bf16[8,32,128]{2,1,0:T(8,128)(2,1)S(1)} %copy.30), channel_id=1, replica_groups=mesh['day'=8,'row_0'=4,'row_1'=8] {'row_1'}, dimensions={0}, use_global_device_ids=true | all-gather | bytes 589824 | tf_op jit(solution)/shard_map/all_gather | solution.py:45
  40.0 0.0 all-gather.2.cloned.1.call-update
  40.1 0.0 reduce-scatter.3.cloned.1.call-start
  40.1 0.8 copy.34
  40.9 0.7 compare_select_fusion
  41.6 0.1 copy.31
  41.7 0.1 reshape.141
  41.8 0.1 reshape.137
  41.9 0.1 eq.35
  41.9 31.2 %all-gather.2.cloned.1.call-done = bf16[256,32,128]{2,1,0:T(8,128)(2,1)} async-done(((bf16[64,32,128]{2,1,0:T(8,128)(2,1)}), bf16[256,32,128]{2,1,0:T(8,128)(2,1)}) %all-gather.2.cloned.1.call-update) | async-done | bytes 2097168 | tf_op jit(solution)/shard_map/all_gather | solution.py:46
  73.1 2.8 %gather_fusion = bf16[384,32,128]{2,1,0:T(8,128)(2,1)S(1)} fusion(bf16[256,32,128]{2,1,0:T(8,128)(2,1)} %all-gather.2.cloned.1.call-done, s32[1024]{0:T(1024)S(1)} %pad_clamp_fusion), kind=kCustom, calls=%fused_computation | custom fusion | bytes 6292992 | tf_op jit(solution)/shard_map/gather | solution.py:51
  76.0 0.0 copy-start.1
  76.0 7.0 %fusion.13 = f32[24,32,128]{2,1,0:T(8,128)S(1)} fusion(bf16[24,16,32,128]{3,2,1,0:T(8,128)(2,1)S(1)} %bitcast.59, bf16[1,24,16,128,128]{4,3,2,1,0:T(8,128)(2,1)} %param.6), kind=kOutput, calls=%fused_computation.16 | convolution fusion | flops 402653184 | bytes 16121856 | tf_op jit(solution)/shard_map/tari,taki->tkr/dot_general | solution.py:53
  83.0 0.0 copy-done.1
  83.0 0.8 subtract_convert_fusion
  83.8 0.1 fusion.19
  83.9 9.0 %fusion.10 = f32[24,16,32,128]{3,2,1,0:T(8,128)} fusion(bf16[1,24,16,128,128]{4,3,2,1,0:T(8,128)(2,1)} %param.6, bf16[24,16,128]{2,1,0:T(8,128)(2,1)S(1)} %fusion.19, bf16[24,16,128]{2,1,0:T(8,128)(2,1)S(1)} %get-tuple-element.10), kind=kOutput, calls=%fused_computation.15 | convolution fusion | flops 403046400 | bytes 19070976 | tf_op jit(solution)/shard_map/tari,tkr->taki/dot_general | solution.py:64
  92.8 7.2 %reshape.130 = f32[1,384,4096]{2,1,0:T(8,128)} reshape(f32[24,16,32,128]{3,2,1,0:T(8,128)} %fusion.10) | data formatting | bytes 12582912 | tf_op jit(solution)/shard_map/reshape | solution.py:65
  100.0 6.6 %copy.32 = f32[1,384,4096]{1,2,0:T(8,128)} copy(f32[1,384,4096]{2,1,0:T(8,128)} %reshape.130) | data formatting | bytes 12582912 | tf_op jit(solution)/shard_map/reshape | solution.py:65
  106.6 3.8 %reduce-precision_convert_fusion = (bf16[1,384,4096]{1,2,0:T(8,128)(2,1)S(1)}, bf16[1,384,4096]{1,2,0:T(8,128)(2,1)S(1)}) fusion(f32[1,384,4096]{1,2,0:T(8,128)} %copy.32), kind=kLoop, calls=%fused_computation.8 | loop fusion | flops 6291456 | bytes 12582912 | tf_op jit(solution)/shard_map/convert_element_type | solution.py:67
  110.3 2.4 %convolution_bitcast_fusion = f32[2,256,4096]{1,2,0:T(8,128)S(1)} fusion(bf16[1,384,4096]{1,2,0:T(8,128)(2,1)S(1)} %get-tuple-element.3, bf16[1,384,4096]{1,2,0:T(8,128)(2,1)S(1)} %get-tuple-element.2, s32[384]{0:T(512)S(1)} %eq.35, s32[256]{0:T(256)S(1)} %reshape.137), kind=kOutput, calls=%fused_computation.9 | convolution fusion | flops 1613856768 | bytes 14682624 | tf_op jit(solution)/shard_map/bp,jpc->jbc/dot_general | solution.py:73
  112.8 2.5 %slice_add_fusion = f32[1,256,4096]{1,2,0:T(8,128)} fusion(f32[2,256,4096]{1,2,0:T(8,128)S(1)} %convolution_bitcast_fusion), kind=kLoop, calls=%fused_computation.14 | loop fusion | flops 1048576 | bytes 12582912 | tf_op jit(solution)/shard_map/add | solution.py:76
  115.3 5.5 %copy.35 = f32[256,32,128]{2,1,0:T(8,128)} copy(f32[256,32,128]{0,2,1:T(8,128)} %bitcast.58) | data formatting | bytes 8388608 | tf_op jit(solution)/shard_map/add | solution.py:76
  120.8 0.0 copy-start
  120.8 0.0 reduce-scatter.3.cloned.1.call-update
  120.8 0.0 reduce-scatter.5.cloned.1.call-start
  120.9 55.5 %reduce-scatter.3.cloned.1.call-done = f32[32,32,128]{2,1,0:T(8,128)} async-done(((f32[256,32,128]{2,1,0:T(8,128)}), f32[32,32,128]{2,1,0:T(8,128)}) %reduce-scatter.3.cloned.1.call-update) | async-done | bytes 524304 | tf_op jit(solution)/shard_map/reduce_scatter | solution.py:77
  176.3 0.0 reduce-scatter.5.cloned.1.call-update
  176.3 1.9 collective-permute-start
  178.3 3.6 %collective-permute-start.1 = (f32[1,32,1024]{2,1,0:T(8,128)S(1)}, f32[1,32,1024]{2,1,0:T(8,128)S(1)}, u32[]{:S(2)}, u32[]{:S(2)}) collective-permute-start(f32[1,32,1024]{2,1,0:T(8,128)S(1)} %get-tuple-element.6), channel_id=1, source_target_pairs={{32,0},{64,32},{96,64},{128,96},{160,128},{192,160},{224,192},{33,... | collective-permute-start | bytes 393224 | tf_op jit(solution)/shard_map/ppermute | solution.py:25
  181.9 0.7 collective-permute-done
  182.6 1.8 collective-permute-done.1
  184.4 17.3 %reduce-scatter.5.cloned.1.call-done = f32[8,32,128]{2,1,0:T(8,128)} async-done(((f32[32,32,128]{2,1,0:T(8,128)}), f32[8,32,128]{2,1,0:T(8,128)}) %reduce-scatter.5.cloned.1.call-update) | async-done | bytes 131088 | tf_op jit(solution)/shard_map/reduce_scatter | solution.py:78
  201.8 0.0 copy-done
  201.8 0.9 bitcast_add_fusion
  202.7 0.7 slice_bitcast_fusion
  (6 shorter events, 0.0 us)
Async XLA Ops:
  7.2 66.0 %all-gather.2.cloned.1.call-start = ((), (), s32[]{:S(2)}) async-start(), calls=%async_computation.2 | async-start | bytes 2621440 | tf_op jit(solution)/shard_map/all_gather | solution.py:46
  40.1 136.3 %reduce-scatter.3.cloned.1.call-start = ((), (), s32[]{:S(2)}) async-start(), calls=%async_computation.3 | async-start | bytes 4718592 | tf_op jit(solution)/shard_map/reduce_scatter | solution.py:77
  76.0 7.1 %copy-start.1 = (s32[1,24,128]{2,1,0:T(8,128)S(1)}, s32[1,24,128]{2,1,0:T(8,128)}, u32[]{:S(2)}) copy-start(s32[1,24,128]{2,1,0:T(8,128)} %param.8) | copy-start | bytes 36868
  120.8 81.0 %copy-start = (f32[1024]{0:T(1024)S(1)}, f32[1024]{0:T(1024)}, u32[]{:S(2)}) copy-start(f32[1024]{0:T(1024)} %param.11) | copy-start | bytes 12292
  120.8 80.9 %reduce-scatter.5.cloned.1.call-start = ((), (), s32[]{:S(2)}) async-start(), calls=%async_computation.4 | async-start | bytes 655360 | tf_op jit(solution)/shard_map/reduce_scatter | solution.py:78
  176.3 6.3 %collective-permute-start = (f32[1,32,1024]{2,1,0:T(8,128)S(1)}, f32[1,32,1024]{2,1,0:T(8,128)S(1)}, u32[]{:S(2)}, u32[]{:S(2)}) collective-permute-start(f32[1,32,1024]{2,1,0:T(8,128)S(1)} %get-tuple-element.6), channel_id=1, source_target_pairs={{0,32},{32,64},{64,96},{96,128},{128,160},{160,192},{192,224},{1,3... | collective-permute-start | bytes 393224 | tf_op jit(solution)/shard_map/ppermute | solution.py:23
  178.3 6.1 %collective-permute-start.1 = (f32[1,32,1024]{2,1,0:T(8,128)S(1)}, f32[1,32,1024]{2,1,0:T(8,128)S(1)}, u32[]{:S(2)}, u32[]{:S(2)}) collective-permute-start(f32[1,32,1024]{2,1,0:T(8,128)S(1)} %get-tuple-element.6), channel_id=1, source_target_pairs={{32,0},{64,32},{96,64},{128,96},{160,128},{192,160},{224,192},{33,... | collective-permute-start | bytes 393224 | tf_op jit(solution)/shard_map/ppermute | solution.py:25
Sparse Core Ops, SparseCore 0:
  40.2 32.8 all-gather.1
  120.9 55.3 reduce-scatter.2
  178.9 22.8 reduce-scatter.4

commit v4 on v3

--- a/solution.py
+++ b/solution.py
@@ -3,6 +3,8 @@
 from jax import lax
 from jax.sharding import Mesh
 from jax.sharding import PartitionSpec as P
+from jax.experimental import pallas as pl
+from jax.experimental.pallas import tpu as pltpu
 
 ROW = ("row_0", "row_1")
 
@@ -36,6 +38,36 @@
     return scatter_axes(nearer, axes[1:], dim)
 
 
+def scatter_kernel(dest_ref, part_ref, out_ref):
+    t = pl.program_id(0)
+    slots = part_ref.shape[1]
+
+    @pl.when(t == 0)
+    def _():
+        out_ref[...] = jnp.zeros_like(out_ref)
+
+    for a in range(slots):
+        q = dest_ref[t * slots + a]
+        out_ref[q] = out_ref[q] + part_ref[0, a]
+
+
+def scatter_rows(dest, contrib, nblk):
+    tiles, slots, rows, width = contrib.shape
+    return pl.pallas_call(
+        scatter_kernel,
+        grid_spec=pltpu.PrefetchScalarGridSpec(
+            num_scalar_prefetch=1,
+            grid=(tiles,),
+            in_specs=[pl.BlockSpec((1, slots, rows, width), lambda t, d: (t, 0, 0, 0))],
+            out_specs=pl.BlockSpec((nblk, rows, width), lambda t, d: (0, 0, 0)),
+        ),
+        out_shape=jax.ShapeDtypeStruct((nblk, rows, width), jnp.float32),
+        compiler_params=pltpu.CompilerParams(
+            dimension_semantics=("arbitrary",), vmem_limit_bytes=40 * 1024 * 1024
+        ),
+    )(dest, contrib)
+
+
 def on_device(features, blocks, labels, coef, direction, prior):
     arms = coef.shape[1]
     width = features.shape[-1]
@@ -62,18 +94,12 @@
     hrow = probs * lin_dir - probs * jnp.sum(probs * lin_dir, axis=1, keepdims=True)
     both_low = jnp.concatenate([resid, hrow], axis=1).astype(jnp.bfloat16)
     contrib = jnp.einsum("tari,tkr->taki", feats, both_low, preferred_element_type=jnp.float32)
-    contrib = contrib.reshape(-1, 2 * arms * width)
-    top = lax.reduce_precision(contrib, exponent_bits=8, mantissa_bits=7)
-    hi = top.astype(jnp.bfloat16)
-    lo = (contrib - top).astype(jnp.bfloat16)
     outer = lax.axis_size("row_0")
     inner = lax.axis_size("row_1")
-    order = jnp.arange(nblk, dtype=jnp.int32).reshape(outer, inner, -1).transpose(1, 0, 2)
-    place = (order.reshape(-1)[:, None] == blks.reshape(-1)[None, :]).astype(jnp.bfloat16)
-    split = jnp.einsum(
-        "bp,jpc->jbc", place, jnp.stack([hi, lo], axis=0), preferred_element_type=jnp.float32
-    )
-    partial_terms = (split[0] + split[1]).reshape(nblk, 2 * arms, width)
+    per = nblk // (outer * inner)
+    flat = blks.reshape(-1)
+    dest = ((flat // per) % inner) * (outer * per) + (flat // (inner * per)) * per + flat % per
+    partial_terms = scatter_rows(dest, contrib, nblk)
     owned = lax.psum_scatter(partial_terms, "row_1", scatter_dimension=0, tiled=True)
     owned = lax.psum_scatter(owned, "row_0", scatter_dimension=0, tiled=True)
     owned = owned.transpose(1, 0, 2).reshape(2 * arms, -1)

time: 211 us -> 183 us (0.87)
  local copies, waits for them, and re-layouts: 23.8 us -> 6.47 us
  other arithmetic: 10.6 us -> 4.36 us
  matrix products: 18.5 us -> 12.6 us
  Pallas kernels: 0 us -> 2.54 us
    reshape x3 -> x0, local copies, waits for them, and re-layouts: 13.8 us -> none  [the longest x2 13.7 us: on_device(): contrib = contrib.reshape(-1, 2 * arms * width)]
    add x1 -> x0, local copies, waits for them, and re-layouts: 5.49 us -> none  [on_device(): partial_terms = (split[0] + split[1]).reshape(nblk, 2 * arms, width)]
    convert_element_type x1 -> x0, other arithmetic: 3.75 us -> none  [on_device(): hi = top.astype(jnp.bfloat16)]
    dot_general x1, matrix products: 8.99 us -> 5.58 us  [on_device(): jnp.einsum('tari,tkr->taki', feats, both_low, preferred_element_type=jnp....]
    pallas_call x0 -> x1, Pallas kernels: none -> 2.54 us  [scatter_rows(): pl.pallas_call(scatter_kernel, grid_spec=pltpu.PrefetchScalarGridSpec(num...]
    add x1, other arithmetic: 2.51 us -> 0.02 us  [on_device(): flat // per % inner * (outer * per) + flat // (inner * per) * per]
    dot_general x1 -> x0, matrix products: 2.45 us -> none  [on_device(): jnp.einsum('bp,jpc->jbc', place, jnp.stack([hi, lo], axis=0), preferred_e...]
where the time goes in v4:
time: 183 us
  waiting for transfers between devices  107 us (58%)
  blocking collectives  30.9 us (17%)
  between operations  13.9 us (8%)
  matrix products  12.6 us (7%)
  local copies, waits for them, and re-layouts  6.47 us (4%)
  starting transfers between devices  5.68 us (3%)
  other arithmetic  4.36 us (2%)
  Pallas kernels  2.54 us (1%)
    reduce_scatter x1, waiting for transfers between devices, on_device(): lax.psum_scatter(partial_terms, 'row_1', scatter_dimension=0, tiled=True)  55.5 us
    all_gather x1, waiting for transfers between devices, on_device(): coef_table = lax.all_gather(coef_table, 'row_0', axis=0, tiled=True)  31.3 us
    all_gather x1, blocking collectives, on_device(): coef_table = lax.all_gather(by_block, 'row_1', axis=0, tiled=True)  30.9 us
    reduce_scatter x1, waiting for transfers between devices, on_device(): owned = lax.psum_scatter(owned, 'row_0', scatter_dimension=0, tiled=True)  17.3 us
    dot_general x1, matrix products, on_device(): jnp.einsum('tari,taki->tkr', feats, selected, preferred_element_type=jnp....  7.04 us
    dot_general x1, matrix products, on_device(): jnp.einsum('tari,tkr->taki', feats, both_low, preferred_element_type=jnp....  5.58 us
  transfers between devices with their start and end apart: 5, of which 5 were waited for; matrix products, arithmetic and copies ran while one was open for 1% of the time, Pallas kernels for 0%

profile of v4, /device:TPU:2, one launch (start us, length us, event | category | flops | bytes accessed | tf_op | source)
XLA Modules:
  0.0 183.0 jit_solution(6468586829646191202)
XLA Ops:
  7.2 0.0 all-gather.2.cloned.1.call-start
  7.2 0.9 constant_dynamic-update-slice_fusion.1
  8.1 0.9 constant_dynamic-update-slice_fusion
  9.1 30.9 %all_gather.6 = bf16[64,32,128]{2,1,0:T(8,128)(2,1)} all-gather(bf16[8,32,128]{2,1,0:T(8,128)(2,1)S(1)} %copy.18), channel_id=1, replica_groups=mesh['day'=8,'row_0'=4,'row_1'=8] {'row_1'}, dimensions={0}, use_global_device_ids=true | all-gather | bytes 589824 | tf_op jit(solution)/shard_map/all_gather | solution.py:77
  40.0 0.0 all-gather.2.cloned.1.call-update
  40.1 0.0 reduce-scatter.3.cloned.1.call-start
  40.1 0.8 copy.17
  40.9 0.7 compare_select_fusion
  41.6 0.1 copy.19
  41.7 0.1 reshape.53
  41.7 0.1 reshape_squeeze.3
  41.9 31.3 %all-gather.2.cloned.1.call-done = bf16[256,32,128]{2,1,0:T(8,128)(2,1)} async-done(((bf16[64,32,128]{2,1,0:T(8,128)(2,1)}), bf16[256,32,128]{2,1,0:T(8,128)(2,1)}) %all-gather.2.cloned.1.call-update) | async-done | bytes 2097168 | tf_op jit(solution)/shard_map/all_gather | solution.py:78
  73.1 2.8 %gather_fusion = bf16[384,32,128]{2,1,0:T(8,128)(2,1)S(1)} fusion(bf16[256,32,128]{2,1,0:T(8,128)(2,1)} %all-gather.2.cloned.1.call-done, s32[1024]{0:T(1024)S(1)} %pad_clamp_fusion), kind=kCustom, calls=%fused_computation | custom fusion | bytes 6292992 | tf_op jit(solution)/shard_map/gather | solution.py:83
  76.0 0.0 copy-start.2
  76.0 7.0 %fusion.9 = f32[24,32,128]{2,1,0:T(8,128)S(1)} fusion(bf16[24,16,32,128]{3,2,1,0:T(8,128)(2,1)S(1)} %bitcast.50, bf16[1,24,16,128,128]{4,3,2,1,0:T(8,128)(2,1)} %param.6), kind=kOutput, calls=%fused_computation.8 | convolution fusion | flops 402653184 | bytes 16121856 | tf_op jit(solution)/shard_map/tari,taki->tkr/dot_general | solution.py:85
  83.0 0.0 copy-done.2
  83.0 0.8 subtract_convert_fusion
  83.8 0.1 fusion.15
  83.9 5.6 %fusion.6.part_ref = f32[24,16,32,128]{3,2,1,0:T(8,128)S(1)} fusion(bf16[1,24,16,128,128]{4,3,2,1,0:T(8,128)(2,1)} %param.6, bf16[24,16,128]{2,1,0:T(8,128)(2,1)S(1)} %fusion.15, bf16[24,16,128]{2,1,0:T(8,128)(2,1)S(1)} %get-tuple-element.8), kind=kOutput, calls=%fused_computation.7 | convolution fusion | flops 403046400 | bytes 19070976 | tf_op jit(solution)/shard_map/tari,tkr->taki/dot_general | solution.py:96
  89.5 2.5 %shard_map.77 = f32[256,32,128]{2,1,0:T(8,128)S(1)} custom-call(s32[384]{0:T(512)S(1)} %fusion.23.dest_ref, f32[24,16,32,128]{3,2,1,0:T(8,128)S(1)} %fusion.6.part_ref), custom_call_target="tpu_custom_call" | custom-call | tf_op jit(solution)/shard_map/pallas_call | solution.py:56
  92.0 0.0 copy-start
  92.0 1.9 %copy-done = f32[256,32,128]{2,1,0:T(8,128)} copy-done((f32[256,32,128]{2,1,0:T(8,128)}, f32[256,32,128]{2,1,0:T(8,128)S(1)}, u32[]{:S(2)}) %copy-start) | copy-done | bytes 4194328
  94.0 0.0 copy-start.1
  94.0 0.0 reduce-scatter.3.cloned.1.call-update
  94.0 0.0 reduce-scatter.5.cloned.1.call-start
  94.0 55.5 %reduce-scatter.3.cloned.1.call-done = f32[32,32,128]{2,1,0:T(8,128)} async-done(((f32[256,32,128]{2,1,0:T(8,128)}), f32[32,32,128]{2,1,0:T(8,128)}) %reduce-scatter.3.cloned.1.call-update) | async-done | bytes 524304 | tf_op jit(solution)/shard_map/reduce_scatter | solution.py:103
  149.5 0.0 reduce-scatter.5.cloned.1.call-update
  149.5 1.9 %collective-permute-start = (f32[1,32,1024]{2,1,0:T(8,128)S(1)}, f32[1,32,1024]{2,1,0:T(8,128)S(1)}, u32[]{:S(2)}, u32[]{:S(2)}) collective-permute-start(f32[1,32,1024]{2,1,0:T(8,128)S(1)} %get-tuple-element.4), channel_id=1, source_target_pairs={{0,32},{32,64},{64,96},{96,128},{128,160},{160,192},{192,224},{1,3... | collective-permute-start | bytes 393224 | tf_op jit(solution)/shard_map/ppermute | solution.py:25
  151.4 3.6 %collective-permute-start.1 = (f32[1,32,1024]{2,1,0:T(8,128)S(1)}, f32[1,32,1024]{2,1,0:T(8,128)S(1)}, u32[]{:S(2)}, u32[]{:S(2)}) collective-permute-start(f32[1,32,1024]{2,1,0:T(8,128)S(1)} %get-tuple-element.4), channel_id=1, source_target_pairs={{32,0},{64,32},{96,64},{128,96},{160,128},{192,160},{224,192},{33,... | collective-permute-start | bytes 393224 | tf_op jit(solution)/shard_map/ppermute | solution.py:27
  155.1 0.7 collective-permute-done
  155.8 1.8 collective-permute-done.1
  157.6 17.3 %reduce-scatter.5.cloned.1.call-done = f32[8,32,128]{2,1,0:T(8,128)} async-done(((f32[32,32,128]{2,1,0:T(8,128)}), f32[8,32,128]{2,1,0:T(8,128)}) %reduce-scatter.5.cloned.1.call-update) | async-done | bytes 131088 | tf_op jit(solution)/shard_map/reduce_scatter | solution.py:104
  174.9 0.0 copy-done.1
  174.9 0.9 bitcast_add_fusion
  175.8 0.7 slice_bitcast_fusion
  (6 shorter events, 0.1 us)
Async XLA Ops:
  7.2 66.0 %all-gather.2.cloned.1.call-start = ((), (), s32[]{:S(2)}) async-start(), calls=%async_computation.2 | async-start | bytes 2621440 | tf_op jit(solution)/shard_map/all_gather | solution.py:78
  40.1 109.4 %reduce-scatter.3.cloned.1.call-start = ((), (), s32[]{:S(2)}) async-start(), calls=%async_computation.3 | async-start | bytes 4718592 | tf_op jit(solution)/shard_map/reduce_scatter | solution.py:103
  76.0 7.1 %copy-start.2 = (s32[1,24,128]{2,1,0:T(8,128)S(1)}, s32[1,24,128]{2,1,0:T(8,128)}, u32[]{:S(2)}) copy-start(s32[1,24,128]{2,1,0:T(8,128)} %param.8) | copy-start | bytes 36868
  92.0 1.9 %copy-start = (f32[256,32,128]{2,1,0:T(8,128)}, f32[256,32,128]{2,1,0:T(8,128)S(1)}, u32[]{:S(2)}) copy-start(f32[256,32,128]{2,1,0:T(8,128)S(1)} %shard_map.77) | copy-start | bytes 12582916
  94.0 80.9 %copy-start.1 = (f32[1024]{0:T(1024)S(1)}, f32[1024]{0:T(1024)}, u32[]{:S(2)}) copy-start(f32[1024]{0:T(1024)} %param.11) | copy-start | bytes 12292
  94.0 80.9 %reduce-scatter.5.cloned.1.call-start = ((), (), s32[]{:S(2)}) async-start(), calls=%async_computation.4 | async-start | bytes 655360 | tf_op jit(solution)/shard_map/reduce_scatter | solution.py:104
  149.5 6.3 %collective-permute-start = (f32[1,32,1024]{2,1,0:T(8,128)S(1)}, f32[1,32,1024]{2,1,0:T(8,128)S(1)}, u32[]{:S(2)}, u32[]{:S(2)}) collective-permute-start(f32[1,32,1024]{2,1,0:T(8,128)S(1)} %get-tuple-element.4), channel_id=1, source_target_pairs={{0,32},{32,64},{64,96},{96,128},{128,160},{160,192},{192,224},{1,3... | collective-permute-start | bytes 393224 | tf_op jit(solution)/shard_map/ppermute | solution.py:25
  151.4 6.1 %collective-permute-start.1 = (f32[1,32,1024]{2,1,0:T(8,128)S(1)}, f32[1,32,1024]{2,1,0:T(8,128)S(1)}, u32[]{:S(2)}, u32[]{:S(2)}) collective-permute-start(f32[1,32,1024]{2,1,0:T(8,128)S(1)} %get-tuple-element.4), channel_id=1, source_target_pairs={{32,0},{64,32},{96,64},{128,96},{160,128},{192,160},{224,192},{33,... | collective-permute-start | bytes 393224 | tf_op jit(solution)/shard_map/ppermute | solution.py:27
Sparse Core Ops, SparseCore 0:
  40.2 32.8 all-gather.1
  94.1 55.3 reduce-scatter.2
  152.0 22.8 reduce-scatter.4

commit v5 on v4

--- a/solution.py
+++ b/solution.py
@@ -74,13 +74,20 @@
     coef_pair = jnp.concatenate([coef[0], direction[0]], axis=0).astype(jnp.bfloat16)
     local_blk = coef_pair.shape[1] // width
     by_block = coef_pair.reshape(2 * arms, local_blk, width).transpose(1, 0, 2)
-    coef_table = lax.all_gather(by_block, "row_1", axis=0, tiled=True)
-    coef_table = lax.all_gather(coef_table, "row_0", axis=0, tiled=True)
+    here = lax.axis_index("row_1")
+    count = lax.axis_size("row_1")
+    pieces = [by_block] + [
+        lax.ppermute(by_block, "row_1", [(i, (i + s) % count) for i in range(count)])
+        for s in range(1, count)
+    ]
+    coef_table = lax.all_gather(jnp.concatenate(pieces, axis=0), "row_0", axis=0, tiled=True)
     nblk = coef_table.shape[0]
     both = jnp.concatenate([coef, direction], axis=1)
     neighbours = extended(both, (("day", 0),), 1)
     blks = blocks[0]
-    selected = coef_table[blks]
+    span = count * local_blk
+    rotated = (blks // span) * span + ((here - (blks // local_blk) % count) % count) * local_blk
+    selected = coef_table[rotated + blks % local_blk]
     feats = features[0]
     logits_dir = jnp.einsum("tari,taki->tkr", feats, selected, preferred_element_type=jnp.float32)
     logits = logits_dir[:, :arms]

time: 183 us -> 177 us (0.967)
  blocking collectives: 30.9 us -> 0 us
  starting transfers between devices: 5.68 us -> 24.3 us
  waiting for transfers between devices: 107 us -> 111 us
    all_gather x1 -> x0, blocking collectives: 30.9 us -> none  [on_device(): coef_table = lax.all_gather(by_block, 'row_1', axis=0, tiled=True)]
    ppermute x0 -> x7, starting transfers between devices: none -> 18.6 us  [on_device(): lax.ppermute(by_block, 'row_1', [(i, (i + s) % count) for i in range(coun...]
    ppermute x0 -> x7, waiting for transfers between devices: none -> 5.49 us  [on_device(): lax.ppermute(by_block, 'row_1', [(i, (i + s) % count) for i in range(coun...]
  transfers between devices with their start and end apart: 5 -> 12, of which waited for: 5 -> 7; matrix products, arithmetic and copies ran while one was open for 1% -> 1% of each run, Pallas kernels for 0% -> 0%
where the time goes in v5:
time: 177 us
  waiting for transfers between devices  111 us (63%)
  starting transfers between devices  24.3 us (14%)
  between operations  14 us (8%)
  matrix products  12.6 us (7%)
  local copies, waits for them, and re-layouts  7.74 us (4%)
  other arithmetic  4.4 us (2%)
  Pallas kernels  2.54 us (1%)
    reduce_scatter x1, waiting for transfers between devices, on_device(): lax.psum_scatter(partial_terms, 'row_1', scatter_dimension=0, tiled=True)  55.5 us
    all_gather x1, waiting for transfers between devices, on_device(): lax.all_gather(jnp.concatenate(pieces, axis=0), 'row_0', axis=0, tiled=True)  30.4 us
    ppermute x7, starting transfers between devices, on_device(): lax.ppermute(by_block, 'row_1', [(i, (i + s) % count) for i in range(coun...  18.6 us
    reduce_scatter x1, waiting for transfers between devices, on_device(): owned = lax.psum_scatter(owned, 'row_0', scatter_dimension=0, tiled=True)  17.3 us
    dot_general x1, matrix products, on_device(): jnp.einsum('tari,taki->tkr', feats, selected, preferred_element_type=jnp....  7.04 us
    dot_general x1, matrix products, on_device(): jnp.einsum('tari,tkr->taki', feats, both_low, preferred_element_type=jnp....  5.58 us
    ppermute x7, waiting for transfers between devices, on_device(): lax.ppermute(by_block, 'row_1', [(i, (i + s) % count) for i in range(coun...  5.49 us
    ppermute x1, starting transfers between devices, extended(): lax.ppermute(head, axis, [((i + 1) % count, i) for i in range(ends)])  3.64 us
  transfers between devices with their start and end apart: 12, of which 7 were waited for; matrix products, arithmetic and copies ran while one was open for 1% of the time, Pallas kernels for 0%

profile of v5, /device:TPU:2, one launch (start us, length us, event | category | flops | bytes accessed | tf_op | source)
XLA Modules:
  0.0 176.7 jit_solution(16428036395706075519)
XLA Ops:
  7.2 0.0 all-gather.2.cloned.1.call-start
  7.2 0.9 constant_dynamic-update-slice_fusion.9
  8.1 0.9 constant_dynamic-update-slice_fusion.8
  9.1 2.0 %collective-permute-start = (bf16[8,32,128]{2,0,1:T(8,128)(2,1)S(1)}, bf16[8,32,128]{2,0,1:T(8,128)(2,1)S(1)}, u32[]{:S(2)}, u32[]{:S(2)}) collective-permute-start(bf16[8,32,128]{2,0,1:T(8,128)(2,1)S(1)} %maximum_bitcast_fusion.2), channel_id=1, source_target_pairs={{0,1},{1,2},{2,3},{3,4},{4,5},{5,6},{6,7},{7,0},{8,9},{9,10},{10,1... | collective-permute-start | bytes 196616 | tf_op jit(solution)/shard_map/ppermute | solution.py:80
  11.1 3.3 %collective-permute-start.1 = (bf16[8,32,128]{2,0,1:T(8,128)(2,1)S(1)}, bf16[8,32,128]{2,0,1:T(8,128)(2,1)S(1)}, u32[]{:S(2)}, u32[]{:S(2)}) collective-permute-start(bf16[8,32,128]{2,0,1:T(8,128)(2,1)S(1)} %maximum_bitcast_fusion.2), channel_id=1, source_target_pairs={{0,2},{1,3},{2,4},{3,5},{4,6},{5,7},{6,0},{7,1},{8,10},{9,11},{10,... | collective-permute-start | bytes 196616 | tf_op jit(solution)/shard_map/ppermute | solution.py:80
  14.4 4.0 %collective-permute-start.2 = (bf16[8,32,128]{2,0,1:T(8,128)(2,1)S(1)}, bf16[8,32,128]{2,0,1:T(8,128)(2,1)S(1)}, u32[]{:S(2)}, u32[]{:S(2)}) collective-permute-start(bf16[8,32,128]{2,0,1:T(8,128)(2,1)S(1)} %maximum_bitcast_fusion.2), channel_id=1, source_target_pairs={{0,3},{1,4},{2,5},{3,6},{4,7},{5,0},{6,1},{7,2},{8,11},{9,12},{10,... | collective-permute-start | bytes 196616 | tf_op jit(solution)/shard_map/ppermute | solution.py:80
  18.4 0.5 collective-permute-start.3
  19.0 4.9 %collective-permute-start.4 = (bf16[8,32,128]{2,0,1:T(8,128)(2,1)S(1)}, bf16[8,32,128]{2,0,1:T(8,128)(2,1)S(1)}, u32[]{:S(2)}, u32[]{:S(2)}) collective-permute-start(bf16[8,32,128]{2,0,1:T(8,128)(2,1)S(1)} %maximum_bitcast_fusion.2), channel_id=1, source_target_pairs={{0,5},{1,6},{2,7},{3,0},{4,1},{5,2},{6,3},{7,4},{8,13},{9,14},{10,... | collective-permute-start | bytes 196616 | tf_op jit(solution)/shard_map/ppermute | solution.py:80
  23.9 0.0 collective-permute-done
  23.9 2.7 %collective-permute-start.5 = (bf16[8,32,128]{2,0,1:T(8,128)(2,1)S(1)}, bf16[8,32,128]{2,0,1:T(8,128)(2,1)S(1)}, u32[]{:S(2)}, u32[]{:S(2)}) collective-permute-start(bf16[8,32,128]{2,0,1:T(8,128)(2,1)S(1)} %maximum_bitcast_fusion.2), channel_id=1, source_target_pairs={{0,6},{1,7},{2,0},{3,1},{4,2},{5,3},{6,4},{7,5},{8,14},{9,15},{10,... | collective-permute-start | bytes 196616 | tf_op jit(solution)/shard_map/ppermute | solution.py:80
  26.7 0.0 collective-permute-done.1
  26.7 1.1 collective-permute-start.6
  27.8 0.0 collective-permute-done.2
  27.9 0.0 collective-permute-done.3
  27.9 5.1 %collective-permute-done.4 = bf16[8,32,128]{2,0,1:T(8,128)(2,1)S(1)} collective-permute-done((bf16[8,32,128]{2,0,1:T(8,128)(2,1)S(1)}, bf16[8,32,128]{2,0,1:T(8,128)(2,1)S(1)}, u32[]{:S(2)}, u32[]{:S(2)}) %collective-permute-start.4) | collective-permute-done | bytes 65568 | tf_op jit(solution)/shard_map/ppermute | solution.py:80
  33.0 0.0 collective-permute-done.5
  33.0 0.4 collective-permute-done.6
  33.4 1.1 copy.18
  34.6 0.0 all-gather.2.cloned.1.call-update
  34.6 0.0 reduce-scatter.3.cloned.1.call-start
  34.7 0.8 copy.17
  35.4 0.7 compare_select_fusion
  36.2 0.1 copy.19
  36.2 0.1 reshape.240
  36.3 0.1 reshape_squeeze.3
  36.4 30.4 %all-gather.2.cloned.1.call-done = bf16[256,32,128]{2,1,0:T(8,128)(2,1)} async-done(((bf16[64,32,128]{2,1,0:T(8,128)(2,1)}), bf16[256,32,128]{2,1,0:T(8,128)(2,1)}) %all-gather.2.cloned.1.call-update) | async-done | bytes 2097168 | tf_op jit(solution)/shard_map/all_gather | solution.py:83
  66.8 2.8 %gather_fusion = bf16[384,32,128]{2,1,0:T(8,128)(2,1)S(1)} fusion(bf16[256,32,128]{2,1,0:T(8,128)(2,1)} %all-gather.2.cloned.1.call-done, s32[1024]{0:T(1024)S(1)} %pad_clamp_fusion), kind=kCustom, calls=%fused_computation | custom fusion | bytes 6292992 | tf_op jit(solution)/shard_map/gather | solution.py:90
  69.6 0.0 copy-start.2
  69.7 7.0 %fusion.9 = f32[24,32,128]{2,1,0:T(8,128)S(1)} fusion(bf16[24,16,32,128]{3,2,1,0:T(8,128)(2,1)S(1)} %bitcast.68, bf16[1,24,16,128,128]{4,3,2,1,0:T(8,128)(2,1)} %param.6), kind=kOutput, calls=%fused_computation.8 | convolution fusion | flops 402653184 | bytes 16121856 | tf_op jit(solution)/shard_map/tari,taki->tkr/dot_general | solution.py:92
  76.7 0.0 copy-done.2
  76.7 0.8 subtract_convert_fusion
  77.5 0.1 fusion.15
  77.5 5.6 %fusion.6.part_ref = f32[24,16,32,128]{3,2,1,0:T(8,128)S(1)} fusion(bf16[1,24,16,128,128]{4,3,2,1,0:T(8,128)(2,1)} %param.6, bf16[24,16,128]{2,1,0:T(8,128)(2,1)S(1)} %fusion.15, bf16[24,16,128]{2,1,0:T(8,128)(2,1)S(1)} %get-tuple-element.8), kind=kOutput, calls=%fused_computation.7 | convolution fusion | flops 403046400 | bytes 19070976 | tf_op jit(solution)/shard_map/tari,tkr->taki/dot_general | solution.py:103
  83.1 2.5 %shard_map.77 = f32[256,32,128]{2,1,0:T(8,128)S(1)} custom-call(s32[384]{0:T(512)S(1)} %fusion.34.dest_ref, f32[24,16,32,128]{3,2,1,0:T(8,128)S(1)} %fusion.6.part_ref), custom_call_target="tpu_custom_call" | custom-call | tf_op jit(solution)/shard_map/pallas_call | solution.py:56
  85.7 0.0 copy-start
  85.7 1.9 %copy-done = f32[256,32,128]{2,1,0:T(8,128)} copy-done((f32[256,32,128]{2,1,0:T(8,128)}, f32[256,32,128]{2,1,0:T(8,128)S(1)}, u32[]{:S(2)}) %copy-start) | copy-done | bytes 4194328
  87.6 0.0 reduce-scatter.3.cloned.1.call-update
  87.7 0.0 reduce-scatter.5.cloned.1.call-start
  87.7 55.5 %reduce-scatter.3.cloned.1.call-done = f32[32,32,128]{2,1,0:T(8,128)} async-done(((f32[256,32,128]{2,1,0:T(8,128)}), f32[32,32,128]{2,1,0:T(8,128)}) %reduce-scatter.3.cloned.1.call-update) | async-done | bytes 524304 | tf_op jit(solution)/shard_map/reduce_scatter | solution.py:110
  143.2 0.0 reduce-scatter.5.cloned.1.call-update
  143.2 1.9 %collective-permute-start.7 = (f32[1,32,1024]{2,1,0:T(8,128)S(1)}, f32[1,32,1024]{2,1,0:T(8,128)S(1)}, u32[]{:S(2)}, u32[]{:S(2)}) collective-permute-start(f32[1,32,1024]{2,1,0:T(8,128)S(1)} %get-tuple-element.4), channel_id=1, source_target_pairs={{0,32},{32,64},{64,96},{96,128},{128,160},{160,192},{192,224},{1,3... | collective-permute-start | bytes 393224 | tf_op jit(solution)/shard_map/ppermute | solution.py:25
  145.1 3.6 %collective-permute-start.8 = (f32[1,32,1024]{2,1,0:T(8,128)S(1)}, f32[1,32,1024]{2,1,0:T(8,128)S(1)}, u32[]{:S(2)}, u32[]{:S(2)}) collective-permute-start(f32[1,32,1024]{2,1,0:T(8,128)S(1)} %get-tuple-element.4), channel_id=1, source_target_pairs={{32,0},{64,32},{96,64},{128,96},{160,128},{192,160},{224,192},{33,... | collective-permute-start | bytes 393224 | tf_op jit(solution)/shard_map/ppermute | solution.py:27
  148.8 0.7 collective-permute-done.7
  149.5 1.8 %collective-permute-done.8 = f32[1,32,1024]{2,1,0:T(8,128)S(1)} collective-permute-done((f32[1,32,1024]{2,1,0:T(8,128)S(1)}, f32[1,32,1024]{2,1,0:T(8,128)S(1)}, u32[]{:S(2)}, u32[]{:S(2)}) %collective-permute-start.8) | collective-permute-done | bytes 131104 | tf_op jit(solution)/shard_map/ppermute | solution.py:27
  151.3 17.3 %reduce-scatter.5.cloned.1.call-done = f32[8,32,128]{2,1,0:T(8,128)} async-done(((f32[32,32,128]{2,1,0:T(8,128)}), f32[8,32,128]{2,1,0:T(8,128)}) %reduce-scatter.5.cloned.1.call-update) | async-done | bytes 131088 | tf_op jit(solution)/shard_map/reduce_scatter | solution.py:111
  168.6 0.0 copy-done.1
  168.6 0.9 bitcast_add_fusion
  169.5 0.7 slice_bitcast_fusion
  (14 shorter events, 0.2 us)
Async XLA Ops:
  7.2 59.6 %all-gather.2.cloned.1.call-start = ((), (), s32[]{:S(2)}) async-start(), calls=%async_computation.2 | async-start | bytes 2621440 | tf_op jit(solution)/shard_map/all_gather | solution.py:83
  9.1 14.8 %collective-permute-start = (bf16[8,32,128]{2,0,1:T(8,128)(2,1)S(1)}, bf16[8,32,128]{2,0,1:T(8,128)(2,1)S(1)}, u32[]{:S(2)}, u32[]{:S(2)}) collective-permute-start(bf16[8,32,128]{2,0,1:T(8,128)(2,1)S(1)} %maximum_bitcast_fusion.2), channel_id=1, source_target_pairs={{0,1},{1,2},{2,3},{3,4},{4,5},{5,6},{6,7},{7,0},{8,9},{9,10},{10,1... | collective-permute-start | bytes 196616 | tf_op jit(solution)/shard_map/ppermute | solution.py:80
  11.1 15.6 %collective-permute-start.1 = (bf16[8,32,128]{2,0,1:T(8,128)(2,1)S(1)}, bf16[8,32,128]{2,0,1:T(8,128)(2,1)S(1)}, u32[]{:S(2)}, u32[]{:S(2)}) collective-permute-start(bf16[8,32,128]{2,0,1:T(8,128)(2,1)S(1)} %maximum_bitcast_fusion.2), channel_id=1, source_target_pairs={{0,2},{1,3},{2,4},{3,5},{4,6},{5,7},{6,0},{7,1},{8,10},{9,11},{10,... | collective-permute-start | bytes 196616 | tf_op jit(solution)/shard_map/ppermute | solution.py:80
  14.4 13.4 %collective-permute-start.2 = (bf16[8,32,128]{2,0,1:T(8,128)(2,1)S(1)}, bf16[8,32,128]{2,0,1:T(8,128)(2,1)S(1)}, u32[]{:S(2)}, u32[]{:S(2)}) collective-permute-start(bf16[8,32,128]{2,0,1:T(8,128)(2,1)S(1)} %maximum_bitcast_fusion.2), channel_id=1, source_target_pairs={{0,3},{1,4},{2,5},{3,6},{4,7},{5,0},{6,1},{7,2},{8,11},{9,12},{10,... | collective-permute-start | bytes 196616 | tf_op jit(solution)/shard_map/ppermute | solution.py:80
  18.4 9.4 %collective-permute-start.3 = (bf16[8,32,128]{2,0,1:T(8,128)(2,1)S(1)}, bf16[8,32,128]{2,0,1:T(8,128)(2,1)S(1)}, u32[]{:S(2)}, u32[]{:S(2)}) collective-permute-start(bf16[8,32,128]{2,0,1:T(8,128)(2,1)S(1)} %maximum_bitcast_fusion.2), channel_id=1, source_target_pairs={{0,4},{1,5},{2,6},{3,7},{4,0},{5,1},{6,2},{7,3},{8,12},{9,13},{10,... | collective-permute-start | bytes 196616 | tf_op jit(solution)/shard_map/ppermute | solution.py:80
  19.0 14.0 %collective-permute-start.4 = (bf16[8,32,128]{2,0,1:T(8,128)(2,1)S(1)}, bf16[8,32,128]{2,0,1:T(8,128)(2,1)S(1)}, u32[]{:S(2)}, u32[]{:S(2)}) collective-permute-start(bf16[8,32,128]{2,0,1:T(8,128)(2,1)S(1)} %maximum_bitcast_fusion.2), channel_id=1, source_target_pairs={{0,5},{1,6},{2,7},{3,0},{4,1},{5,2},{6,3},{7,4},{8,13},{9,14},{10,... | collective-permute-start | bytes 196616 | tf_op jit(solution)/shard_map/ppermute | solution.py:80
  23.9 9.0 %collective-permute-start.5 = (bf16[8,32,128]{2,0,1:T(8,128)(2,1)S(1)}, bf16[8,32,128]{2,0,1:T(8,128)(2,1)S(1)}, u32[]{:S(2)}, u32[]{:S(2)}) collective-permute-start(bf16[8,32,128]{2,0,1:T(8,128)(2,1)S(1)} %maximum_bitcast_fusion.2), channel_id=1, source_target_pairs={{0,6},{1,7},{2,0},{3,1},{4,2},{5,3},{6,4},{7,5},{8,14},{9,15},{10,... | collective-permute-start | bytes 196616 | tf_op jit(solution)/shard_map/ppermute | solution.py:80
  26.7 6.7 %collective-permute-start.6 = (bf16[8,32,128]{2,0,1:T(8,128)(2,1)S(1)}, bf16[8,32,128]{2,0,1:T(8,128)(2,1)S(1)}, u32[]{:S(2)}, u32[]{:S(2)}) collective-permute-start(bf16[8,32,128]{2,0,1:T(8,128)(2,1)S(1)} %maximum_bitcast_fusion.2), channel_id=1, source_target_pairs={{0,7},{1,0},{2,1},{3,2},{4,3},{5,4},{6,5},{7,6},{8,15},{9,8},{10,9... | collective-permute-start | bytes 196616 | tf_op jit(solution)/shard_map/ppermute | solution.py:80
  34.6 108.6 %reduce-scatter.3.cloned.1.call-start = ((), (), s32[]{:S(2)}) async-start(), calls=%async_computation.3 | async-start | bytes 4718592 | tf_op jit(solution)/shard_map/reduce_scatter | solution.py:110
  69.6 7.1 %copy-start.2 = (s32[1,24,128]{2,1,0:T(8,128)S(1)}, s32[1,24,128]{2,1,0:T(8,128)}, u32[]{:S(2)}) copy-start(s32[1,24,128]{2,1,0:T(8,128)} %param.8) | copy-start | bytes 36868
  85.7 1.9 %copy-start = (f32[256,32,128]{2,1,0:T(8,128)}, f32[256,32,128]{2,1,0:T(8,128)S(1)}, u32[]{:S(2)}) copy-start(f32[256,32,128]{2,1,0:T(8,128)S(1)} %shard_map.77) | copy-start | bytes 12582916
  87.6 80.9 %copy-start.1 = (f32[1024]{0:T(1024)S(1)}, f32[1024]{0:T(1024)}, u32[]{:S(2)}) copy-start(f32[1024]{0:T(1024)} %param.11) | copy-start | bytes 12292
  87.7 80.9 %reduce-scatter.5.cloned.1.call-start = ((), (), s32[]{:S(2)}) async-start(), calls=%async_computation.4 | async-start | bytes 655360 | tf_op jit(solution)/shard_map/reduce_scatter | solution.py:111
  143.2 6.3 %collective-permute-start.7 = (f32[1,32,1024]{2,1,0:T(8,128)S(1)}, f32[1,32,1024]{2,1,0:T(8,128)S(1)}, u32[]{:S(2)}, u32[]{:S(2)}) collective-permute-start(f32[1,32,1024]{2,1,0:T(8,128)S(1)} %get-tuple-element.4), channel_id=1, source_target_pairs={{0,32},{32,64},{64,96},{96,128},{128,160},{160,192},{192,224},{1,3... | collective-permute-start | bytes 393224 | tf_op jit(solution)/shard_map/ppermute | solution.py:25
  145.1 6.1 %collective-permute-start.8 = (f32[1,32,1024]{2,1,0:T(8,128)S(1)}, f32[1,32,1024]{2,1,0:T(8,128)S(1)}, u32[]{:S(2)}, u32[]{:S(2)}) collective-permute-start(f32[1,32,1024]{2,1,0:T(8,128)S(1)} %get-tuple-element.4), channel_id=1, source_target_pairs={{32,0},{64,32},{96,64},{128,96},{160,128},{192,160},{224,192},{33,... | collective-permute-start | bytes 393224 | tf_op jit(solution)/shard_map/ppermute | solution.py:27
Sparse Core Ops, SparseCore 0:
  34.7 32.0 all-gather.1
  87.8 55.3 reduce-scatter.2
  145.7 22.8 reduce-scatter.4

commit v6 on v5

--- a/solution.py
+++ b/solution.py
@@ -80,13 +80,25 @@
         lax.ppermute(by_block, "row_1", [(i, (i + s) % count) for i in range(count)])
         for s in range(1, count)
     ]
-    coef_table = lax.all_gather(jnp.concatenate(pieces, axis=0), "row_0", axis=0, tiled=True)
+    stage = jnp.concatenate(pieces, axis=0)
+    there = lax.axis_index("row_0")
+    around = lax.axis_size("row_0")
+    coef_table = jnp.concatenate(
+        [stage]
+        + [
+            lax.ppermute(stage, "row_0", [(i, (i + s) % around) for i in range(around)])
+            for s in range(1, around)
+        ],
+        axis=0,
+    )
     nblk = coef_table.shape[0]
     both = jnp.concatenate([coef, direction], axis=1)
     neighbours = extended(both, (("day", 0),), 1)
     blks = blocks[0]
     span = count * local_blk
-    rotated = (blks // span) * span + ((here - (blks // local_blk) % count) % count) * local_blk
+    rotated = ((there - blks // span) % around) * span + (
+        (here - (blks // local_blk) % count) % count
+    ) * local_blk
     selected = coef_table[rotated + blks % local_blk]
     feats = features[0]
     logits_dir = jnp.einsum("tari,taki->tkr", feats, selected, preferred_element_type=jnp.float32)
@@ -108,7 +120,13 @@
     dest = ((flat // per) % inner) * (outer * per) + (flat // (inner * per)) * per + flat % per
     partial_terms = scatter_rows(dest, contrib, nblk)
     owned = lax.psum_scatter(partial_terms, "row_1", scatter_dimension=0, tiled=True)
-    owned = lax.psum_scatter(owned, "row_0", scatter_dimension=0, tiled=True)
+    chunks = owned.reshape(around, -1, 2 * arms, width)
+    total = chunks[there]
+    for s in range(1, around):
+        total = total + lax.ppermute(
+            chunks[(there + s) % around], "row_0", [(i, (i + s) % around) for i in range(around)]
+        )
+    owned = total
     owned = owned.transpose(1, 0, 2).reshape(2 * arms, -1)
     day_index = lax.axis_index("day")
     ndays = lax.axis_size("day")

time: 177 us -> 157 us (0.89)
  waiting for transfers between devices: 111 us -> 73 us
  starting transfers between devices: 24.3 us -> 35.6 us
  local copies, waits for them, and re-layouts: 7.74 us -> 13.9 us
    all_gather x1 -> x0, waiting for transfers between devices: 30.4 us -> none  [on_device(): lax.all_gather(jnp.concatenate(pieces, axis=0), 'row_0', axis=0, tiled=True)]
    ppermute x0 -> x6, waiting for transfers between devices: none -> 24.3 us  [the longest x3 19.8 us: on_device(): lax.ppermute(stage, 'row_0', [(i, (i + s) % around) for i in range(around)])]
    reduce_scatter x1 -> x0, waiting for transfers between devices: 17.3 us -> none  [on_device(): owned = lax.psum_scatter(owned, 'row_0', scatter_dimension=0, tiled=True)]
    ppermute x0 -> x6, starting transfers between devices: none -> 11.6 us  [the longest x3 5.84 us: on_device(): lax.ppermute(stage, 'row_0', [(i, (i + s) % around) for i in range(around)])]
    reduce_scatter x1, waiting for transfers between devices: 55.5 us -> 46.8 us  [on_device(): lax.psum_scatter(partial_terms, 'row_1', scatter_dimension=0, tiled=True)]
    unnamed x15 -> x19, local copies, waits for them, and re-layouts: 2.85 us -> 7.6 us
    ppermute x7, waiting for transfers between devices: 5.49 us -> 1.81 us  [on_device(): lax.ppermute(by_block, 'row_1', [(i, (i + s) % count) for i in range(coun...]
    ppermute x1, waiting for transfers between devices: 1.79 us -> 0.01 us  [extended(): lax.ppermute(head, axis, [((i + 1) % count, i) for i in range(ends)])]
  transfers between devices with their start and end apart: 12 -> 16, of which waited for: 7 -> 6; matrix products, arithmetic and copies ran while one was open for 1% -> 5% of each run, Pallas kernels for 0% -> 0%
where the time goes in v6:
time: 157 us; the launch traced here: 156 us
  waiting for transfers between devices  73 us (46%)
  starting transfers between devices  35.6 us (23%)
  between operations  14.2 us (9%)
  local copies, waits for them, and re-layouts  13.9 us (9%)
  matrix products  12.6 us (8%)
  other arithmetic  4.37 us (3%)
  Pallas kernels  2.54 us (2%)
    reduce_scatter x1, waiting for transfers between devices, on_device(): lax.psum_scatter(partial_terms, 'row_1', scatter_dimension=0, tiled=True)  46.8 us
    ppermute x3, waiting for transfers between devices, on_device(): lax.ppermute(stage, 'row_0', [(i, (i + s) % around) for i in range(around)])  19.8 us
    ppermute x7, starting transfers between devices, on_device(): lax.ppermute(by_block, 'row_1', [(i, (i + s) % count) for i in range(coun...  18.5 us
    unnamed x19, local copies, waits for them, and re-layouts  7.6 us
    dot_general x1, matrix products, on_device(): jnp.einsum('tari,taki->tkr', feats, selected, preferred_element_type=jnp....  7.05 us
    ppermute x3, starting transfers between devices, on_device(): lax.ppermute(stage, 'row_0', [(i, (i + s) % around) for i in range(around)])  5.84 us
    ppermute x3, starting transfers between devices, on_device(): lax.ppermute(chunks[(there + s) % around], 'row_0', [(i, (i + s) % around...  5.72 us
    dot_general x1, matrix products, on_device(): jnp.einsum('tari,tkr->taki', feats, both_low, preferred_element_type=jnp....  5.58 us
  transfers between devices with their start and end apart: 16, of which 6 were waited for; matrix products, arithmetic and copies ran while one was open for 5% of the time, Pallas kernels for 0%

profile of v6, /device:TPU:2, one launch (start us, length us, event | category | flops | bytes accessed | tf_op | source)
XLA Modules:
  0.0 156.2 jit_solution(8645848418295797221)
XLA Ops:
  7.2 0.9 constant_dynamic-update-slice_fusion.20
  8.1 0.9 constant_dynamic-update-slice_fusion.19
  9.2 2.0 %collective-permute-start = (bf16[8,32,128]{2,1,0:T(8,128)(2,1)S(1)}, bf16[8,32,128]{2,1,0:T(8,128)(2,1)S(1)}, u32[]{:S(2)}, u32[]{:S(2)}) collective-permute-start(bf16[8,32,128]{2,1,0:T(8,128)(2,1)S(1)} %maximum_bitcast_fusion.2), channel_id=1, source_target_pairs={{0,1},{1,2},{2,3},{3,4},{4,5},{5,6},{6,7},{7,0},{8,9},{9,10},{10,1... | collective-permute-start | bytes 196616 | tf_op jit(solution)/shard_map/ppermute | solution.py:80
  11.1 3.3 %collective-permute-start.1 = (bf16[8,32,128]{2,1,0:T(8,128)(2,1)S(1)}, bf16[8,32,128]{2,1,0:T(8,128)(2,1)S(1)}, u32[]{:S(2)}, u32[]{:S(2)}) collective-permute-start(bf16[8,32,128]{2,1,0:T(8,128)(2,1)S(1)} %maximum_bitcast_fusion.2), channel_id=1, source_target_pairs={{0,2},{1,3},{2,4},{3,5},{4,6},{5,7},{6,0},{7,1},{8,10},{9,11},{10,... | collective-permute-start | bytes 196616 | tf_op jit(solution)/shard_map/ppermute | solution.py:80
  14.4 4.0 %collective-permute-start.2 = (bf16[8,32,128]{2,1,0:T(8,128)(2,1)S(1)}, bf16[8,32,128]{2,1,0:T(8,128)(2,1)S(1)}, u32[]{:S(2)}, u32[]{:S(2)}) collective-permute-start(bf16[8,32,128]{2,1,0:T(8,128)(2,1)S(1)} %maximum_bitcast_fusion.2), channel_id=1, source_target_pairs={{0,3},{1,4},{2,5},{3,6},{4,7},{5,0},{6,1},{7,2},{8,11},{9,12},{10,... | collective-permute-start | bytes 196616 | tf_op jit(solution)/shard_map/ppermute | solution.py:80
  18.5 0.5 collective-permute-start.3
  19.0 4.9 %collective-permute-start.4 = (bf16[8,32,128]{2,1,0:T(8,128)(2,1)S(1)}, bf16[8,32,128]{2,1,0:T(8,128)(2,1)S(1)}, u32[]{:S(2)}, u32[]{:S(2)}) collective-permute-start(bf16[8,32,128]{2,1,0:T(8,128)(2,1)S(1)} %maximum_bitcast_fusion.2), channel_id=1, source_target_pairs={{0,5},{1,6},{2,7},{3,0},{4,1},{5,2},{6,3},{7,4},{8,13},{9,14},{10,... | collective-permute-start | bytes 196616 | tf_op jit(solution)/shard_map/ppermute | solution.py:80
  23.9 0.6 constant_dynamic-update-slice_fusion.7
  24.6 2.7 %collective-permute-start.5 = (bf16[8,32,128]{2,1,0:T(8,128)(2,1)S(1)}, bf16[8,32,128]{2,1,0:T(8,128)(2,1)S(1)}, u32[]{:S(2)}, u32[]{:S(2)}) collective-permute-start(bf16[8,32,128]{2,1,0:T(8,128)(2,1)S(1)} %maximum_bitcast_fusion.2), channel_id=1, source_target_pairs={{0,6},{1,7},{2,0},{3,1},{4,2},{5,3},{6,4},{7,5},{8,14},{9,15},{10,... | collective-permute-start | bytes 196616 | tf_op jit(solution)/shard_map/ppermute | solution.py:80
  27.3 0.6 constant_dynamic-update-slice_fusion.6
  27.9 1.0 collective-permute-start.6
  28.9 0.6 constant_dynamic-update-slice_fusion.5
  29.6 0.6 constant_dynamic-update-slice_fusion.4
  30.2 0.6 constant_dynamic-update-slice_fusion.3
  30.9 1.8 %collective-permute-done.4 = bf16[8,32,128]{2,1,0:T(8,128)(2,1)S(1)} collective-permute-done((bf16[8,32,128]{2,1,0:T(8,128)(2,1)S(1)}, bf16[8,32,128]{2,1,0:T(8,128)(2,1)S(1)}, u32[]{:S(2)}, u32[]{:S(2)}) %collective-permute-start.4) | collective-permute-done | bytes 65568 | tf_op jit(solution)/shard_map/ppermute | solution.py:80
  32.7 0.6 constant_dynamic-update-slice_fusion.2
  33.3 0.7 constant_dynamic-update-slice_fusion.1
  34.0 0.6 constant_dynamic-update-slice_fusion
  34.6 1.6 %collective-permute-start.7 = (bf16[64,32,128]{2,1,0:T(8,128)(2,1)S(1)}, bf16[64,32,128]{2,1,0:T(8,128)(2,1)S(1)}, u32[]{:S(2)}, u32[]{:S(2)}) collective-permute-start(bf16[64,32,128]{2,1,0:T(8,128)(2,1)S(1)} %get-tuple-element.11), channel_id=1, source_target_pairs={{0,8},{8,16},{16,24},{24,0},{1,9},{9,17},{17,25},{25,1},{2,10},{10... | collective-permute-start | bytes 1572872 | tf_op jit(solution)/shard_map/ppermute | solution.py:89
  36.2 2.9 %collective-permute-start.8 = (bf16[64,32,128]{2,1,0:T(8,128)(2,1)S(1)}, bf16[64,32,128]{2,1,0:T(8,128)(2,1)S(1)}, u32[]{:S(2)}, u32[]{:S(2)}) collective-permute-start(bf16[64,32,128]{2,1,0:T(8,128)(2,1)S(1)} %get-tuple-element.11), channel_id=1, source_target_pairs={{0,16},{8,24},{16,0},{24,8},{1,17},{9,25},{17,1},{25,9},{2,18},{10... | collective-permute-start | bytes 1572872 | tf_op jit(solution)/shard_map/ppermute | solution.py:89
  39.1 0.1 copy.14
  39.2 0.1 reshape.280
  39.3 1.4 collective-permute-start.9
  40.6 0.1 copy.11
  40.7 0.1 reshape_squeeze.3
  40.8 8.7 %collective-permute-done.7 = bf16[64,32,128]{2,1,0:T(8,128)(2,1)S(1)} collective-permute-done((bf16[64,32,128]{2,1,0:T(8,128)(2,1)S(1)}, bf16[64,32,128]{2,1,0:T(8,128)(2,1)S(1)}, u32[]{:S(2)}, u32[]{:S(2)}) %collective-permute-start.7) | collective-permute-done | bytes 524320 | tf_op jit(solution)/shard_map/ppermute | solution.py:89
  49.5 0.8 constant_dynamic-update-slice_fusion.10
  50.3 11.1 %collective-permute-done.8 = bf16[64,32,128]{2,1,0:T(8,128)(2,1)S(1)} collective-permute-done((bf16[64,32,128]{2,1,0:T(8,128)(2,1)S(1)}, bf16[64,32,128]{2,1,0:T(8,128)(2,1)S(1)}, u32[]{:S(2)}, u32[]{:S(2)}) %collective-permute-start.8) | collective-permute-done | bytes 524320 | tf_op jit(solution)/shard_map/ppermute | solution.py:89
  61.5 0.9 constant_dynamic-update-slice_fusion.9
  62.3 0.8 constant_dynamic-update-slice_fusion.8
  63.2 2.8 %gather_fusion = bf16[384,32,128]{2,1,0:T(8,128)(2,1)S(1)} fusion(bf16[256,32,128]{2,1,0:T(8,128)(2,1)} %constant_dynamic-update-slice_fusion.8, s32[1024]{0:T(1024)S(1)} %pad_clamp_fusion), kind=kCustom, calls=%fused_computation | custom fusion | bytes 6292992 | tf_op jit(solution)/shard_map/gather | solution.py:102
  66.0 7.0 %fusion.9 = f32[24,32,128]{2,1,0:T(8,128)S(1)} fusion(bf16[24,16,32,128]{3,2,1,0:T(8,128)(2,1)S(1)} %bitcast.86, bf16[1,24,16,128,128]{4,3,2,1,0:T(8,128)(2,1)} %param.6), kind=kOutput, calls=%fused_computation.8 | convolution fusion | flops 402653184 | bytes 16121856 | tf_op jit(solution)/shard_map/tari,taki->tkr/dot_general | solution.py:104
  73.1 0.8 subtract_convert_fusion
  73.8 0.1 fusion.15
  73.9 5.6 %fusion.6.part_ref = f32[24,16,32,128]{3,2,1,0:T(8,128)S(1)} fusion(bf16[1,24,16,128,128]{4,3,2,1,0:T(8,128)(2,1)} %param.6, bf16[24,16,128]{2,1,0:T(8,128)(2,1)S(1)} %fusion.15, bf16[24,16,128]{2,1,0:T(8,128)(2,1)S(1)} %get-tuple-element.27), kind=kOutput, calls=%fused_computation.7 | convolution fusion | flops 403046400 | bytes 19070976 | tf_op jit(solution)/shard_map/tari,tkr->taki/dot_general | solution.py:115
  79.5 2.5 %shard_map.77 = f32[256,32,128]{2,1,0:T(8,128)S(1)} custom-call(s32[384]{0:T(512)S(1)} %fusion.38.dest_ref, f32[24,16,32,128]{3,2,1,0:T(8,128)S(1)} %fusion.6.part_ref), custom_call_target="tpu_custom_call" | custom-call | tf_op jit(solution)/shard_map/pallas_call | solution.py:56
  82.1 1.9 %copy-done = f32[256,32,128]{2,1,0:T(8,128)} copy-done((f32[256,32,128]{2,1,0:T(8,128)}, f32[256,32,128]{2,1,0:T(8,128)S(1)}, u32[]{:S(2)}) %copy-start) | copy-done | bytes 4194328
  84.0 1.9 %collective-permute-start.13 = (f32[1,32,1024]{2,1,0:T(8,128)S(1)}, f32[1,32,1024]{2,1,0:T(8,128)S(1)}, u32[]{:S(2)}, u32[]{:S(2)}) collective-permute-start(f32[1,32,1024]{2,1,0:T(8,128)S(1)} %get-tuple-element.7), channel_id=1, source_target_pairs={{0,32},{32,64},{64,96},{96,128},{128,160},{160,192},{192,224},{1,3... | collective-permute-start | bytes 393224 | tf_op jit(solution)/shard_map/ppermute | solution.py:25
  85.9 3.6 %collective-permute-start.14 = (f32[1,32,1024]{2,1,0:T(8,128)S(1)}, f32[1,32,1024]{2,1,0:T(8,128)S(1)}, u32[]{:S(2)}, u32[]{:S(2)}) collective-permute-start(f32[1,32,1024]{2,1,0:T(8,128)S(1)} %get-tuple-element.7), channel_id=1, source_target_pairs={{32,0},{64,32},{96,64},{128,96},{160,128},{192,160},{224,192},{33,... | collective-permute-start | bytes 393224 | tf_op jit(solution)/shard_map/ppermute | solution.py:27
  89.6 46.8 %reduce-scatter.2.cloned.1.call-done = f32[32,32,128]{2,1,0:T(8,128)} async-done(((f32[256,32,128]{2,1,0:T(8,128)}), f32[32,32,128]{2,1,0:T(8,128)}) %reduce-scatter.2.cloned.1.call-update) | async-done | bytes 524304 | tf_op jit(solution)/shard_map/reduce_scatter | solution.py:122
  136.5 1.1 dynamic-slice_bitcast_fusion.2
  137.5 1.6 collective-permute-start.10
  139.1 2.7 %collective-permute-start.11 = (f32[8,32,128]{2,1,0:T(8,128)S(1)}, f32[8,32,128]{2,1,0:T(8,128)S(1)}, u32[]{:S(2)}, u32[]{:S(2)}) collective-permute-start(f32[8,32,128]{2,1,0:T(8,128)S(1)} %get-tuple-element.4), channel_id=1, source_target_pairs={{0,16},{8,24},{16,0},{24,8},{1,17},{9,25},{17,1},{25,9},{2,18},{10... | collective-permute-start | bytes 393224 | tf_op jit(solution)/shard_map/ppermute | solution.py:126
  141.8 1.5 collective-permute-start.12
  143.2 0.9 collective-permute-done.10
  144.2 3.6 %collective-permute-done.11 = f32[8,32,128]{2,1,0:T(8,128)S(1)} collective-permute-done((f32[8,32,128]{2,1,0:T(8,128)S(1)}, f32[8,32,128]{2,1,0:T(8,128)S(1)}, u32[]{:S(2)}, u32[]{:S(2)}) %collective-permute-start.11) | collective-permute-done | bytes 131104 | tf_op jit(solution)/shard_map/ppermute | solution.py:126
  147.8 1.0 bitcast_add_fusion
  148.7 0.7 slice_bitcast_fusion
  (27 shorter events, 0.2 us)
Async XLA Ops:
  7.2 31.9 %copy-start.1 = (s32[1,24,16]{1,2,0:T(8,128)S(1)}, s32[1,24,16]{1,2,0:T(8,128)}, u32[]{:S(2)}) copy-start(s32[1,24,16]{1,2,0:T(8,128)} %param.7) | copy-start | bytes 4612
  7.2 129.3 %reduce-scatter.2.cloned.1.call-start = ((), (), s32[]{:S(2)}) async-start(), calls=%async_computation.1 | async-start | bytes 4718592 | tf_op jit(solution)/shard_map/reduce_scatter | solution.py:122
  9.2 15.4 %collective-permute-start = (bf16[8,32,128]{2,1,0:T(8,128)(2,1)S(1)}, bf16[8,32,128]{2,1,0:T(8,128)(2,1)S(1)}, u32[]{:S(2)}, u32[]{:S(2)}) collective-permute-start(bf16[8,32,128]{2,1,0:T(8,128)(2,1)S(1)} %maximum_bitcast_fusion.2), channel_id=1, source_target_pairs={{0,1},{1,2},{2,3},{3,4},{4,5},{5,6},{6,7},{7,0},{8,9},{9,10},{10,1... | collective-permute-start | bytes 196616 | tf_op jit(solution)/shard_map/ppermute | solution.py:80
  11.1 16.8 %collective-permute-start.1 = (bf16[8,32,128]{2,1,0:T(8,128)(2,1)S(1)}, bf16[8,32,128]{2,1,0:T(8,128)(2,1)S(1)}, u32[]{:S(2)}, u32[]{:S(2)}) collective-permute-start(bf16[8,32,128]{2,1,0:T(8,128)(2,1)S(1)} %maximum_bitcast_fusion.2), channel_id=1, source_target_pairs={{0,2},{1,3},{2,4},{3,5},{4,6},{5,7},{6,0},{7,1},{8,10},{9,11},{10,... | collective-permute-start | bytes 196616 | tf_op jit(solution)/shard_map/ppermute | solution.py:80
  14.4 15.1 %collective-permute-start.2 = (bf16[8,32,128]{2,1,0:T(8,128)(2,1)S(1)}, bf16[8,32,128]{2,1,0:T(8,128)(2,1)S(1)}, u32[]{:S(2)}, u32[]{:S(2)}) collective-permute-start(bf16[8,32,128]{2,1,0:T(8,128)(2,1)S(1)} %maximum_bitcast_fusion.2), channel_id=1, source_target_pairs={{0,3},{1,4},{2,5},{3,6},{4,7},{5,0},{6,1},{7,2},{8,11},{9,12},{10,... | collective-permute-start | bytes 196616 | tf_op jit(solution)/shard_map/ppermute | solution.py:80
  18.5 11.8 %collective-permute-start.3 = (bf16[8,32,128]{2,1,0:T(8,128)(2,1)S(1)}, bf16[8,32,128]{2,1,0:T(8,128)(2,1)S(1)}, u32[]{:S(2)}, u32[]{:S(2)}) collective-permute-start(bf16[8,32,128]{2,1,0:T(8,128)(2,1)S(1)} %maximum_bitcast_fusion.2), channel_id=1, source_target_pairs={{0,4},{1,5},{2,6},{3,7},{4,0},{5,1},{6,2},{7,3},{8,12},{9,13},{10,... | collective-permute-start | bytes 196616 | tf_op jit(solution)/shard_map/ppermute | solution.py:80
  19.0 13.7 %collective-permute-start.4 = (bf16[8,32,128]{2,1,0:T(8,128)(2,1)S(1)}, bf16[8,32,128]{2,1,0:T(8,128)(2,1)S(1)}, u32[]{:S(2)}, u32[]{:S(2)}) collective-permute-start(bf16[8,32,128]{2,1,0:T(8,128)(2,1)S(1)} %maximum_bitcast_fusion.2), channel_id=1, source_target_pairs={{0,5},{1,6},{2,7},{3,0},{4,1},{5,2},{6,3},{7,4},{8,13},{9,14},{10,... | collective-permute-start | bytes 196616 | tf_op jit(solution)/shard_map/ppermute | solution.py:80
  24.6 8.7 %collective-permute-start.5 = (bf16[8,32,128]{2,1,0:T(8,128)(2,1)S(1)}, bf16[8,32,128]{2,1,0:T(8,128)(2,1)S(1)}, u32[]{:S(2)}, u32[]{:S(2)}) collective-permute-start(bf16[8,32,128]{2,1,0:T(8,128)(2,1)S(1)} %maximum_bitcast_fusion.2), channel_id=1, source_target_pairs={{0,6},{1,7},{2,0},{3,1},{4,2},{5,3},{6,4},{7,5},{8,14},{9,15},{10,... | collective-permute-start | bytes 196616 | tf_op jit(solution)/shard_map/ppermute | solution.py:80
  27.9 6.0 %collective-permute-start.6 = (bf16[8,32,128]{2,1,0:T(8,128)(2,1)S(1)}, bf16[8,32,128]{2,1,0:T(8,128)(2,1)S(1)}, u32[]{:S(2)}, u32[]{:S(2)}) collective-permute-start(bf16[8,32,128]{2,1,0:T(8,128)(2,1)S(1)} %maximum_bitcast_fusion.2), channel_id=1, source_target_pairs={{0,7},{1,0},{2,1},{3,2},{4,3},{5,4},{6,5},{7,6},{8,15},{9,8},{10,9... | collective-permute-start | bytes 196616 | tf_op jit(solution)/shard_map/ppermute | solution.py:80
  34.6 14.9 %collective-permute-start.7 = (bf16[64,32,128]{2,1,0:T(8,128)(2,1)S(1)}, bf16[64,32,128]{2,1,0:T(8,128)(2,1)S(1)}, u32[]{:S(2)}, u32[]{:S(2)}) collective-permute-start(bf16[64,32,128]{2,1,0:T(8,128)(2,1)S(1)} %get-tuple-element.11), channel_id=1, source_target_pairs={{0,8},{8,16},{16,24},{24,0},{1,9},{9,17},{17,25},{25,1},{2,10},{10... | collective-permute-start | bytes 1572872 | tf_op jit(solution)/shard_map/ppermute | solution.py:89
  36.2 25.3 %collective-permute-start.8 = (bf16[64,32,128]{2,1,0:T(8,128)(2,1)S(1)}, bf16[64,32,128]{2,1,0:T(8,128)(2,1)S(1)}, u32[]{:S(2)}, u32[]{:S(2)}) collective-permute-start(bf16[64,32,128]{2,1,0:T(8,128)(2,1)S(1)} %get-tuple-element.11), channel_id=1, source_target_pairs={{0,16},{8,24},{16,0},{24,8},{1,17},{9,25},{17,1},{25,9},{2,18},{10... | collective-permute-start | bytes 1572872 | tf_op jit(solution)/shard_map/ppermute | solution.py:89
  39.3 23.1 %collective-permute-start.9 = (bf16[64,32,128]{2,1,0:T(8,128)(2,1)S(1)}, bf16[64,32,128]{2,1,0:T(8,128)(2,1)S(1)}, u32[]{:S(2)}, u32[]{:S(2)}) collective-permute-start(bf16[64,32,128]{2,1,0:T(8,128)(2,1)S(1)} %get-tuple-element.11), channel_id=1, source_target_pairs={{0,24},{8,0},{16,8},{24,16},{1,25},{9,1},{17,9},{25,17},{2,26},{10... | collective-permute-start | bytes 1572872 | tf_op jit(solution)/shard_map/ppermute | solution.py:89
  66.0 7.1 %copy-start.3 = (s32[1,24,128]{2,1,0:T(8,128)S(1)}, s32[1,24,128]{2,1,0:T(8,128)}, u32[]{:S(2)}) copy-start(s32[1,24,128]{2,1,0:T(8,128)} %param.8) | copy-start | bytes 36868
  82.1 1.9 %copy-start = (f32[256,32,128]{2,1,0:T(8,128)}, f32[256,32,128]{2,1,0:T(8,128)S(1)}, u32[]{:S(2)}) copy-start(f32[256,32,128]{2,1,0:T(8,128)S(1)} %shard_map.77) | copy-start | bytes 12582916
  84.0 63.8 %copy-start.2 = (f32[1024]{0:T(1024)S(1)}, f32[1024]{0:T(1024)}, u32[]{:S(2)}) copy-start(f32[1024]{0:T(1024)} %param.11) | copy-start | bytes 12292
  84.0 59.2 %collective-permute-start.13 = (f32[1,32,1024]{2,1,0:T(8,128)S(1)}, f32[1,32,1024]{2,1,0:T(8,128)S(1)}, u32[]{:S(2)}, u32[]{:S(2)}) collective-permute-start(f32[1,32,1024]{2,1,0:T(8,128)S(1)} %get-tuple-element.7), channel_id=1, source_target_pairs={{0,32},{32,64},{64,96},{96,128},{128,160},{160,192},{192,224},{1,3... | collective-permute-start | bytes 393224 | tf_op jit(solution)/shard_map/ppermute | solution.py:25
  85.9 57.3 %collective-permute-start.14 = (f32[1,32,1024]{2,1,0:T(8,128)S(1)}, f32[1,32,1024]{2,1,0:T(8,128)S(1)}, u32[]{:S(2)}, u32[]{:S(2)}) collective-permute-start(f32[1,32,1024]{2,1,0:T(8,128)S(1)} %get-tuple-element.7), channel_id=1, source_target_pairs={{32,0},{64,32},{96,64},{128,96},{160,128},{192,160},{224,192},{33,... | collective-permute-start | bytes 393224 | tf_op jit(solution)/shard_map/ppermute | solution.py:27
  137.5 6.6 %collective-permute-start.10 = (f32[8,32,128]{2,1,0:T(8,128)S(1)}, f32[8,32,128]{2,1,0:T(8,128)S(1)}, u32[]{:S(2)}, u32[]{:S(2)}) collective-permute-start(f32[8,32,128]{2,1,0:T(8,128)S(1)} %get-tuple-element.2), channel_id=1, source_target_pairs={{0,8},{8,16},{16,24},{24,0},{1,9},{9,17},{17,25},{25,1},{2,10},{10... | collective-permute-start | bytes 393224 | tf_op jit(solution)/shard_map/ppermute | solution.py:126
  139.1 8.7 %collective-permute-start.11 = (f32[8,32,128]{2,1,0:T(8,128)S(1)}, f32[8,32,128]{2,1,0:T(8,128)S(1)}, u32[]{:S(2)}, u32[]{:S(2)}) collective-permute-start(f32[8,32,128]{2,1,0:T(8,128)S(1)} %get-tuple-element.4), channel_id=1, source_target_pairs={{0,16},{8,24},{16,0},{24,8},{1,17},{9,25},{17,1},{25,9},{2,18},{10... | collective-permute-start | bytes 393224 | tf_op jit(solution)/shard_map/ppermute | solution.py:126
  141.8 6.0 %collective-permute-start.12 = (f32[8,32,128]{2,1,0:T(8,128)S(1)}, f32[8,32,128]{2,1,0:T(8,128)S(1)}, u32[]{:S(2)}, u32[]{:S(2)}) collective-permute-start(f32[8,32,128]{2,1,0:T(8,128)S(1)} %get-tuple-element.3), channel_id=1, source_target_pairs={{0,24},{8,0},{16,8},{24,16},{1,25},{9,1},{17,9},{25,17},{2,26},{10... | collective-permute-start | bytes 393224 | tf_op jit(solution)/shard_map/ppermute | solution.py:126
Sparse Core Ops, SparseCore 0:
  84.1 52.2 reduce-scatter.1

commit v7 on v6

--- a/solution.py
+++ b/solution.py
@@ -119,14 +119,26 @@
     flat = blks.reshape(-1)
     dest = ((flat // per) % inner) * (outer * per) + (flat // (inner * per)) * per + flat % per
     partial_terms = scatter_rows(dest, contrib, nblk)
-    owned = lax.psum_scatter(partial_terms, "row_1", scatter_dimension=0, tiled=True)
-    chunks = owned.reshape(around, -1, 2 * arms, width)
+    grad_part = partial_terms[:, :arms]
+    hv_part = partial_terms[:, arms:].reshape(count, around, local_blk, arms, width)
+    owned = lax.psum_scatter(grad_part, "row_1", scatter_dimension=0, tiled=True)
+    chunks = owned.reshape(around, -1, arms, width)
     total = chunks[there]
     for s in range(1, around):
         total = total + lax.ppermute(
             chunks[(there + s) % around], "row_0", [(i, (i + s) % around) for i in range(around)]
         )
-    owned = total
+    across = hv_part[:, there]
+    for s in range(1, around):
+        across = across + lax.ppermute(
+            hv_part[:, (there + s) % around], "row_0", [(i, (i + s) % around) for i in range(around)]
+        )
+    hv_total = across[here]
+    for s in range(1, count):
+        hv_total = hv_total + lax.ppermute(
+            across[(here + s) % count], "row_1", [(i, (i + s) % count) for i in range(count)]
+        )
+    owned = jnp.concatenate([total, hv_total], axis=1)
     owned = owned.transpose(1, 0, 2).reshape(2 * arms, -1)
     day_index = lax.axis_index("day")
     ndays = lax.axis_size("day")

time: 157 us -> 156 us (level)
  waiting for transfers between devices: 73 us -> 52 us
  starting transfers between devices: 35.6 us -> 53.8 us
    reduce_scatter x1, waiting for transfers between devices: 46.8 us -> 4.93 us  [on_device(): lax.psum_scatter(grad_part, 'row_1', scatter_dimension=0, tiled=True)]
    ppermute x0 -> x10, waiting for transfers between devices: none -> 21.9 us  [the longest x3 21.7 us: on_device(): lax.ppermute(hv_part[:, (there + s) % around], 'row_0', [(i, (i + s) % ar...]
    ppermute x0 -> x10, starting transfers between devices: none -> 18.1 us  [the longest x7 13.7 us: on_device(): lax.ppermute(across[(here + s) % count], 'row_1', [(i, (i + s) % count) f...]
    add x0 -> x3, other arithmetic: none -> 2.41 us  [the longest x1 1.51 us: on_device(): across + lax.ppermute(hv_part[:, (there + s) % around], 'row_0', [(i, (i...]
    unnamed x19 -> x17, local copies, waits for them, and re-layouts: 7.6 us -> 5.65 us
    slice x0 -> x1, local copies, waits for them, and re-layouts: none -> 1.7 us  [on_device(): grad_part = partial_terms[:, :arms]]
  transfers between devices with their start and end apart: 16 -> 26, of which waited for: 6 -> 9; matrix products, arithmetic and copies ran while one was open for 5% -> 7% of each run, Pallas kernels for 0% -> 0%
where the time goes in v7:
time: 156 us
  starting transfers between devices  53.8 us (34%)
  waiting for transfers between devices  52 us (33%)
  local copies, waits for them, and re-layouts  14.5 us (9%)
  between operations  14.3 us (9%)
  matrix products  12.6 us (8%)
  other arithmetic  5.86 us (4%)
  Pallas kernels  2.54 us (2%)
    ppermute x3, waiting for transfers between devices, on_device(): lax.ppermute(hv_part[:, (there + s) % around], 'row_0', [(i, (i + s) % ar...  21.7 us
    ppermute x3, waiting for transfers between devices, on_device(): lax.ppermute(stage, 'row_0', [(i, (i + s) % around) for i in range(around)])  19.8 us
    ppermute x7, starting transfers between devices, on_device(): lax.ppermute(by_block, 'row_1', [(i, (i + s) % count) for i in range(coun...  18.5 us
    ppermute x7, starting transfers between devices, on_device(): lax.ppermute(across[(here + s) % count], 'row_1', [(i, (i + s) % count) f...  13.7 us
    dot_general x1, matrix products, on_device(): jnp.einsum('tari,taki->tkr', feats, selected, preferred_element_type=jnp....  7.04 us
    ppermute x3, starting transfers between devices, on_device(): lax.ppermute(stage, 'row_0', [(i, (i + s) % around) for i in range(around)])  5.84 us
    ppermute x3, starting transfers between devices, on_device(): lax.ppermute(chunks[(there + s) % around], 'row_0', [(i, (i + s) % around...  5.82 us
    unnamed x17, local copies, waits for them, and re-layouts  5.65 us
  transfers between devices with their start and end apart: 26, of which 9 were waited for; matrix products, arithmetic and copies ran while one was open for 7% of the time, Pallas kernels for 0%

profile of v7, /device:TPU:2, one launch (start us, length us, event | category | flops | bytes accessed | tf_op | source)
XLA Modules:
  0.0 155.6 jit_solution(13224408461434835654)
XLA Ops:
  7.2 0.9 constant_dynamic-update-slice_fusion.20
  8.1 0.9 constant_dynamic-update-slice_fusion.19
  9.2 2.0 %collective-permute-start = (bf16[8,32,128]{2,1,0:T(8,128)(2,1)S(1)}, bf16[8,32,128]{2,1,0:T(8,128)(2,1)S(1)}, u32[]{:S(2)}, u32[]{:S(2)}) collective-permute-start(bf16[8,32,128]{2,1,0:T(8,128)(2,1)S(1)} %maximum_bitcast_fusion.3), channel_id=1, source_target_pairs={{0,1},{1,2},{2,3},{3,4},{4,5},{5,6},{6,7},{7,0},{8,9},{9,10},{10,1... | collective-permute-start | bytes 196616 | tf_op jit(solution)/shard_map/ppermute | solution.py:80
  11.1 3.3 %collective-permute-start.1 = (bf16[8,32,128]{2,1,0:T(8,128)(2,1)S(1)}, bf16[8,32,128]{2,1,0:T(8,128)(2,1)S(1)}, u32[]{:S(2)}, u32[]{:S(2)}) collective-permute-start(bf16[8,32,128]{2,1,0:T(8,128)(2,1)S(1)} %maximum_bitcast_fusion.3), channel_id=1, source_target_pairs={{0,2},{1,3},{2,4},{3,5},{4,6},{5,7},{6,0},{7,1},{8,10},{9,11},{10,... | collective-permute-start | bytes 196616 | tf_op jit(solution)/shard_map/ppermute | solution.py:80
  14.4 4.0 %collective-permute-start.2 = (bf16[8,32,128]{2,1,0:T(8,128)(2,1)S(1)}, bf16[8,32,128]{2,1,0:T(8,128)(2,1)S(1)}, u32[]{:S(2)}, u32[]{:S(2)}) collective-permute-start(bf16[8,32,128]{2,1,0:T(8,128)(2,1)S(1)} %maximum_bitcast_fusion.3), channel_id=1, source_target_pairs={{0,3},{1,4},{2,5},{3,6},{4,7},{5,0},{6,1},{7,2},{8,11},{9,12},{10,... | collective-permute-start | bytes 196616 | tf_op jit(solution)/shard_map/ppermute | solution.py:80
  19.0 4.9 %collective-permute-start.4 = (bf16[8,32,128]{2,1,0:T(8,128)(2,1)S(1)}, bf16[8,32,128]{2,1,0:T(8,128)(2,1)S(1)}, u32[]{:S(2)}, u32[]{:S(2)}) collective-permute-start(bf16[8,32,128]{2,1,0:T(8,128)(2,1)S(1)} %maximum_bitcast_fusion.3), channel_id=1, source_target_pairs={{0,5},{1,6},{2,7},{3,0},{4,1},{5,2},{6,3},{7,4},{8,13},{9,14},{10,... | collective-permute-start | bytes 196616 | tf_op jit(solution)/shard_map/ppermute | solution.py:80
  24.6 2.7 %collective-permute-start.5 = (bf16[8,32,128]{2,1,0:T(8,128)(2,1)S(1)}, bf16[8,32,128]{2,1,0:T(8,128)(2,1)S(1)}, u32[]{:S(2)}, u32[]{:S(2)}) collective-permute-start(bf16[8,32,128]{2,1,0:T(8,128)(2,1)S(1)} %maximum_bitcast_fusion.3), channel_id=1, source_target_pairs={{0,6},{1,7},{2,0},{3,1},{4,2},{5,3},{6,4},{7,5},{8,14},{9,15},{10,... | collective-permute-start | bytes 196616 | tf_op jit(solution)/shard_map/ppermute | solution.py:80
  27.9 1.0 collective-permute-start.6
  29.6 0.7 constant_dynamic-update-slice_fusion.4
  30.9 1.8 %collective-permute-done.4 = bf16[8,32,128]{2,1,0:T(8,128)(2,1)S(1)} collective-permute-done((bf16[8,32,128]{2,1,0:T(8,128)(2,1)S(1)}, bf16[8,32,128]{2,1,0:T(8,128)(2,1)S(1)}, u32[]{:S(2)}, u32[]{:S(2)}) %collective-permute-start.4) | collective-permute-done | bytes 65568 | tf_op jit(solution)/shard_map/ppermute | solution.py:80
  34.6 1.6 %collective-permute-start.7 = (bf16[64,32,128]{2,1,0:T(8,128)(2,1)S(1)}, bf16[64,32,128]{2,1,0:T(8,128)(2,1)S(1)}, u32[]{:S(2)}, u32[]{:S(2)}) collective-permute-start(bf16[64,32,128]{2,1,0:T(8,128)(2,1)S(1)} %get-tuple-element.23), channel_id=1, source_target_pairs={{0,8},{8,16},{16,24},{24,0},{1,9},{9,17},{17,25},{25,1},{2,10},{10... | collective-permute-start | bytes 1572872 | tf_op jit(solution)/shard_map/ppermute | solution.py:89
  36.2 2.9 %collective-permute-start.8 = (bf16[64,32,128]{2,1,0:T(8,128)(2,1)S(1)}, bf16[64,32,128]{2,1,0:T(8,128)(2,1)S(1)}, u32[]{:S(2)}, u32[]{:S(2)}) collective-permute-start(bf16[64,32,128]{2,1,0:T(8,128)(2,1)S(1)} %get-tuple-element.23), channel_id=1, source_target_pairs={{0,16},{8,24},{16,0},{24,8},{1,17},{9,25},{17,1},{25,9},{2,18},{10... | collective-permute-start | bytes 1572872 | tf_op jit(solution)/shard_map/ppermute | solution.py:89
  39.3 1.4 collective-permute-start.9
  40.8 8.7 %collective-permute-done.7 = bf16[64,32,128]{2,1,0:T(8,128)(2,1)S(1)} collective-permute-done((bf16[64,32,128]{2,1,0:T(8,128)(2,1)S(1)}, bf16[64,32,128]{2,1,0:T(8,128)(2,1)S(1)}, u32[]{:S(2)}, u32[]{:S(2)}) %collective-permute-start.7) | collective-permute-done | bytes 524320 | tf_op jit(solution)/shard_map/ppermute | solution.py:89
  49.5 0.8 constant_dynamic-update-slice_fusion.10
  50.3 11.1 %collective-permute-done.8 = bf16[64,32,128]{2,1,0:T(8,128)(2,1)S(1)} collective-permute-done((bf16[64,32,128]{2,1,0:T(8,128)(2,1)S(1)}, bf16[64,32,128]{2,1,0:T(8,128)(2,1)S(1)}, u32[]{:S(2)}, u32[]{:S(2)}) %collective-permute-start.8) | collective-permute-done | bytes 524320 | tf_op jit(solution)/shard_map/ppermute | solution.py:89
  61.5 0.8 constant_dynamic-update-slice_fusion.9
  62.3 0.8 constant_dynamic-update-slice_fusion.8
  63.2 2.8 %gather_fusion = bf16[384,32,128]{2,1,0:T(8,128)(2,1)S(1)} fusion(bf16[256,32,128]{2,1,0:T(8,128)(2,1)} %constant_dynamic-update-slice_fusion.8, s32[1024]{0:T(1024)S(1)} %pad_clamp_fusion), kind=kCustom, calls=%fused_computation | custom fusion | bytes 6292992 | tf_op jit(solution)/shard_map/gather | solution.py:102
  66.0 7.0 %fusion.9 = f32[24,32,128]{2,1,0:T(8,128)S(1)} fusion(bf16[24,16,32,128]{3,2,1,0:T(8,128)(2,1)S(1)} %bitcast.124, bf16[1,24,16,128,128]{4,3,2,1,0:T(8,128)(2,1)} %param.6), kind=kOutput, calls=%fused_computation.8 | convolution fusion | flops 402653184 | bytes 16121856 | tf_op jit(solution)/shard_map/tari,taki->tkr/dot_general | solution.py:104
  73.0 0.8 subtract_convert_fusion
  73.9 5.6 %fusion.6.part_ref = f32[24,16,32,128]{3,2,1,0:T(8,128)S(1)} fusion(bf16[1,24,16,128,128]{4,3,2,1,0:T(8,128)(2,1)} %param.6, bf16[24,16,128]{2,1,0:T(8,128)(2,1)S(1)} %fusion.15, bf16[24,16,128]{2,1,0:T(8,128)(2,1)S(1)} %get-tuple-element.39), kind=kOutput, calls=%fused_computation.7 | convolution fusion | flops 403046400 | bytes 19070976 | tf_op jit(solution)/shard_map/tari,tkr->taki/dot_general | solution.py:115
  79.5 2.5 %shard_map.77 = f32[256,32,128]{2,1,0:T(8,128)S(1)} custom-call(s32[384]{0:T(512)S(1)} %fusion.45.dest_ref, f32[24,16,32,128]{3,2,1,0:T(8,128)S(1)} %fusion.6.part_ref), custom_call_target="tpu_custom_call" | custom-call | tf_op jit(solution)/shard_map/pallas_call | solution.py:56
  82.0 1.7 %fusion.50 = (f32[256,16,128]{2,1,0:T(8,128)}, f32[256,16,128]{2,1,0:T(8,128)S(1)}) fusion(f32[256,32,128]{2,1,0:T(8,128)S(1)} %shard_map.77), kind=kLoop, calls=%fused_computation.130 | loop fusion | bytes 8388608 | tf_op jit(solution)/shard_map/slice | solution.py:122
  83.8 1.0 dynamic-slice_bitcast_fusion.2
  85.3 2.2 %collective-permute-start.14 = (f32[8,8,16,128]{3,2,1,0:T(8,128)S(1)}, f32[8,8,16,128]{3,2,1,0:T(8,128)}, u32[]{:S(2)}, u32[]{:S(2)}) collective-permute-start(f32[8,8,16,128]{3,2,1,0:T(8,128)S(1)} %get-tuple-element.6), channel_id=1, source_target_pairs={{0,16},{8,24},{16,0},{24,8},{1,17},{9,25},{17,1},{25,9},{2,18},{10... | collective-permute-start | bytes 1572872 | tf_op jit(solution)/shard_map/ppermute | solution.py:133
  87.5 1.7 %collective-permute-start.15 = (f32[8,8,16,128]{3,2,1,0:T(8,128)S(1)}, f32[8,8,16,128]{3,2,1,0:T(8,128)}, u32[]{:S(2)}, u32[]{:S(2)}) collective-permute-start(f32[8,8,16,128]{3,2,1,0:T(8,128)S(1)} %get-tuple-element.5), channel_id=1, source_target_pairs={{0,24},{8,0},{16,8},{24,16},{1,25},{9,1},{17,9},{25,17},{2,26},{10... | collective-permute-start | bytes 1572872 | tf_op jit(solution)/shard_map/ppermute | solution.py:133
  89.2 9.5 %collective-permute-done.13 = f32[8,8,16,128]{3,2,1,0:T(8,128)} collective-permute-done((f32[8,8,16,128]{3,2,1,0:T(8,128)}, f32[8,8,16,128]{3,2,1,0:T(8,128)}, u32[]{:S(2)}, u32[]{:S(2)}) %collective-permute-start.13) | collective-permute-done | bytes 524320 | tf_op jit(solution)/shard_map/ppermute | solution.py:133
  98.6 12.2 %collective-permute-done.14 = f32[8,8,16,128]{3,2,1,0:T(8,128)} collective-permute-done((f32[8,8,16,128]{3,2,1,0:T(8,128)S(1)}, f32[8,8,16,128]{3,2,1,0:T(8,128)}, u32[]{:S(2)}, u32[]{:S(2)}) %collective-permute-start.14) | collective-permute-done | bytes 524320 | tf_op jit(solution)/shard_map/ppermute | solution.py:133
  110.9 1.5 fusion.17
  112.4 2.1 %collective-permute-start.16 = (f32[8,16,128]{2,1,0:T(8,128)S(1)}, f32[8,16,128]{2,1,0:T(8,128)S(1)}, u32[]{:S(2)}, u32[]{:S(2)}) collective-permute-start(f32[8,16,128]{2,1,0:T(8,128)S(1)} %get-tuple-element.7), channel_id=1, source_target_pairs={{0,1},{1,2},{2,3},{3,4},{4,5},{5,6},{6,7},{7,0},{8,9},{9,10},{10,1... | collective-permute-start | bytes 196616 | tf_op jit(solution)/shard_map/ppermute | solution.py:138
  114.6 0.8 collective-permute-start.17
  115.3 1.8 %collective-permute-start.18 = (f32[8,16,128]{2,1,0:T(8,128)S(1)}, f32[8,16,128]{2,1,0:T(8,128)S(1)}, u32[]{:S(2)}, u32[]{:S(2)}) collective-permute-start(f32[8,16,128]{2,1,0:T(8,128)S(1)} %get-tuple-element.12), channel_id=1, source_target_pairs={{0,3},{1,4},{2,5},{3,6},{4,7},{5,0},{6,1},{7,2},{8,11},{9,12},{10,... | collective-permute-start | bytes 196616 | tf_op jit(solution)/shard_map/ppermute | solution.py:138
  117.1 3.5 %collective-permute-start.19 = (f32[8,16,128]{2,1,0:T(8,128)S(1)}, f32[8,16,128]{2,1,0:T(8,128)S(1)}, u32[]{:S(2)}, u32[]{:S(2)}) collective-permute-start(f32[8,16,128]{2,1,0:T(8,128)S(1)} %get-tuple-element.11), channel_id=1, source_target_pairs={{0,4},{1,5},{2,6},{3,7},{4,0},{5,1},{6,2},{7,3},{8,12},{9,13},{10,... | collective-permute-start | bytes 196616 | tf_op jit(solution)/shard_map/ppermute | solution.py:138
  120.6 2.6 %collective-permute-start.20 = (f32[8,16,128]{2,1,0:T(8,128)S(1)}, f32[8,16,128]{2,1,0:T(8,128)S(1)}, u32[]{:S(2)}, u32[]{:S(2)}) collective-permute-start(f32[8,16,128]{2,1,0:T(8,128)S(1)} %get-tuple-element.10), channel_id=1, source_target_pairs={{0,5},{1,6},{2,7},{3,0},{4,1},{5,2},{6,3},{7,4},{8,13},{9,14},{10,... | collective-permute-start | bytes 196616 | tf_op jit(solution)/shard_map/ppermute | solution.py:138
  123.2 1.4 collective-permute-start.21
  124.9 1.5 collective-permute-start.22
  126.4 4.9 %reduce-scatter.2.cloned.1.call-done = f32[32,16,128]{2,1,0:T(8,128)} async-done(((f32[256,16,128]{2,1,0:T(8,128)}), f32[32,16,128]{2,1,0:T(8,128)}) %reduce-scatter.2.cloned.1.call-update) | async-done | bytes 262160 | tf_op jit(solution)/shard_map/reduce_scatter | solution.py:124
  131.3 0.9 dynamic-slice_bitcast_fusion.12
  132.2 1.9 %collective-permute-start.23 = (f32[1,32,1024]{2,1,0:T(8,128)S(1)}, f32[1,32,1024]{2,1,0:T(8,128)S(1)}, u32[]{:S(2)}, u32[]{:S(2)}) collective-permute-start(f32[1,32,1024]{2,1,0:T(8,128)S(1)} %get-tuple-element.19), channel_id=1, source_target_pairs={{0,32},{32,64},{64,96},{96,128},{128,160},{160,192},{192,224},{1,3... | collective-permute-start | bytes 393224 | tf_op jit(solution)/shard_map/ppermute | solution.py:25
  134.2 3.6 %collective-permute-start.24 = (f32[1,32,1024]{2,1,0:T(8,128)S(1)}, f32[1,32,1024]{2,1,0:T(8,128)S(1)}, u32[]{:S(2)}, u32[]{:S(2)}) collective-permute-start(f32[1,32,1024]{2,1,0:T(8,128)S(1)} %get-tuple-element.19), channel_id=1, source_target_pairs={{32,0},{64,32},{96,64},{128,96},{160,128},{192,160},{224,192},{33,... | collective-permute-start | bytes 393224 | tf_op jit(solution)/shard_map/ppermute | solution.py:27
  137.8 2.0 %collective-permute-start.10 = (f32[8,16,128]{2,1,0:T(8,128)S(1)}, f32[8,16,128]{2,1,0:T(8,128)S(1)}, u32[]{:S(2)}, u32[]{:S(2)}) collective-permute-start(f32[8,16,128]{2,1,0:T(8,128)S(1)} %get-tuple-element.14), channel_id=1, source_target_pairs={{0,8},{8,16},{16,24},{24,0},{1,9},{9,17},{17,25},{25,1},{2,10},{10... | collective-permute-start | bytes 196616 | tf_op jit(solution)/shard_map/ppermute | solution.py:128
  139.8 3.1 %collective-permute-start.11 = (f32[8,16,128]{2,1,0:T(8,128)S(1)}, f32[8,16,128]{2,1,0:T(8,128)S(1)}, u32[]{:S(2)}, u32[]{:S(2)}) collective-permute-start(f32[8,16,128]{2,1,0:T(8,128)S(1)} %get-tuple-element.16), channel_id=1, source_target_pairs={{0,16},{8,24},{16,0},{24,8},{1,17},{9,25},{17,1},{25,9},{2,18},{10... | collective-permute-start | bytes 196616 | tf_op jit(solution)/shard_map/ppermute | solution.py:128
  142.9 0.8 collective-permute-start.12
  143.7 2.1 %collective-permute-done.11 = f32[8,16,128]{2,1,0:T(8,128)S(1)} collective-permute-done((f32[8,16,128]{2,1,0:T(8,128)S(1)}, f32[8,16,128]{2,1,0:T(8,128)S(1)}, u32[]{:S(2)}, u32[]{:S(2)}) %collective-permute-start.11) | collective-permute-done | bytes 65568 | tf_op jit(solution)/shard_map/ppermute | solution.py:128
  145.8 1.3 collective-permute-done.12
  147.1 0.9 fusion.29
  148.1 0.7 slice_bitcast_fusion
  (51 shorter events, 6.5 us)
Async XLA Ops:
  7.2 31.9 %copy-start = (s32[1,24,16]{1,2,0:T(8,128)S(1)}, s32[1,24,16]{1,2,0:T(8,128)}, u32[]{:S(2)}) copy-start(s32[1,24,16]{1,2,0:T(8,128)} %param.7) | copy-start | bytes 4612
  7.2 124.1 %reduce-scatter.2.cloned.1.call-start = ((), (), s32[]{:S(2)}) async-start(), calls=%async_computation.1 | async-start | bytes 2359296 | tf_op jit(solution)/shard_map/reduce_scatter | solution.py:124
  9.2 15.4 %collective-permute-start = (bf16[8,32,128]{2,1,0:T(8,128)(2,1)S(1)}, bf16[8,32,128]{2,1,0:T(8,128)(2,1)S(1)}, u32[]{:S(2)}, u32[]{:S(2)}) collective-permute-start(bf16[8,32,128]{2,1,0:T(8,128)(2,1)S(1)} %maximum_bitcast_fusion.3), channel_id=1, source_target_pairs={{0,1},{1,2},{2,3},{3,4},{4,5},{5,6},{6,7},{7,0},{8,9},{9,10},{10,1... | collective-permute-start | bytes 196616 | tf_op jit(solution)/shard_map/ppermute | solution.py:80
  11.1 16.8 %collective-permute-start.1 = (bf16[8,32,128]{2,1,0:T(8,128)(2,1)S(1)}, bf16[8,32,128]{2,1,0:T(8,128)(2,1)S(1)}, u32[]{:S(2)}, u32[]{:S(2)}) collective-permute-start(bf16[8,32,128]{2,1,0:T(8,128)(2,1)S(1)} %maximum_bitcast_fusion.3), channel_id=1, source_target_pairs={{0,2},{1,3},{2,4},{3,5},{4,6},{5,7},{6,0},{7,1},{8,10},{9,11},{10,... | collective-permute-start | bytes 196616 | tf_op jit(solution)/shard_map/ppermute | solution.py:80
  14.4 15.1 %collective-permute-start.2 = (bf16[8,32,128]{2,1,0:T(8,128)(2,1)S(1)}, bf16[8,32,128]{2,1,0:T(8,128)(2,1)S(1)}, u32[]{:S(2)}, u32[]{:S(2)}) collective-permute-start(bf16[8,32,128]{2,1,0:T(8,128)(2,1)S(1)} %maximum_bitcast_fusion.3), channel_id=1, source_target_pairs={{0,3},{1,4},{2,5},{3,6},{4,7},{5,0},{6,1},{7,2},{8,11},{9,12},{10,... | collective-permute-start | bytes 196616 | tf_op jit(solution)/shard_map/ppermute | solution.py:80
  18.5 11.8 %collective-permute-start.3 = (bf16[8,32,128]{2,1,0:T(8,128)(2,1)S(1)}, bf16[8,32,128]{2,1,0:T(8,128)(2,1)S(1)}, u32[]{:S(2)}, u32[]{:S(2)}) collective-permute-start(bf16[8,32,128]{2,1,0:T(8,128)(2,1)S(1)} %maximum_bitcast_fusion.3), channel_id=1, source_target_pairs={{0,4},{1,5},{2,6},{3,7},{4,0},{5,1},{6,2},{7,3},{8,12},{9,13},{10,... | collective-permute-start | bytes 196616 | tf_op jit(solution)/shard_map/ppermute | solution.py:80
  19.0 13.7 %collective-permute-start.4 = (bf16[8,32,128]{2,1,0:T(8,128)(2,1)S(1)}, bf16[8,32,128]{2,1,0:T(8,128)(2,1)S(1)}, u32[]{:S(2)}, u32[]{:S(2)}) collective-permute-start(bf16[8,32,128]{2,1,0:T(8,128)(2,1)S(1)} %maximum_bitcast_fusion.3), channel_id=1, source_target_pairs={{0,5},{1,6},{2,7},{3,0},{4,1},{5,2},{6,3},{7,4},{8,13},{9,14},{10,... | collective-permute-start | bytes 196616 | tf_op jit(solution)/shard_map/ppermute | solution.py:80
  24.6 8.7 %collective-permute-start.5 = (bf16[8,32,128]{2,1,0:T(8,128)(2,1)S(1)}, bf16[8,32,128]{2,1,0:T(8,128)(2,1)S(1)}, u32[]{:S(2)}, u32[]{:S(2)}) collective-permute-start(bf16[8,32,128]{2,1,0:T(8,128)(2,1)S(1)} %maximum_bitcast_fusion.3), channel_id=1, source_target_pairs={{0,6},{1,7},{2,0},{3,1},{4,2},{5,3},{6,4},{7,5},{8,14},{9,15},{10,... | collective-permute-start | bytes 196616 | tf_op jit(solution)/shard_map/ppermute | solution.py:80
  27.9 6.1 %collective-permute-start.6 = (bf16[8,32,128]{2,1,0:T(8,128)(2,1)S(1)}, bf16[8,32,128]{2,1,0:T(8,128)(2,1)S(1)}, u32[]{:S(2)}, u32[]{:S(2)}) collective-permute-start(bf16[8,32,128]{2,1,0:T(8,128)(2,1)S(1)} %maximum_bitcast_fusion.3), channel_id=1, source_target_pairs={{0,7},{1,0},{2,1},{3,2},{4,3},{5,4},{6,5},{7,6},{8,15},{9,8},{10,9... | collective-permute-start | bytes 196616 | tf_op jit(solution)/shard_map/ppermute | solution.py:80
  34.6 14.9 %collective-permute-start.7 = (bf16[64,32,128]{2,1,0:T(8,128)(2,1)S(1)}, bf16[64,32,128]{2,1,0:T(8,128)(2,1)S(1)}, u32[]{:S(2)}, u32[]{:S(2)}) collective-permute-start(bf16[64,32,128]{2,1,0:T(8,128)(2,1)S(1)} %get-tuple-element.23), channel_id=1, source_target_pairs={{0,8},{8,16},{16,24},{24,0},{1,9},{9,17},{17,25},{25,1},{2,10},{10... | collective-permute-start | bytes 1572872 | tf_op jit(solution)/shard_map/ppermute | solution.py:89
  36.2 25.3 %collective-permute-start.8 = (bf16[64,32,128]{2,1,0:T(8,128)(2,1)S(1)}, bf16[64,32,128]{2,1,0:T(8,128)(2,1)S(1)}, u32[]{:S(2)}, u32[]{:S(2)}) collective-permute-start(bf16[64,32,128]{2,1,0:T(8,128)(2,1)S(1)} %get-tuple-element.23), channel_id=1, source_target_pairs={{0,16},{8,24},{16,0},{24,8},{1,17},{9,25},{17,1},{25,9},{2,18},{10... | collective-permute-start | bytes 1572872 | tf_op jit(solution)/shard_map/ppermute | solution.py:89
  39.3 23.0 %collective-permute-start.9 = (bf16[64,32,128]{2,1,0:T(8,128)(2,1)S(1)}, bf16[64,32,128]{2,1,0:T(8,128)(2,1)S(1)}, u32[]{:S(2)}, u32[]{:S(2)}) collective-permute-start(bf16[64,32,128]{2,1,0:T(8,128)(2,1)S(1)} %get-tuple-element.23), channel_id=1, source_target_pairs={{0,24},{8,0},{16,8},{24,16},{1,25},{9,1},{17,9},{25,17},{2,26},{10... | collective-permute-start | bytes 1572872 | tf_op jit(solution)/shard_map/ppermute | solution.py:89
  66.0 7.1 %copy-start.2 = (s32[1,24,128]{2,1,0:T(8,128)S(1)}, s32[1,24,128]{2,1,0:T(8,128)}, u32[]{:S(2)}) copy-start(s32[1,24,128]{2,1,0:T(8,128)} %param.8) | copy-start | bytes 36868
  84.8 13.8 %collective-permute-start.13 = (f32[8,8,16,128]{3,2,1,0:T(8,128)}, f32[8,8,16,128]{3,2,1,0:T(8,128)}, u32[]{:S(2)}, u32[]{:S(2)}) collective-permute-start(f32[8,8,16,128]{3,2,1,0:T(8,128)} %get-tuple-element.4), channel_id=1, source_target_pairs={{0,8},{8,16},{16,24},{24,0},{1,9},{9,17},{17,25},{25,1},{2,10},{10... | collective-permute-start | bytes 1572872 | tf_op jit(solution)/shard_map/ppermute | solution.py:133
  85.3 25.6 %collective-permute-start.14 = (f32[8,8,16,128]{3,2,1,0:T(8,128)S(1)}, f32[8,8,16,128]{3,2,1,0:T(8,128)}, u32[]{:S(2)}, u32[]{:S(2)}) collective-permute-start(f32[8,8,16,128]{3,2,1,0:T(8,128)S(1)} %get-tuple-element.6), channel_id=1, source_target_pairs={{0,16},{8,24},{16,0},{24,8},{1,17},{9,25},{17,1},{25,9},{2,18},{10... | collective-permute-start | bytes 1572872 | tf_op jit(solution)/shard_map/ppermute | solution.py:133
  87.5 23.4 %collective-permute-start.15 = (f32[8,8,16,128]{3,2,1,0:T(8,128)S(1)}, f32[8,8,16,128]{3,2,1,0:T(8,128)}, u32[]{:S(2)}, u32[]{:S(2)}) collective-permute-start(f32[8,8,16,128]{3,2,1,0:T(8,128)S(1)} %get-tuple-element.5), channel_id=1, source_target_pairs={{0,24},{8,0},{16,8},{24,16},{1,25},{9,1},{17,9},{25,17},{2,26},{10... | collective-permute-start | bytes 1572872 | tf_op jit(solution)/shard_map/ppermute | solution.py:133
  89.2 58.9 %copy-start.1 = (f32[1024]{0:T(1024)S(1)}, f32[1024]{0:T(1024)}, u32[]{:S(2)}) copy-start(f32[1024]{0:T(1024)} %param.11) | copy-start | bytes 12292
  112.4 10.8 %collective-permute-start.16 = (f32[8,16,128]{2,1,0:T(8,128)S(1)}, f32[8,16,128]{2,1,0:T(8,128)S(1)}, u32[]{:S(2)}, u32[]{:S(2)}) collective-permute-start(f32[8,16,128]{2,1,0:T(8,128)S(1)} %get-tuple-element.7), channel_id=1, source_target_pairs={{0,1},{1,2},{2,3},{3,4},{4,5},{5,6},{6,7},{7,0},{8,9},{9,10},{10,1... | collective-permute-start | bytes 196616 | tf_op jit(solution)/shard_map/ppermute | solution.py:138
  114.6 10.3 %collective-permute-start.17 = (f32[8,16,128]{2,1,0:T(8,128)S(1)}, f32[8,16,128]{2,1,0:T(8,128)S(1)}, u32[]{:S(2)}, u32[]{:S(2)}) collective-permute-start(f32[8,16,128]{2,1,0:T(8,128)S(1)} %get-tuple-element.13), channel_id=1, source_target_pairs={{0,2},{1,3},{2,4},{3,5},{4,6},{5,7},{6,0},{7,1},{8,10},{9,11},{10,... | collective-permute-start | bytes 196616 | tf_op jit(solution)/shard_map/ppermute | solution.py:138
  115.3 16.9 %collective-permute-start.18 = (f32[8,16,128]{2,1,0:T(8,128)S(1)}, f32[8,16,128]{2,1,0:T(8,128)S(1)}, u32[]{:S(2)}, u32[]{:S(2)}) collective-permute-start(f32[8,16,128]{2,1,0:T(8,128)S(1)} %get-tuple-element.12), channel_id=1, source_target_pairs={{0,3},{1,4},{2,5},{3,6},{4,7},{5,0},{6,1},{7,2},{8,11},{9,12},{10,... | collective-permute-start | bytes 196616 | tf_op jit(solution)/shard_map/ppermute | solution.py:138
  117.1 17.1 %collective-permute-start.19 = (f32[8,16,128]{2,1,0:T(8,128)S(1)}, f32[8,16,128]{2,1,0:T(8,128)S(1)}, u32[]{:S(2)}, u32[]{:S(2)}) collective-permute-start(f32[8,16,128]{2,1,0:T(8,128)S(1)} %get-tuple-element.11), channel_id=1, source_target_pairs={{0,4},{1,5},{2,6},{3,7},{4,0},{5,1},{6,2},{7,3},{8,12},{9,13},{10,... | collective-permute-start | bytes 196616 | tf_op jit(solution)/shard_map/ppermute | solution.py:138
  120.6 17.2 %collective-permute-start.20 = (f32[8,16,128]{2,1,0:T(8,128)S(1)}, f32[8,16,128]{2,1,0:T(8,128)S(1)}, u32[]{:S(2)}, u32[]{:S(2)}) collective-permute-start(f32[8,16,128]{2,1,0:T(8,128)S(1)} %get-tuple-element.10), channel_id=1, source_target_pairs={{0,5},{1,6},{2,7},{3,0},{4,1},{5,2},{6,3},{7,4},{8,13},{9,14},{10,... | collective-permute-start | bytes 196616 | tf_op jit(solution)/shard_map/ppermute | solution.py:138
  123.2 16.6 %collective-permute-start.21 = (f32[8,16,128]{2,1,0:T(8,128)S(1)}, f32[8,16,128]{2,1,0:T(8,128)S(1)}, u32[]{:S(2)}, u32[]{:S(2)}) collective-permute-start(f32[8,16,128]{2,1,0:T(8,128)S(1)} %get-tuple-element.9), channel_id=1, source_target_pairs={{0,6},{1,7},{2,0},{3,1},{4,2},{5,3},{6,4},{7,5},{8,14},{9,15},{10,... | collective-permute-start | bytes 196616 | tf_op jit(solution)/shard_map/ppermute | solution.py:138
  124.9 18.0 %collective-permute-start.22 = (f32[8,16,128]{2,1,0:T(8,128)S(1)}, f32[8,16,128]{2,1,0:T(8,128)S(1)}, u32[]{:S(2)}, u32[]{:S(2)}) collective-permute-start(f32[8,16,128]{2,1,0:T(8,128)S(1)} %get-tuple-element.8), channel_id=1, source_target_pairs={{0,7},{1,0},{2,1},{3,2},{4,3},{5,4},{6,5},{7,6},{8,15},{9,8},{10,9... | collective-permute-start | bytes 196616 | tf_op jit(solution)/shard_map/ppermute | solution.py:138
  132.2 15.8 %collective-permute-start.23 = (f32[1,32,1024]{2,1,0:T(8,128)S(1)}, f32[1,32,1024]{2,1,0:T(8,128)S(1)}, u32[]{:S(2)}, u32[]{:S(2)}) collective-permute-start(f32[1,32,1024]{2,1,0:T(8,128)S(1)} %get-tuple-element.19), channel_id=1, source_target_pairs={{0,32},{32,64},{64,96},{96,128},{128,160},{160,192},{192,224},{1,3... | collective-permute-start | bytes 393224 | tf_op jit(solution)/shard_map/ppermute | solution.py:25
  134.2 13.8 %collective-permute-start.24 = (f32[1,32,1024]{2,1,0:T(8,128)S(1)}, f32[1,32,1024]{2,1,0:T(8,128)S(1)}, u32[]{:S(2)}, u32[]{:S(2)}) collective-permute-start(f32[1,32,1024]{2,1,0:T(8,128)S(1)} %get-tuple-element.19), channel_id=1, source_target_pairs={{32,0},{64,32},{96,64},{128,96},{160,128},{192,160},{224,192},{33,... | collective-permute-start | bytes 393224 | tf_op jit(solution)/shard_map/ppermute | solution.py:27
  137.8 5.9 %collective-permute-start.10 = (f32[8,16,128]{2,1,0:T(8,128)S(1)}, f32[8,16,128]{2,1,0:T(8,128)S(1)}, u32[]{:S(2)}, u32[]{:S(2)}) collective-permute-start(f32[8,16,128]{2,1,0:T(8,128)S(1)} %get-tuple-element.14), channel_id=1, source_target_pairs={{0,8},{8,16},{16,24},{24,0},{1,9},{9,17},{17,25},{25,1},{2,10},{10... | collective-permute-start | bytes 196616 | tf_op jit(solution)/shard_map/ppermute | solution.py:128
  139.8 6.0 %collective-permute-start.11 = (f32[8,16,128]{2,1,0:T(8,128)S(1)}, f32[8,16,128]{2,1,0:T(8,128)S(1)}, u32[]{:S(2)}, u32[]{:S(2)}) collective-permute-start(f32[8,16,128]{2,1,0:T(8,128)S(1)} %get-tuple-element.16), channel_id=1, source_target_pairs={{0,16},{8,24},{16,0},{24,8},{1,17},{9,25},{17,1},{25,9},{2,18},{10... | collective-permute-start | bytes 196616 | tf_op jit(solution)/shard_map/ppermute | solution.py:128
  142.9 4.3 %collective-permute-start.12 = (f32[8,16,128]{2,1,0:T(8,128)S(1)}, f32[8,16,128]{2,1,0:T(8,128)S(1)}, u32[]{:S(2)}, u32[]{:S(2)}) collective-permute-start(f32[8,16,128]{2,1,0:T(8,128)S(1)} %get-tuple-element.15), channel_id=1, source_target_pairs={{0,24},{8,0},{16,8},{24,16},{1,25},{9,1},{17,9},{25,17},{2,26},{10... | collective-permute-start | bytes 196616 | tf_op jit(solution)/shard_map/ppermute | solution.py:128
Sparse Core Ops, SparseCore 0:
  83.9 47.3 reduce-scatter.1

commit v8 on v7

--- a/solution.py
+++ b/solution.py
@@ -66,6 +66,60 @@
             dimension_semantics=("arbitrary",), vmem_limit_bytes=40 * 1024 * 1024
         ),
     )(dest, contrib)
+
+
+def fused_kernel(dest_ref, feat_ref, sel_ref, lab_ref, out_ref):
+    t = pl.program_id(0)
+    slots = feat_ref.shape[1]
+    arms = sel_ref.shape[2] // 2
+
+    @pl.when(t == 0)
+    def _():
+        out_ref[...] = jnp.zeros_like(out_ref)
+
+    acc = None
+    for a in range(slots):
+        part = lax.dot_general(
+            sel_ref[0, a], feat_ref[0, a], (((1,), (1,)), ((), ())),
+            preferred_element_type=jnp.float32,
+        )
+        acc = part if acc is None else acc + part
+    logits = acc[:arms]
+    lin_dir = acc[arms:]
+    expo = jnp.exp(logits)
+    probs = expo / jnp.sum(expo, axis=0, keepdims=True)
+    arm_ids = lax.broadcasted_iota(jnp.int32, logits.shape, 0)
+    onehot = (lab_ref[0] == arm_ids).astype(jnp.float32)
+    resid = probs - onehot
+    hrow = probs * lin_dir - probs * jnp.sum(probs * lin_dir, axis=0, keepdims=True)
+    both_low = jnp.concatenate([resid, hrow], axis=0).astype(jnp.bfloat16)
+    for a in range(slots):
+        q = dest_ref[t * slots + a]
+        out_ref[q] = out_ref[q] + jnp.dot(
+            both_low, feat_ref[0, a], preferred_element_type=jnp.float32
+        )
+
+
+def fused_rows(dest, feats, selected, labels, nblk):
+    tiles, slots, rows, width = feats.shape
+    pair = selected.shape[2]
+    return pl.pallas_call(
+        fused_kernel,
+        grid_spec=pltpu.PrefetchScalarGridSpec(
+            num_scalar_prefetch=1,
+            grid=(tiles,),
+            in_specs=[
+                pl.BlockSpec((1, slots, rows, width), lambda t, d: (t, 0, 0, 0)),
+                pl.BlockSpec((1, slots, pair, width), lambda t, d: (t, 0, 0, 0)),
+                pl.BlockSpec((1, 1, rows), lambda t, d: (t, 0, 0)),
+            ],
+            out_specs=pl.BlockSpec((nblk, pair, width), lambda t, d: (0, 0, 0)),
+        ),
+        out_shape=jax.ShapeDtypeStruct((nblk, pair, width), jnp.float32),
+        compiler_params=pltpu.CompilerParams(
+            dimension_semantics=("arbitrary",), vmem_limit_bytes=40 * 1024 * 1024
+        ),
+    )(dest, feats, selected, labels)
 
 
 def on_device(features, blocks, labels, coef, direction, prior):
@@ -101,24 +155,12 @@
     ) * local_blk
     selected = coef_table[rotated + blks % local_blk]
     feats = features[0]
-    logits_dir = jnp.einsum("tari,taki->tkr", feats, selected, preferred_element_type=jnp.float32)
-    logits = logits_dir[:, :arms]
-    lin_dir = logits_dir[:, arms:]
-    expo = jnp.exp(logits)
-    probs = expo / jnp.sum(expo, axis=1, keepdims=True)
-    onehot = (labels[0][:, None, :] == jnp.arange(arms, dtype=jnp.int32)[None, :, None]).astype(
-        jnp.float32
-    )
-    resid = probs - onehot
-    hrow = probs * lin_dir - probs * jnp.sum(probs * lin_dir, axis=1, keepdims=True)
-    both_low = jnp.concatenate([resid, hrow], axis=1).astype(jnp.bfloat16)
-    contrib = jnp.einsum("tari,tkr->taki", feats, both_low, preferred_element_type=jnp.float32)
     outer = lax.axis_size("row_0")
     inner = lax.axis_size("row_1")
     per = nblk // (outer * inner)
     flat = blks.reshape(-1)
     dest = ((flat // per) % inner) * (outer * per) + (flat // (inner * per)) * per + flat % per
-    partial_terms = scatter_rows(dest, contrib, nblk)
+    partial_terms = fused_rows(dest, feats, selected, labels[0][:, None, :], nblk)
     grad_part = partial_terms[:, :arms]
     hv_part = partial_terms[:, arms:].reshape(count, around, local_blk, arms, width)
     owned = lax.psum_scatter(grad_part, "row_1", scatter_dimension=0, tiled=True)

time: 156 us -> 165 us (1.058)
  Pallas kernels: 2.54 us -> 25.6 us
  matrix products: 12.6 us -> 0 us
    pallas_call x1, Pallas kernels: 2.54 us -> 25.6 us  [fused_rows(): pl.pallas_call(fused_kernel, grid_spec=pltpu.PrefetchScalarGridSpec(num_s...]
    dot_general x2 -> x0, matrix products: 12.6 us -> none  [the longest x1 7.04 us: on_device(): jnp.einsum('tari,taki->tkr', feats, selected, preferred_element_type=jnp....]
where the time goes in v8:
time: 165 us; the launch traced here: 164 us
  starting transfers between devices  54.1 us (33%)
  waiting for transfers between devices  50.9 us (31%)
  Pallas kernels  25.6 us (16%)
  local copies, waits for them, and re-layouts  14.5 us (9%)
  between operations  14.3 us (9%)
  other arithmetic  5 us (3%)
    pallas_call x1, Pallas kernels, fused_rows(): pl.pallas_call(fused_kernel, grid_spec=pltpu.PrefetchScalarGridSpec(num_s...  25.6 us
    ppermute x3, waiting for transfers between devices, on_device(): lax.ppermute(hv_part[:, (there + s) % around], 'row_0', [(i, (i + s) % ar...  21.7 us
    ppermute x3, waiting for transfers between devices, on_device(): lax.ppermute(stage, 'row_0', [(i, (i + s) % around) for i in range(around)])  19.8 us
    ppermute x7, starting transfers between devices, on_device(): lax.ppermute(by_block, 'row_1', [(i, (i + s) % count) for i in range(coun...  18.5 us
    ppermute x7, starting transfers between devices, on_device(): lax.ppermute(across[(here + s) % count], 'row_1', [(i, (i + s) % count) f...  13.5 us
    ppermute x3, starting transfers between devices, on_device(): lax.ppermute(chunks[(there + s) % around], 'row_0', [(i, (i + s) % around...  6.27 us
    ppermute x3, starting transfers between devices, on_device(): lax.ppermute(stage, 'row_0', [(i, (i + s) % around) for i in range(around)])  5.84 us
    unnamed x17, local copies, waits for them, and re-layouts  5.63 us
  transfers between devices with their start and end apart: 26, of which 9 were waited for; matrix products, arithmetic and copies ran while one was open for 7% of the time, Pallas kernels for 0%

profile of v8, /device:TPU:2, one launch (start us, length us, event | category | flops | bytes accessed | tf_op | source)
XLA Modules:
  0.0 164.3 jit_solution(4928257575069137033)
XLA Ops:
  7.2 0.9 constant_dynamic-update-slice_fusion.20
  8.1 0.9 constant_dynamic-update-slice_fusion.19
  9.2 2.0 %collective-permute-start = (bf16[8,32,128]{2,1,0:T(8,128)(2,1)S(1)}, bf16[8,32,128]{2,1,0:T(8,128)(2,1)S(1)}, u32[]{:S(2)}, u32[]{:S(2)}) collective-permute-start(bf16[8,32,128]{2,1,0:T(8,128)(2,1)S(1)} %maximum_bitcast_fusion.1), channel_id=1, source_target_pairs={{0,1},{1,2},{2,3},{3,4},{4,5},{5,6},{6,7},{7,0},{8,9},{9,10},{10,1... | collective-permute-start | bytes 196616 | tf_op jit(solution)/shard_map/ppermute | solution.py:134
  11.1 3.3 %collective-permute-start.1 = (bf16[8,32,128]{2,1,0:T(8,128)(2,1)S(1)}, bf16[8,32,128]{2,1,0:T(8,128)(2,1)S(1)}, u32[]{:S(2)}, u32[]{:S(2)}) collective-permute-start(bf16[8,32,128]{2,1,0:T(8,128)(2,1)S(1)} %maximum_bitcast_fusion.1), channel_id=1, source_target_pairs={{0,2},{1,3},{2,4},{3,5},{4,6},{5,7},{6,0},{7,1},{8,10},{9,11},{10,... | collective-permute-start | bytes 196616 | tf_op jit(solution)/shard_map/ppermute | solution.py:134
  14.4 4.0 %collective-permute-start.2 = (bf16[8,32,128]{2,1,0:T(8,128)(2,1)S(1)}, bf16[8,32,128]{2,1,0:T(8,128)(2,1)S(1)}, u32[]{:S(2)}, u32[]{:S(2)}) collective-permute-start(bf16[8,32,128]{2,1,0:T(8,128)(2,1)S(1)} %maximum_bitcast_fusion.1), channel_id=1, source_target_pairs={{0,3},{1,4},{2,5},{3,6},{4,7},{5,0},{6,1},{7,2},{8,11},{9,12},{10,... | collective-permute-start | bytes 196616 | tf_op jit(solution)/shard_map/ppermute | solution.py:134
  19.0 4.9 %collective-permute-start.4 = (bf16[8,32,128]{2,1,0:T(8,128)(2,1)S(1)}, bf16[8,32,128]{2,1,0:T(8,128)(2,1)S(1)}, u32[]{:S(2)}, u32[]{:S(2)}) collective-permute-start(bf16[8,32,128]{2,1,0:T(8,128)(2,1)S(1)} %maximum_bitcast_fusion.1), channel_id=1, source_target_pairs={{0,5},{1,6},{2,7},{3,0},{4,1},{5,2},{6,3},{7,4},{8,13},{9,14},{10,... | collective-permute-start | bytes 196616 | tf_op jit(solution)/shard_map/ppermute | solution.py:134
  24.6 2.7 %collective-permute-start.5 = (bf16[8,32,128]{2,1,0:T(8,128)(2,1)S(1)}, bf16[8,32,128]{2,1,0:T(8,128)(2,1)S(1)}, u32[]{:S(2)}, u32[]{:S(2)}) collective-permute-start(bf16[8,32,128]{2,1,0:T(8,128)(2,1)S(1)} %maximum_bitcast_fusion.1), channel_id=1, source_target_pairs={{0,6},{1,7},{2,0},{3,1},{4,2},{5,3},{6,4},{7,5},{8,14},{9,15},{10,... | collective-permute-start | bytes 196616 | tf_op jit(solution)/shard_map/ppermute | solution.py:134
  27.9 1.0 collective-permute-start.6
  28.9 0.6 constant_dynamic-update-slice_fusion.5
  29.5 0.6 constant_dynamic-update-slice_fusion.4
  30.2 0.7 constant_dynamic-update-slice_fusion.3
  30.8 1.8 %collective-permute-done.4 = bf16[8,32,128]{2,1,0:T(8,128)(2,1)S(1)} collective-permute-done((bf16[8,32,128]{2,1,0:T(8,128)(2,1)S(1)}, bf16[8,32,128]{2,1,0:T(8,128)(2,1)S(1)}, u32[]{:S(2)}, u32[]{:S(2)}) %collective-permute-start.4) | collective-permute-done | bytes 65568 | tf_op jit(solution)/shard_map/ppermute | solution.py:134
  32.7 0.6 constant_dynamic-update-slice_fusion.2
  34.0 0.6 constant_dynamic-update-slice_fusion
  34.6 1.6 collective-permute-start.7
  36.2 2.9 %collective-permute-start.8 = (bf16[64,32,128]{2,1,0:T(8,128)(2,1)S(1)}, bf16[64,32,128]{2,1,0:T(8,128)(2,1)S(1)}, u32[]{:S(2)}, u32[]{:S(2)}) collective-permute-start(bf16[64,32,128]{2,1,0:T(8,128)(2,1)S(1)} %get-tuple-element.23), channel_id=1, source_target_pairs={{0,16},{8,24},{16,0},{24,8},{1,17},{9,25},{17,1},{25,9},{2,18},{10... | collective-permute-start | bytes 1572872 | tf_op jit(solution)/shard_map/ppermute | solution.py:143
  39.3 1.4 collective-permute-start.9
  40.8 8.7 %collective-permute-done.7 = bf16[64,32,128]{2,1,0:T(8,128)(2,1)S(1)} collective-permute-done((bf16[64,32,128]{2,1,0:T(8,128)(2,1)S(1)}, bf16[64,32,128]{2,1,0:T(8,128)(2,1)S(1)}, u32[]{:S(2)}, u32[]{:S(2)}) %collective-permute-start.7) | collective-permute-done | bytes 524320 | tf_op jit(solution)/shard_map/ppermute | solution.py:143
  49.5 0.9 constant_dynamic-update-slice_fusion.10
  50.3 11.1 %collective-permute-done.8 = bf16[64,32,128]{2,1,0:T(8,128)(2,1)S(1)} collective-permute-done((bf16[64,32,128]{2,1,0:T(8,128)(2,1)S(1)}, bf16[64,32,128]{2,1,0:T(8,128)(2,1)S(1)}, u32[]{:S(2)}, u32[]{:S(2)}) %collective-permute-start.8) | collective-permute-done | bytes 524320 | tf_op jit(solution)/shard_map/ppermute | solution.py:143
  61.5 0.8 constant_dynamic-update-slice_fusion.9
  62.3 0.8 constant_dynamic-update-slice_fusion.8
  63.1 2.9 %gather_fusion = bf16[384,32,128]{2,1,0:T(8,128)(2,1)S(1)} fusion(bf16[256,32,128]{2,1,0:T(8,128)(2,1)} %constant_dynamic-update-slice_fusion.8, s32[1024]{0:T(1024)S(1)} %pad_clamp_fusion), kind=kCustom, calls=%fused_computation | custom fusion | bytes 6292992 | tf_op jit(solution)/shard_map/gather | solution.py:156
  66.0 25.6 %shard_map.77 = f32[256,32,128]{2,1,0:T(8,128)S(1)} custom-call(s32[384]{0:T(512)S(1)} %fusion.25.dest_ref, bf16[24,16,128,128]{3,2,1,0:T(8,128)(2,1)} %bitcast.107, bf16[24,16,32,128]{3,2,1,0:T(8,128)(2,1)S(1)} %bitcast.105, s32[24,1,128]{2,1,0:T(1,128)S(1)} %bitcast.106), custom_call_target="tpu_custom_call" | custom-call | tf_op jit(solution)/shard_map/pallas_call | solution.py:106
  91.6 1.7 %fusion.29 = (f32[256,16,128]{2,1,0:T(8,128)}, f32[256,16,128]{2,1,0:T(8,128)S(1)}) fusion(f32[256,32,128]{2,1,0:T(8,128)S(1)} %shard_map.77), kind=kLoop, calls=%fused_computation.108 | loop fusion | bytes 8388608 | tf_op jit(solution)/shard_map/slice | solution.py:164
  93.3 1.0 dynamic-slice_bitcast_fusion.2
  94.8 2.2 %collective-permute-start.14 = (f32[8,8,16,128]{3,2,1,0:T(8,128)S(1)}, f32[8,8,16,128]{3,2,1,0:T(8,128)}, u32[]{:S(2)}, u32[]{:S(2)}) collective-permute-start(f32[8,8,16,128]{3,2,1,0:T(8,128)S(1)} %get-tuple-element.6), channel_id=1, source_target_pairs={{0,16},{8,24},{16,0},{24,8},{1,17},{9,25},{17,1},{25,9},{2,18},{10... | collective-permute-start | bytes 1572872 | tf_op jit(solution)/shard_map/ppermute | solution.py:175
  97.0 1.7 %collective-permute-start.15 = (f32[8,8,16,128]{3,2,1,0:T(8,128)S(1)}, f32[8,8,16,128]{3,2,1,0:T(8,128)}, u32[]{:S(2)}, u32[]{:S(2)}) collective-permute-start(f32[8,8,16,128]{3,2,1,0:T(8,128)S(1)} %get-tuple-element.5), channel_id=1, source_target_pairs={{0,24},{8,0},{16,8},{24,16},{1,25},{9,1},{17,9},{25,17},{2,26},{10... | collective-permute-start | bytes 1572872 | tf_op jit(solution)/shard_map/ppermute | solution.py:175
  98.7 9.5 %collective-permute-done.13 = f32[8,8,16,128]{3,2,1,0:T(8,128)} collective-permute-done((f32[8,8,16,128]{3,2,1,0:T(8,128)}, f32[8,8,16,128]{3,2,1,0:T(8,128)}, u32[]{:S(2)}, u32[]{:S(2)}) %collective-permute-start.13) | collective-permute-done | bytes 524320 | tf_op jit(solution)/shard_map/ppermute | solution.py:175
  108.1 12.2 %collective-permute-done.14 = f32[8,8,16,128]{3,2,1,0:T(8,128)} collective-permute-done((f32[8,8,16,128]{3,2,1,0:T(8,128)S(1)}, f32[8,8,16,128]{3,2,1,0:T(8,128)}, u32[]{:S(2)}, u32[]{:S(2)}) %collective-permute-start.14) | collective-permute-done | bytes 524320 | tf_op jit(solution)/shard_map/ppermute | solution.py:175
  120.4 1.5 fusion.1
  121.9 2.1 %collective-permute-start.16 = (f32[8,16,128]{2,1,0:T(8,128)S(1)}, f32[8,16,128]{2,1,0:T(8,128)S(1)}, u32[]{:S(2)}, u32[]{:S(2)}) collective-permute-start(f32[8,16,128]{2,1,0:T(8,128)S(1)} %get-tuple-element.7), channel_id=1, source_target_pairs={{0,1},{1,2},{2,3},{3,4},{4,5},{5,6},{6,7},{7,0},{8,9},{9,10},{10,1... | collective-permute-start | bytes 196616 | tf_op jit(solution)/shard_map/ppermute | solution.py:180
  124.1 0.8 collective-permute-start.17
  124.8 1.8 %collective-permute-start.18 = (f32[8,16,128]{2,1,0:T(8,128)S(1)}, f32[8,16,128]{2,1,0:T(8,128)S(1)}, u32[]{:S(2)}, u32[]{:S(2)}) collective-permute-start(f32[8,16,128]{2,1,0:T(8,128)S(1)} %get-tuple-element.12), channel_id=1, source_target_pairs={{0,3},{1,4},{2,5},{3,6},{4,7},{5,0},{6,1},{7,2},{8,11},{9,12},{10,... | collective-permute-start | bytes 196616 | tf_op jit(solution)/shard_map/ppermute | solution.py:180
  126.6 3.5 %collective-permute-start.19 = (f32[8,16,128]{2,1,0:T(8,128)S(1)}, f32[8,16,128]{2,1,0:T(8,128)S(1)}, u32[]{:S(2)}, u32[]{:S(2)}) collective-permute-start(f32[8,16,128]{2,1,0:T(8,128)S(1)} %get-tuple-element.11), channel_id=1, source_target_pairs={{0,4},{1,5},{2,6},{3,7},{4,0},{5,1},{6,2},{7,3},{8,12},{9,13},{10,... | collective-permute-start | bytes 196616 | tf_op jit(solution)/shard_map/ppermute | solution.py:180
  130.1 2.6 %collective-permute-start.20 = (f32[8,16,128]{2,1,0:T(8,128)S(1)}, f32[8,16,128]{2,1,0:T(8,128)S(1)}, u32[]{:S(2)}, u32[]{:S(2)}) collective-permute-start(f32[8,16,128]{2,1,0:T(8,128)S(1)} %get-tuple-element.10), channel_id=1, source_target_pairs={{0,5},{1,6},{2,7},{3,0},{4,1},{5,2},{6,3},{7,4},{8,13},{9,14},{10,... | collective-permute-start | bytes 196616 | tf_op jit(solution)/shard_map/ppermute | solution.py:180
  132.7 1.4 collective-permute-start.21
  134.5 1.3 collective-permute-start.22
  135.9 4.5 %reduce-scatter.2.cloned.1.call-done = f32[32,16,128]{2,1,0:T(8,128)} async-done(((f32[256,16,128]{2,1,0:T(8,128)}), f32[32,16,128]{2,1,0:T(8,128)}) %reduce-scatter.2.cloned.1.call-update) | async-done | bytes 262160 | tf_op jit(solution)/shard_map/reduce_scatter | solution.py:166
  140.4 0.9 dynamic-slice_bitcast_fusion.12
  141.3 1.9 %collective-permute-start.23 = (f32[1,32,1024]{2,1,0:T(8,128)S(1)}, f32[1,32,1024]{2,1,0:T(8,128)S(1)}, u32[]{:S(2)}, u32[]{:S(2)}) collective-permute-start(f32[1,32,1024]{2,1,0:T(8,128)S(1)} %get-tuple-element.19), channel_id=1, source_target_pairs={{0,32},{32,64},{64,96},{96,128},{128,160},{160,192},{192,224},{1,3... | collective-permute-start | bytes 393224 | tf_op jit(solution)/shard_map/ppermute | solution.py:25
  143.2 3.6 %collective-permute-start.24 = (f32[1,32,1024]{2,1,0:T(8,128)S(1)}, f32[1,32,1024]{2,1,0:T(8,128)S(1)}, u32[]{:S(2)}, u32[]{:S(2)}) collective-permute-start(f32[1,32,1024]{2,1,0:T(8,128)S(1)} %get-tuple-element.19), channel_id=1, source_target_pairs={{32,0},{64,32},{96,64},{128,96},{160,128},{192,160},{224,192},{33,... | collective-permute-start | bytes 393224 | tf_op jit(solution)/shard_map/ppermute | solution.py:27
  146.9 2.5 %collective-permute-start.10 = (f32[8,16,128]{2,1,0:T(8,128)S(1)}, f32[8,16,128]{2,1,0:T(8,128)S(1)}, u32[]{:S(2)}, u32[]{:S(2)}) collective-permute-start(f32[8,16,128]{2,1,0:T(8,128)S(1)} %get-tuple-element.14), channel_id=1, source_target_pairs={{0,8},{8,16},{16,24},{24,0},{1,9},{9,17},{17,25},{25,1},{2,10},{10... | collective-permute-start | bytes 196616 | tf_op jit(solution)/shard_map/ppermute | solution.py:170
  149.4 2.2 %collective-permute-start.11 = (f32[8,16,128]{2,1,0:T(8,128)S(1)}, f32[8,16,128]{2,1,0:T(8,128)S(1)}, u32[]{:S(2)}, u32[]{:S(2)}) collective-permute-start(f32[8,16,128]{2,1,0:T(8,128)S(1)} %get-tuple-element.16), channel_id=1, source_target_pairs={{0,16},{8,24},{16,0},{24,8},{1,17},{9,25},{17,1},{25,9},{2,18},{10... | collective-permute-start | bytes 196616 | tf_op jit(solution)/shard_map/ppermute | solution.py:170
  151.6 1.6 collective-permute-start.12
  153.2 2.0 %collective-permute-done.11 = f32[8,16,128]{2,1,0:T(8,128)S(1)} collective-permute-done((f32[8,16,128]{2,1,0:T(8,128)S(1)}, f32[8,16,128]{2,1,0:T(8,128)S(1)}, u32[]{:S(2)}, u32[]{:S(2)}) %collective-permute-start.11) | collective-permute-done | bytes 65568 | tf_op jit(solution)/shard_map/ppermute | solution.py:170
  155.8 0.9 fusion.9
  156.8 0.7 slice_bitcast_fusion
  (47 shorter events, 4.6 us)
Async XLA Ops:
  7.2 31.9 %copy-start.1 = (s32[1,24,16]{1,2,0:T(8,128)S(1)}, s32[1,24,16]{1,2,0:T(8,128)}, u32[]{:S(2)}) copy-start(s32[1,24,16]{1,2,0:T(8,128)} %param.7) | copy-start | bytes 4612
  7.2 133.2 %reduce-scatter.2.cloned.1.call-start = ((), (), s32[]{:S(2)}) async-start(), calls=%async_computation.1 | async-start | bytes 2359296 | tf_op jit(solution)/shard_map/reduce_scatter | solution.py:166
  9.2 15.4 %collective-permute-start = (bf16[8,32,128]{2,1,0:T(8,128)(2,1)S(1)}, bf16[8,32,128]{2,1,0:T(8,128)(2,1)S(1)}, u32[]{:S(2)}, u32[]{:S(2)}) collective-permute-start(bf16[8,32,128]{2,1,0:T(8,128)(2,1)S(1)} %maximum_bitcast_fusion.1), channel_id=1, source_target_pairs={{0,1},{1,2},{2,3},{3,4},{4,5},{5,6},{6,7},{7,0},{8,9},{9,10},{10,1... | collective-permute-start | bytes 196616 | tf_op jit(solution)/shard_map/ppermute | solution.py:134
  11.1 16.7 %collective-permute-start.1 = (bf16[8,32,128]{2,1,0:T(8,128)(2,1)S(1)}, bf16[8,32,128]{2,1,0:T(8,128)(2,1)S(1)}, u32[]{:S(2)}, u32[]{:S(2)}) collective-permute-start(bf16[8,32,128]{2,1,0:T(8,128)(2,1)S(1)} %maximum_bitcast_fusion.1), channel_id=1, source_target_pairs={{0,2},{1,3},{2,4},{3,5},{4,6},{5,7},{6,0},{7,1},{8,10},{9,11},{10,... | collective-permute-start | bytes 196616 | tf_op jit(solution)/shard_map/ppermute | solution.py:134
  14.4 15.1 %collective-permute-start.2 = (bf16[8,32,128]{2,1,0:T(8,128)(2,1)S(1)}, bf16[8,32,128]{2,1,0:T(8,128)(2,1)S(1)}, u32[]{:S(2)}, u32[]{:S(2)}) collective-permute-start(bf16[8,32,128]{2,1,0:T(8,128)(2,1)S(1)} %maximum_bitcast_fusion.1), channel_id=1, source_target_pairs={{0,3},{1,4},{2,5},{3,6},{4,7},{5,0},{6,1},{7,2},{8,11},{9,12},{10,... | collective-permute-start | bytes 196616 | tf_op jit(solution)/shard_map/ppermute | solution.py:134
  18.5 11.7 %collective-permute-start.3 = (bf16[8,32,128]{2,1,0:T(8,128)(2,1)S(1)}, bf16[8,32,128]{2,1,0:T(8,128)(2,1)S(1)}, u32[]{:S(2)}, u32[]{:S(2)}) collective-permute-start(bf16[8,32,128]{2,1,0:T(8,128)(2,1)S(1)} %maximum_bitcast_fusion.1), channel_id=1, source_target_pairs={{0,4},{1,5},{2,6},{3,7},{4,0},{5,1},{6,2},{7,3},{8,12},{9,13},{10,... | collective-permute-start | bytes 196616 | tf_op jit(solution)/shard_map/ppermute | solution.py:134
  19.0 13.7 %collective-permute-start.4 = (bf16[8,32,128]{2,1,0:T(8,128)(2,1)S(1)}, bf16[8,32,128]{2,1,0:T(8,128)(2,1)S(1)}, u32[]{:S(2)}, u32[]{:S(2)}) collective-permute-start(bf16[8,32,128]{2,1,0:T(8,128)(2,1)S(1)} %maximum_bitcast_fusion.1), channel_id=1, source_target_pairs={{0,5},{1,6},{2,7},{3,0},{4,1},{5,2},{6,3},{7,4},{8,13},{9,14},{10,... | collective-permute-start | bytes 196616 | tf_op jit(solution)/shard_map/ppermute | solution.py:134
  24.6 8.7 %collective-permute-start.5 = (bf16[8,32,128]{2,1,0:T(8,128)(2,1)S(1)}, bf16[8,32,128]{2,1,0:T(8,128)(2,1)S(1)}, u32[]{:S(2)}, u32[]{:S(2)}) collective-permute-start(bf16[8,32,128]{2,1,0:T(8,128)(2,1)S(1)} %maximum_bitcast_fusion.1), channel_id=1, source_target_pairs={{0,6},{1,7},{2,0},{3,1},{4,2},{5,3},{6,4},{7,5},{8,14},{9,15},{10,... | collective-permute-start | bytes 196616 | tf_op jit(solution)/shard_map/ppermute | solution.py:134
  27.9 6.1 %collective-permute-start.6 = (bf16[8,32,128]{2,1,0:T(8,128)(2,1)S(1)}, bf16[8,32,128]{2,1,0:T(8,128)(2,1)S(1)}, u32[]{:S(2)}, u32[]{:S(2)}) collective-permute-start(bf16[8,32,128]{2,1,0:T(8,128)(2,1)S(1)} %maximum_bitcast_fusion.1), channel_id=1, source_target_pairs={{0,7},{1,0},{2,1},{3,2},{4,3},{5,4},{6,5},{7,6},{8,15},{9,8},{10,9... | collective-permute-start | bytes 196616 | tf_op jit(solution)/shard_map/ppermute | solution.py:134
  34.6 14.9 %collective-permute-start.7 = (bf16[64,32,128]{2,1,0:T(8,128)(2,1)S(1)}, bf16[64,32,128]{2,1,0:T(8,128)(2,1)S(1)}, u32[]{:S(2)}, u32[]{:S(2)}) collective-permute-start(bf16[64,32,128]{2,1,0:T(8,128)(2,1)S(1)} %get-tuple-element.23), channel_id=1, source_target_pairs={{0,8},{8,16},{16,24},{24,0},{1,9},{9,17},{17,25},{25,1},{2,10},{10... | collective-permute-start | bytes 1572872 | tf_op jit(solution)/shard_map/ppermute | solution.py:143
  36.2 25.3 %collective-permute-start.8 = (bf16[64,32,128]{2,1,0:T(8,128)(2,1)S(1)}, bf16[64,32,128]{2,1,0:T(8,128)(2,1)S(1)}, u32[]{:S(2)}, u32[]{:S(2)}) collective-permute-start(bf16[64,32,128]{2,1,0:T(8,128)(2,1)S(1)} %get-tuple-element.23), channel_id=1, source_target_pairs={{0,16},{8,24},{16,0},{24,8},{1,17},{9,25},{17,1},{25,9},{2,18},{10... | collective-permute-start | bytes 1572872 | tf_op jit(solution)/shard_map/ppermute | solution.py:143
  39.3 23.0 %collective-permute-start.9 = (bf16[64,32,128]{2,1,0:T(8,128)(2,1)S(1)}, bf16[64,32,128]{2,1,0:T(8,128)(2,1)S(1)}, u32[]{:S(2)}, u32[]{:S(2)}) collective-permute-start(bf16[64,32,128]{2,1,0:T(8,128)(2,1)S(1)} %get-tuple-element.23), channel_id=1, source_target_pairs={{0,24},{8,0},{16,8},{24,16},{1,25},{9,1},{17,9},{25,17},{2,26},{10... | collective-permute-start | bytes 1572872 | tf_op jit(solution)/shard_map/ppermute | solution.py:143
  63.1 2.9 %copy-start = (s32[1,24,128]{2,1,0:T(8,128)S(1)}, s32[1,24,128]{2,1,0:T(8,128)}, u32[]{:S(2)}) copy-start(s32[1,24,128]{2,1,0:T(8,128)} %param.8) | copy-start | bytes 36868
  94.3 13.8 %collective-permute-start.13 = (f32[8,8,16,128]{3,2,1,0:T(8,128)}, f32[8,8,16,128]{3,2,1,0:T(8,128)}, u32[]{:S(2)}, u32[]{:S(2)}) collective-permute-start(f32[8,8,16,128]{3,2,1,0:T(8,128)} %get-tuple-element.4), channel_id=1, source_target_pairs={{0,8},{8,16},{16,24},{24,0},{1,9},{9,17},{17,25},{25,1},{2,10},{10... | collective-permute-start | bytes 1572872 | tf_op jit(solution)/shard_map/ppermute | solution.py:175
  94.8 25.6 %collective-permute-start.14 = (f32[8,8,16,128]{3,2,1,0:T(8,128)S(1)}, f32[8,8,16,128]{3,2,1,0:T(8,128)}, u32[]{:S(2)}, u32[]{:S(2)}) collective-permute-start(f32[8,8,16,128]{3,2,1,0:T(8,128)S(1)} %get-tuple-element.6), channel_id=1, source_target_pairs={{0,16},{8,24},{16,0},{24,8},{1,17},{9,25},{17,1},{25,9},{2,18},{10... | collective-permute-start | bytes 1572872 | tf_op jit(solution)/shard_map/ppermute | solution.py:175
  97.0 23.4 %collective-permute-start.15 = (f32[8,8,16,128]{3,2,1,0:T(8,128)S(1)}, f32[8,8,16,128]{3,2,1,0:T(8,128)}, u32[]{:S(2)}, u32[]{:S(2)}) collective-permute-start(f32[8,8,16,128]{3,2,1,0:T(8,128)S(1)} %get-tuple-element.5), channel_id=1, source_target_pairs={{0,24},{8,0},{16,8},{24,16},{1,25},{9,1},{17,9},{25,17},{2,26},{10... | collective-permute-start | bytes 1572872 | tf_op jit(solution)/shard_map/ppermute | solution.py:175
  98.7 58.1 %copy-start.2 = (f32[1024]{0:T(1024)S(1)}, f32[1024]{0:T(1024)}, u32[]{:S(2)}) copy-start(f32[1024]{0:T(1024)} %param.11) | copy-start | bytes 12292
  121.9 10.8 %collective-permute-start.16 = (f32[8,16,128]{2,1,0:T(8,128)S(1)}, f32[8,16,128]{2,1,0:T(8,128)S(1)}, u32[]{:S(2)}, u32[]{:S(2)}) collective-permute-start(f32[8,16,128]{2,1,0:T(8,128)S(1)} %get-tuple-element.7), channel_id=1, source_target_pairs={{0,1},{1,2},{2,3},{3,4},{4,5},{5,6},{6,7},{7,0},{8,9},{9,10},{10,1... | collective-permute-start | bytes 196616 | tf_op jit(solution)/shard_map/ppermute | solution.py:180
  124.1 10.4 %collective-permute-start.17 = (f32[8,16,128]{2,1,0:T(8,128)S(1)}, f32[8,16,128]{2,1,0:T(8,128)S(1)}, u32[]{:S(2)}, u32[]{:S(2)}) collective-permute-start(f32[8,16,128]{2,1,0:T(8,128)S(1)} %get-tuple-element.13), channel_id=1, source_target_pairs={{0,2},{1,3},{2,4},{3,5},{4,6},{5,7},{6,0},{7,1},{8,10},{9,11},{10,... | collective-permute-start | bytes 196616 | tf_op jit(solution)/shard_map/ppermute | solution.py:180
  124.8 16.4 %collective-permute-start.18 = (f32[8,16,128]{2,1,0:T(8,128)S(1)}, f32[8,16,128]{2,1,0:T(8,128)S(1)}, u32[]{:S(2)}, u32[]{:S(2)}) collective-permute-start(f32[8,16,128]{2,1,0:T(8,128)S(1)} %get-tuple-element.12), channel_id=1, source_target_pairs={{0,3},{1,4},{2,5},{3,6},{4,7},{5,0},{6,1},{7,2},{8,11},{9,12},{10,... | collective-permute-start | bytes 196616 | tf_op jit(solution)/shard_map/ppermute | solution.py:180
  126.6 16.6 %collective-permute-start.19 = (f32[8,16,128]{2,1,0:T(8,128)S(1)}, f32[8,16,128]{2,1,0:T(8,128)S(1)}, u32[]{:S(2)}, u32[]{:S(2)}) collective-permute-start(f32[8,16,128]{2,1,0:T(8,128)S(1)} %get-tuple-element.11), channel_id=1, source_target_pairs={{0,4},{1,5},{2,6},{3,7},{4,0},{5,1},{6,2},{7,3},{8,12},{9,13},{10,... | collective-permute-start | bytes 196616 | tf_op jit(solution)/shard_map/ppermute | solution.py:180
  130.1 16.8 %collective-permute-start.20 = (f32[8,16,128]{2,1,0:T(8,128)S(1)}, f32[8,16,128]{2,1,0:T(8,128)S(1)}, u32[]{:S(2)}, u32[]{:S(2)}) collective-permute-start(f32[8,16,128]{2,1,0:T(8,128)S(1)} %get-tuple-element.10), channel_id=1, source_target_pairs={{0,5},{1,6},{2,7},{3,0},{4,1},{5,2},{6,3},{7,4},{8,13},{9,14},{10,... | collective-permute-start | bytes 196616 | tf_op jit(solution)/shard_map/ppermute | solution.py:180
  132.7 16.7 %collective-permute-start.21 = (f32[8,16,128]{2,1,0:T(8,128)S(1)}, f32[8,16,128]{2,1,0:T(8,128)S(1)}, u32[]{:S(2)}, u32[]{:S(2)}) collective-permute-start(f32[8,16,128]{2,1,0:T(8,128)S(1)} %get-tuple-element.9), channel_id=1, source_target_pairs={{0,6},{1,7},{2,0},{3,1},{4,2},{5,3},{6,4},{7,5},{8,14},{9,15},{10,... | collective-permute-start | bytes 196616 | tf_op jit(solution)/shard_map/ppermute | solution.py:180
  134.5 17.0 %collective-permute-start.22 = (f32[8,16,128]{2,1,0:T(8,128)S(1)}, f32[8,16,128]{2,1,0:T(8,128)S(1)}, u32[]{:S(2)}, u32[]{:S(2)}) collective-permute-start(f32[8,16,128]{2,1,0:T(8,128)S(1)} %get-tuple-element.8), channel_id=1, source_target_pairs={{0,7},{1,0},{2,1},{3,2},{4,3},{5,4},{6,5},{7,6},{8,15},{9,8},{10,9... | collective-permute-start | bytes 196616 | tf_op jit(solution)/shard_map/ppermute | solution.py:180
  141.3 15.4 %collective-permute-start.23 = (f32[1,32,1024]{2,1,0:T(8,128)S(1)}, f32[1,32,1024]{2,1,0:T(8,128)S(1)}, u32[]{:S(2)}, u32[]{:S(2)}) collective-permute-start(f32[1,32,1024]{2,1,0:T(8,128)S(1)} %get-tuple-element.19), channel_id=1, source_target_pairs={{0,32},{32,64},{64,96},{96,128},{128,160},{160,192},{192,224},{1,3... | collective-permute-start | bytes 393224 | tf_op jit(solution)/shard_map/ppermute | solution.py:25
  143.2 13.5 %collective-permute-start.24 = (f32[1,32,1024]{2,1,0:T(8,128)S(1)}, f32[1,32,1024]{2,1,0:T(8,128)S(1)}, u32[]{:S(2)}, u32[]{:S(2)}) collective-permute-start(f32[1,32,1024]{2,1,0:T(8,128)S(1)} %get-tuple-element.19), channel_id=1, source_target_pairs={{32,0},{64,32},{96,64},{128,96},{160,128},{192,160},{224,192},{33,... | collective-permute-start | bytes 393224 | tf_op jit(solution)/shard_map/ppermute | solution.py:27
  146.9 6.3 %collective-permute-start.10 = (f32[8,16,128]{2,1,0:T(8,128)S(1)}, f32[8,16,128]{2,1,0:T(8,128)S(1)}, u32[]{:S(2)}, u32[]{:S(2)}) collective-permute-start(f32[8,16,128]{2,1,0:T(8,128)S(1)} %get-tuple-element.14), channel_id=1, source_target_pairs={{0,8},{8,16},{16,24},{24,0},{1,9},{9,17},{17,25},{25,1},{2,10},{10... | collective-permute-start | bytes 196616 | tf_op jit(solution)/shard_map/ppermute | solution.py:170
  149.4 5.8 %collective-permute-start.11 = (f32[8,16,128]{2,1,0:T(8,128)S(1)}, f32[8,16,128]{2,1,0:T(8,128)S(1)}, u32[]{:S(2)}, u32[]{:S(2)}) collective-permute-start(f32[8,16,128]{2,1,0:T(8,128)S(1)} %get-tuple-element.16), channel_id=1, source_target_pairs={{0,16},{8,24},{16,0},{24,8},{1,17},{9,25},{17,1},{25,9},{2,18},{10... | collective-permute-start | bytes 196616 | tf_op jit(solution)/shard_map/ppermute | solution.py:170
  151.6 4.3 %collective-permute-start.12 = (f32[8,16,128]{2,1,0:T(8,128)S(1)}, f32[8,16,128]{2,1,0:T(8,128)S(1)}, u32[]{:S(2)}, u32[]{:S(2)}) collective-permute-start(f32[8,16,128]{2,1,0:T(8,128)S(1)} %get-tuple-element.15), channel_id=1, source_target_pairs={{0,24},{8,0},{16,8},{24,16},{1,25},{9,1},{17,9},{25,17},{2,26},{10... | collective-permute-start | bytes 196616 | tf_op jit(solution)/shard_map/ppermute | solution.py:170
Sparse Core Ops, SparseCore 0:
  93.4 46.9 reduce-scatter.1

commit v9 on v7

--- a/solution.py
+++ b/solution.py
@@ -119,10 +119,11 @@
     flat = blks.reshape(-1)
     dest = ((flat // per) % inner) * (outer * per) + (flat // (inner * per)) * per + flat % per
     partial_terms = scatter_rows(dest, contrib, nblk)
-    grad_part = partial_terms[:, :arms]
-    hv_part = partial_terms[:, arms:].reshape(count, around, local_blk, arms, width)
+    cut = 3 * arms // 2
+    grad_part = partial_terms[:, :cut]
+    hv_part = partial_terms[:, cut:].reshape(count, around, local_blk, 2 * arms - cut, width)
     owned = lax.psum_scatter(grad_part, "row_1", scatter_dimension=0, tiled=True)
-    chunks = owned.reshape(around, -1, arms, width)
+    chunks = owned.reshape(around, -1, cut, width)
     total = chunks[there]
     for s in range(1, around):
         total = total + lax.ppermute(

time: 156 us -> 161 us (1.032)
  local copies, waits for them, and re-layouts: 14.5 us -> 17.2 us
  waiting for transfers between devices: 52 us -> 54.4 us
    reduce_scatter x1, waiting for transfers between devices: 4.93 us -> 19.5 us  [on_device(): lax.psum_scatter(grad_part, 'row_1', scatter_dimension=0, tiled=True)]
    ppermute x3, waiting for transfers between devices: 21.7 us -> 10.1 us  [on_device(): lax.ppermute(hv_part[:, (there + s) % around], 'row_0', [(i, (i + s) % ar...]
    unnamed x17 -> x19, local copies, waits for them, and re-layouts: 5.65 us -> 7.62 us
    slice x1 -> x2, local copies, waits for them, and re-layouts: 1.7 us -> 3.28 us  [the longest x1 1.99 us: on_device(): grad_part = partial_terms[:, :cut]]
  transfers between devices with their start and end apart: 26 -> 26, of which waited for: 9 -> 9; matrix products, arithmetic and copies ran while one was open for 7% -> 6% of each run, Pallas kernels for 0% -> 0%
where the time goes in v9:
time: 161 us; the launch traced here: 160 us
  starting transfers between devices  54.6 us (34%)
  waiting for transfers between devices  54.4 us (34%)
  local copies, waits for them, and re-layouts  17.2 us (11%)
  between operations  14.3 us (9%)
  matrix products  12.6 us (8%)
  other arithmetic  4.45 us (3%)
  Pallas kernels  2.54 us (2%)
    ppermute x3, waiting for transfers between devices, on_device(): lax.ppermute(stage, 'row_0', [(i, (i + s) % around) for i in range(around)])  19.8 us
    reduce_scatter x1, waiting for transfers between devices, on_device(): lax.psum_scatter(grad_part, 'row_1', scatter_dimension=0, tiled=True)  19.5 us
    ppermute x7, starting transfers between devices, on_device(): lax.ppermute(by_block, 'row_1', [(i, (i + s) % count) for i in range(coun...  18.5 us
    ppermute x7, starting transfers between devices, on_device(): lax.ppermute(across[(here + s) % count], 'row_1', [(i, (i + s) % count) f...  13.9 us
    ppermute x3, waiting for transfers between devices, on_device(): lax.ppermute(hv_part[:, (there + s) % around], 'row_0', [(i, (i + s) % ar...  10.1 us
    unnamed x19, local copies, waits for them, and re-layouts  7.62 us
    dot_general x1, matrix products, on_device(): jnp.einsum('tari,taki->tkr', feats, selected, preferred_element_type=jnp....  7.05 us
    ppermute x3, starting transfers between devices, on_device(): lax.ppermute(chunks[(there + s) % around], 'row_0', [(i, (i + s) % around...  6.12 us
  transfers between devices with their start and end apart: 26, of which 9 were waited for; matrix products, arithmetic and copies ran while one was open for 6% of the time, Pallas kernels for 0%

profile of v9, /device:TPU:2, one launch (start us, length us, event | category | flops | bytes accessed | tf_op | source)
XLA Modules:
  0.0 160.1 jit_solution(17223779845752654943)
XLA Ops:
  7.2 0.9 constant_dynamic-update-slice_fusion.20
  8.1 0.9 constant_dynamic-update-slice_fusion.19
  9.2 2.0 %collective-permute-start = (bf16[8,32,128]{2,1,0:T(8,128)(2,1)S(1)}, bf16[8,32,128]{2,1,0:T(8,128)(2,1)S(1)}, u32[]{:S(2)}, u32[]{:S(2)}) collective-permute-start(bf16[8,32,128]{2,1,0:T(8,128)(2,1)S(1)} %maximum_bitcast_fusion.3), channel_id=1, source_target_pairs={{0,1},{1,2},{2,3},{3,4},{4,5},{5,6},{6,7},{7,0},{8,9},{9,10},{10,1... | collective-permute-start | bytes 196616 | tf_op jit(solution)/shard_map/ppermute | solution.py:80
  11.1 3.3 %collective-permute-start.1 = (bf16[8,32,128]{2,1,0:T(8,128)(2,1)S(1)}, bf16[8,32,128]{2,1,0:T(8,128)(2,1)S(1)}, u32[]{:S(2)}, u32[]{:S(2)}) collective-permute-start(bf16[8,32,128]{2,1,0:T(8,128)(2,1)S(1)} %maximum_bitcast_fusion.3), channel_id=1, source_target_pairs={{0,2},{1,3},{2,4},{3,5},{4,6},{5,7},{6,0},{7,1},{8,10},{9,11},{10,... | collective-permute-start | bytes 196616 | tf_op jit(solution)/shard_map/ppermute | solution.py:80
  14.4 4.0 %collective-permute-start.2 = (bf16[8,32,128]{2,1,0:T(8,128)(2,1)S(1)}, bf16[8,32,128]{2,1,0:T(8,128)(2,1)S(1)}, u32[]{:S(2)}, u32[]{:S(2)}) collective-permute-start(bf16[8,32,128]{2,1,0:T(8,128)(2,1)S(1)} %maximum_bitcast_fusion.3), channel_id=1, source_target_pairs={{0,3},{1,4},{2,5},{3,6},{4,7},{5,0},{6,1},{7,2},{8,11},{9,12},{10,... | collective-permute-start | bytes 196616 | tf_op jit(solution)/shard_map/ppermute | solution.py:80
  19.0 4.9 %collective-permute-start.4 = (bf16[8,32,128]{2,1,0:T(8,128)(2,1)S(1)}, bf16[8,32,128]{2,1,0:T(8,128)(2,1)S(1)}, u32[]{:S(2)}, u32[]{:S(2)}) collective-permute-start(bf16[8,32,128]{2,1,0:T(8,128)(2,1)S(1)} %maximum_bitcast_fusion.3), channel_id=1, source_target_pairs={{0,5},{1,6},{2,7},{3,0},{4,1},{5,2},{6,3},{7,4},{8,13},{9,14},{10,... | collective-permute-start | bytes 196616 | tf_op jit(solution)/shard_map/ppermute | solution.py:80
  24.6 2.7 %collective-permute-start.5 = (bf16[8,32,128]{2,1,0:T(8,128)(2,1)S(1)}, bf16[8,32,128]{2,1,0:T(8,128)(2,1)S(1)}, u32[]{:S(2)}, u32[]{:S(2)}) collective-permute-start(bf16[8,32,128]{2,1,0:T(8,128)(2,1)S(1)} %maximum_bitcast_fusion.3), channel_id=1, source_target_pairs={{0,6},{1,7},{2,0},{3,1},{4,2},{5,3},{6,4},{7,5},{8,14},{9,15},{10,... | collective-permute-start | bytes 196616 | tf_op jit(solution)/shard_map/ppermute | solution.py:80
  27.9 1.0 collective-permute-start.6
  29.6 0.7 constant_dynamic-update-slice_fusion.4
  30.9 1.8 %collective-permute-done.4 = bf16[8,32,128]{2,1,0:T(8,128)(2,1)S(1)} collective-permute-done((bf16[8,32,128]{2,1,0:T(8,128)(2,1)S(1)}, bf16[8,32,128]{2,1,0:T(8,128)(2,1)S(1)}, u32[]{:S(2)}, u32[]{:S(2)}) %collective-permute-start.4) | collective-permute-done | bytes 65568 | tf_op jit(solution)/shard_map/ppermute | solution.py:80
  32.7 0.7 constant_dynamic-update-slice_fusion.2
  34.6 1.6 collective-permute-start.7
  36.2 2.9 %collective-permute-start.8 = (bf16[64,32,128]{2,1,0:T(8,128)(2,1)S(1)}, bf16[64,32,128]{2,1,0:T(8,128)(2,1)S(1)}, u32[]{:S(2)}, u32[]{:S(2)}) collective-permute-start(bf16[64,32,128]{2,1,0:T(8,128)(2,1)S(1)} %get-tuple-element.21), channel_id=1, source_target_pairs={{0,16},{8,24},{16,0},{24,8},{1,17},{9,25},{17,1},{25,9},{2,18},{10... | collective-permute-start | bytes 1572872 | tf_op jit(solution)/shard_map/ppermute | solution.py:89
  39.3 1.4 collective-permute-start.9
  40.8 8.7 %collective-permute-done.7 = bf16[64,32,128]{2,1,0:T(8,128)(2,1)S(1)} collective-permute-done((bf16[64,32,128]{2,1,0:T(8,128)(2,1)S(1)}, bf16[64,32,128]{2,1,0:T(8,128)(2,1)S(1)}, u32[]{:S(2)}, u32[]{:S(2)}) %collective-permute-start.7) | collective-permute-done | bytes 524320 | tf_op jit(solution)/shard_map/ppermute | solution.py:89
  49.5 0.8 constant_dynamic-update-slice_fusion.10
  50.3 11.1 %collective-permute-done.8 = bf16[64,32,128]{2,1,0:T(8,128)(2,1)S(1)} collective-permute-done((bf16[64,32,128]{2,1,0:T(8,128)(2,1)S(1)}, bf16[64,32,128]{2,1,0:T(8,128)(2,1)S(1)}, u32[]{:S(2)}, u32[]{:S(2)}) %collective-permute-start.8) | collective-permute-done | bytes 524320 | tf_op jit(solution)/shard_map/ppermute | solution.py:89
  61.5 0.8 constant_dynamic-update-slice_fusion.9
  62.3 0.8 constant_dynamic-update-slice_fusion.8
  63.2 2.8 %gather_fusion = bf16[384,32,128]{2,1,0:T(8,128)(2,1)S(1)} fusion(bf16[256,32,128]{2,1,0:T(8,128)(2,1)} %constant_dynamic-update-slice_fusion.8, s32[1024]{0:T(1024)S(1)} %pad_clamp_fusion), kind=kCustom, calls=%fused_computation | custom fusion | bytes 6292992 | tf_op jit(solution)/shard_map/gather | solution.py:102
  66.0 7.0 %fusion.9 = f32[24,32,128]{2,1,0:T(8,128)S(1)} fusion(bf16[24,16,32,128]{3,2,1,0:T(8,128)(2,1)S(1)} %bitcast.124, bf16[1,24,16,128,128]{4,3,2,1,0:T(8,128)(2,1)} %param.6), kind=kOutput, calls=%fused_computation.8 | convolution fusion | flops 402653184 | bytes 16121856 | tf_op jit(solution)/shard_map/tari,taki->tkr/dot_general | solution.py:104
  73.1 0.8 subtract_convert_fusion
  73.9 5.6 %fusion.6.part_ref = f32[24,16,32,128]{3,2,1,0:T(8,128)S(1)} fusion(bf16[1,24,16,128,128]{4,3,2,1,0:T(8,128)(2,1)} %param.6, bf16[24,16,128]{2,1,0:T(8,128)(2,1)S(1)} %fusion.15, bf16[24,16,128]{2,1,0:T(8,128)(2,1)S(1)} %get-tuple-element.37), kind=kOutput, calls=%fused_computation.7 | convolution fusion | flops 403046400 | bytes 19070976 | tf_op jit(solution)/shard_map/tari,tkr->taki/dot_general | solution.py:115
  79.5 2.5 %shard_map.77 = f32[256,32,128]{2,1,0:T(8,128)S(1)} custom-call(s32[384]{0:T(512)S(1)} %fusion.45.dest_ref, f32[24,16,32,128]{3,2,1,0:T(8,128)S(1)} %fusion.6.part_ref), custom_call_target="tpu_custom_call" | custom-call | tf_op jit(solution)/shard_map/pallas_call | solution.py:56
  82.1 2.0 %copy-done = f32[256,32,128]{2,1,0:T(8,128)} copy-done((f32[256,32,128]{2,1,0:T(8,128)}, f32[256,32,128]{2,1,0:T(8,128)S(1)}, u32[]{:S(2)}) %copy-start) | copy-done | bytes 4194328
  84.0 2.0 %slice.28 = f32[256,24,128]{2,1,0:T(8,128)} slice(f32[256,32,128]{2,1,0:T(8,128)S(1)} %shard_map.77), slice={[0:256], [0:24], [0:128]} | slice | bytes 6291456 | tf_op jit(solution)/shard_map/slice | solution.py:123
  86.1 1.3 slice.29
  87.5 0.8 collective-permute-start.13
  88.2 2.2 %collective-permute-start.14 = (f32[8,8,8,128]{3,2,1,0:T(8,128)S(1)}, f32[8,8,8,128]{3,2,1,0:T(8,128)S(1)}, u32[]{:S(2)}, u32[]{:S(2)}) collective-permute-start(f32[8,8,8,128]{3,2,1,0:T(8,128)S(1)} %get-tuple-element.4), channel_id=1, source_target_pairs={{0,16},{8,24},{16,0},{24,8},{1,17},{9,25},{17,1},{25,9},{2,18},{10... | collective-permute-start | bytes 786440 | tf_op jit(solution)/shard_map/ppermute | solution.py:134
  90.4 1.7 %collective-permute-start.15 = (f32[8,8,8,128]{3,2,1,0:T(8,128)S(1)}, f32[8,8,8,128]{3,2,1,0:T(8,128)S(1)}, u32[]{:S(2)}, u32[]{:S(2)}) collective-permute-start(f32[8,8,8,128]{3,2,1,0:T(8,128)S(1)} %get-tuple-element.3), channel_id=1, source_target_pairs={{0,24},{8,0},{16,8},{24,16},{1,25},{9,1},{17,9},{25,17},{2,26},{10... | collective-permute-start | bytes 786440 | tf_op jit(solution)/shard_map/ppermute | solution.py:134
  92.1 3.5 %collective-permute-done.13 = f32[8,8,8,128]{3,2,1,0:T(8,128)S(1)} collective-permute-done((f32[8,8,8,128]{3,2,1,0:T(8,128)S(1)}, f32[8,8,8,128]{3,2,1,0:T(8,128)S(1)}, u32[]{:S(2)}, u32[]{:S(2)}) %collective-permute-start.13) | collective-permute-done | bytes 262176 | tf_op jit(solution)/shard_map/ppermute | solution.py:134
  95.6 6.6 %collective-permute-done.14 = f32[8,8,8,128]{3,2,1,0:T(8,128)S(1)} collective-permute-done((f32[8,8,8,128]{3,2,1,0:T(8,128)S(1)}, f32[8,8,8,128]{3,2,1,0:T(8,128)S(1)}, u32[]{:S(2)}, u32[]{:S(2)}) %collective-permute-start.14) | collective-permute-done | bytes 262176 | tf_op jit(solution)/shard_map/ppermute | solution.py:134
  102.3 2.4 %collective-permute-start.16 = (f32[8,8,128]{2,1,0:T(8,128)S(1)}, f32[8,8,128]{2,1,0:T(8,128)S(1)}, u32[]{:S(2)}, u32[]{:S(2)}) collective-permute-start(f32[8,8,128]{2,1,0:T(8,128)S(1)} %get-tuple-element.8), channel_id=1, source_target_pairs={{0,1},{1,2},{2,3},{3,4},{4,5},{5,6},{6,7},{7,0},{8,9},{9,10},{10,1... | collective-permute-start | bytes 98312 | tf_op jit(solution)/shard_map/ppermute | solution.py:139
  105.3 1.8 %collective-permute-start.18 = (f32[8,8,128]{2,1,0:T(8,128)S(1)}, f32[8,8,128]{2,1,0:T(8,128)S(1)}, u32[]{:S(2)}, u32[]{:S(2)}) collective-permute-start(f32[8,8,128]{2,1,0:T(8,128)S(1)} %get-tuple-element.13), channel_id=1, source_target_pairs={{0,3},{1,4},{2,5},{3,6},{4,7},{5,0},{6,1},{7,2},{8,11},{9,12},{10,... | collective-permute-start | bytes 98312 | tf_op jit(solution)/shard_map/ppermute | solution.py:139
  107.0 3.7 %collective-permute-start.19 = (f32[8,8,128]{2,1,0:T(8,128)S(1)}, f32[8,8,128]{2,1,0:T(8,128)S(1)}, u32[]{:S(2)}, u32[]{:S(2)}) collective-permute-start(f32[8,8,128]{2,1,0:T(8,128)S(1)} %get-tuple-element.12), channel_id=1, source_target_pairs={{0,4},{1,5},{2,6},{3,7},{4,0},{5,1},{6,2},{7,3},{8,12},{9,13},{10,... | collective-permute-start | bytes 98312 | tf_op jit(solution)/shard_map/ppermute | solution.py:139
  110.7 2.4 %collective-permute-start.20 = (f32[8,8,128]{2,1,0:T(8,128)S(1)}, f32[8,8,128]{2,1,0:T(8,128)S(1)}, u32[]{:S(2)}, u32[]{:S(2)}) collective-permute-start(f32[8,8,128]{2,1,0:T(8,128)S(1)} %get-tuple-element.11), channel_id=1, source_target_pairs={{0,5},{1,6},{2,7},{3,0},{4,1},{5,2},{6,3},{7,4},{8,13},{9,14},{10,... | collective-permute-start | bytes 98312 | tf_op jit(solution)/shard_map/ppermute | solution.py:139
  113.1 1.4 collective-permute-start.21
  114.5 1.7 %collective-permute-start.22 = (f32[8,8,128]{2,1,0:T(8,128)S(1)}, f32[8,8,128]{2,1,0:T(8,128)S(1)}, u32[]{:S(2)}, u32[]{:S(2)}) collective-permute-start(f32[8,8,128]{2,1,0:T(8,128)S(1)} %get-tuple-element.9), channel_id=1, source_target_pairs={{0,7},{1,0},{2,1},{3,2},{4,3},{5,4},{6,5},{7,6},{8,15},{9,8},{10,9... | collective-permute-start | bytes 98312 | tf_op jit(solution)/shard_map/ppermute | solution.py:139
  116.3 19.5 %reduce-scatter.2.cloned.1.call-done = f32[32,24,128]{2,1,0:T(8,128)} async-done(((f32[256,24,128]{2,1,0:T(8,128)}), f32[32,24,128]{2,1,0:T(8,128)}) %reduce-scatter.2.cloned.1.call-update) | async-done | bytes 393232 | tf_op jit(solution)/shard_map/reduce_scatter | solution.py:125
  135.8 1.0 dynamic-slice_bitcast_fusion.5
  136.8 1.9 %collective-permute-start.23 = (f32[1,32,1024]{2,1,0:T(8,128)S(1)}, f32[1,32,1024]{2,1,0:T(8,128)S(1)}, u32[]{:S(2)}, u32[]{:S(2)}) collective-permute-start(f32[1,32,1024]{2,1,0:T(8,128)S(1)} %get-tuple-element.17), channel_id=1, source_target_pairs={{0,32},{32,64},{64,96},{96,128},{128,160},{160,192},{192,224},{1,3... | collective-permute-start | bytes 393224 | tf_op jit(solution)/shard_map/ppermute | solution.py:25
  138.8 3.6 %collective-permute-start.24 = (f32[1,32,1024]{2,1,0:T(8,128)S(1)}, f32[1,32,1024]{2,1,0:T(8,128)S(1)}, u32[]{:S(2)}, u32[]{:S(2)}) collective-permute-start(f32[1,32,1024]{2,1,0:T(8,128)S(1)} %get-tuple-element.17), channel_id=1, source_target_pairs={{32,0},{64,32},{96,64},{128,96},{160,128},{192,160},{224,192},{33,... | collective-permute-start | bytes 393224 | tf_op jit(solution)/shard_map/ppermute | solution.py:27
  142.4 1.6 collective-permute-start.10
  144.0 3.0 %collective-permute-start.11 = (f32[8,24,128]{2,1,0:T(8,128)S(1)}, f32[8,24,128]{2,1,0:T(8,128)S(1)}, u32[]{:S(2)}, u32[]{:S(2)}) collective-permute-start(f32[8,24,128]{2,1,0:T(8,128)S(1)} %get-tuple-element.7), channel_id=1, source_target_pairs={{0,16},{8,24},{16,0},{24,8},{1,17},{9,25},{17,1},{25,9},{2,18},{10... | collective-permute-start | bytes 294920 | tf_op jit(solution)/shard_map/ppermute | solution.py:129
  147.0 1.6 collective-permute-start.12
  148.8 2.8 %collective-permute-done.11 = f32[8,24,128]{2,1,0:T(8,128)S(1)} collective-permute-done((f32[8,24,128]{2,1,0:T(8,128)S(1)}, f32[8,24,128]{2,1,0:T(8,128)S(1)}, u32[]{:S(2)}, u32[]{:S(2)}) %collective-permute-start.11) | collective-permute-done | bytes 98336 | tf_op jit(solution)/shard_map/ppermute | solution.py:129
  151.6 0.9 fusion.23
  152.6 0.7 slice_bitcast_fusion
  (54 shorter events, 6.0 us)
Async XLA Ops:
  7.2 31.9 %copy-start.1 = (s32[1,24,16]{1,2,0:T(8,128)S(1)}, s32[1,24,16]{1,2,0:T(8,128)}, u32[]{:S(2)}) copy-start(s32[1,24,16]{1,2,0:T(8,128)} %param.7) | copy-start | bytes 4612
  7.2 128.7 %reduce-scatter.2.cloned.1.call-start = ((), (), s32[]{:S(2)}) async-start(), calls=%async_computation.1 | async-start | bytes 3538944 | tf_op jit(solution)/shard_map/reduce_scatter | solution.py:125
  9.2 15.4 %collective-permute-start = (bf16[8,32,128]{2,1,0:T(8,128)(2,1)S(1)}, bf16[8,32,128]{2,1,0:T(8,128)(2,1)S(1)}, u32[]{:S(2)}, u32[]{:S(2)}) collective-permute-start(bf16[8,32,128]{2,1,0:T(8,128)(2,1)S(1)} %maximum_bitcast_fusion.3), channel_id=1, source_target_pairs={{0,1},{1,2},{2,3},{3,4},{4,5},{5,6},{6,7},{7,0},{8,9},{9,10},{10,1... | collective-permute-start | bytes 196616 | tf_op jit(solution)/shard_map/ppermute | solution.py:80
  11.1 16.8 %collective-permute-start.1 = (bf16[8,32,128]{2,1,0:T(8,128)(2,1)S(1)}, bf16[8,32,128]{2,1,0:T(8,128)(2,1)S(1)}, u32[]{:S(2)}, u32[]{:S(2)}) collective-permute-start(bf16[8,32,128]{2,1,0:T(8,128)(2,1)S(1)} %maximum_bitcast_fusion.3), channel_id=1, source_target_pairs={{0,2},{1,3},{2,4},{3,5},{4,6},{5,7},{6,0},{7,1},{8,10},{9,11},{10,... | collective-permute-start | bytes 196616 | tf_op jit(solution)/shard_map/ppermute | solution.py:80
  14.4 15.1 %collective-permute-start.2 = (bf16[8,32,128]{2,1,0:T(8,128)(2,1)S(1)}, bf16[8,32,128]{2,1,0:T(8,128)(2,1)S(1)}, u32[]{:S(2)}, u32[]{:S(2)}) collective-permute-start(bf16[8,32,128]{2,1,0:T(8,128)(2,1)S(1)} %maximum_bitcast_fusion.3), channel_id=1, source_target_pairs={{0,3},{1,4},{2,5},{3,6},{4,7},{5,0},{6,1},{7,2},{8,11},{9,12},{10,... | collective-permute-start | bytes 196616 | tf_op jit(solution)/shard_map/ppermute | solution.py:80
  18.5 11.8 %collective-permute-start.3 = (bf16[8,32,128]{2,1,0:T(8,128)(2,1)S(1)}, bf16[8,32,128]{2,1,0:T(8,128)(2,1)S(1)}, u32[]{:S(2)}, u32[]{:S(2)}) collective-permute-start(bf16[8,32,128]{2,1,0:T(8,128)(2,1)S(1)} %maximum_bitcast_fusion.3), channel_id=1, source_target_pairs={{0,4},{1,5},{2,6},{3,7},{4,0},{5,1},{6,2},{7,3},{8,12},{9,13},{10,... | collective-permute-start | bytes 196616 | tf_op jit(solution)/shard_map/ppermute | solution.py:80
  19.0 13.7 %collective-permute-start.4 = (bf16[8,32,128]{2,1,0:T(8,128)(2,1)S(1)}, bf16[8,32,128]{2,1,0:T(8,128)(2,1)S(1)}, u32[]{:S(2)}, u32[]{:S(2)}) collective-permute-start(bf16[8,32,128]{2,1,0:T(8,128)(2,1)S(1)} %maximum_bitcast_fusion.3), channel_id=1, source_target_pairs={{0,5},{1,6},{2,7},{3,0},{4,1},{5,2},{6,3},{7,4},{8,13},{9,14},{10,... | collective-permute-start | bytes 196616 | tf_op jit(solution)/shard_map/ppermute | solution.py:80
  24.6 8.7 %collective-permute-start.5 = (bf16[8,32,128]{2,1,0:T(8,128)(2,1)S(1)}, bf16[8,32,128]{2,1,0:T(8,128)(2,1)S(1)}, u32[]{:S(2)}, u32[]{:S(2)}) collective-permute-start(bf16[8,32,128]{2,1,0:T(8,128)(2,1)S(1)} %maximum_bitcast_fusion.3), channel_id=1, source_target_pairs={{0,6},{1,7},{2,0},{3,1},{4,2},{5,3},{6,4},{7,5},{8,14},{9,15},{10,... | collective-permute-start | bytes 196616 | tf_op jit(solution)/shard_map/ppermute | solution.py:80
  27.9 6.1 %collective-permute-start.6 = (bf16[8,32,128]{2,1,0:T(8,128)(2,1)S(1)}, bf16[8,32,128]{2,1,0:T(8,128)(2,1)S(1)}, u32[]{:S(2)}, u32[]{:S(2)}) collective-permute-start(bf16[8,32,128]{2,1,0:T(8,128)(2,1)S(1)} %maximum_bitcast_fusion.3), channel_id=1, source_target_pairs={{0,7},{1,0},{2,1},{3,2},{4,3},{5,4},{6,5},{7,6},{8,15},{9,8},{10,9... | collective-permute-start | bytes 196616 | tf_op jit(solution)/shard_map/ppermute | solution.py:80
  34.6 14.9 %collective-permute-start.7 = (bf16[64,32,128]{2,1,0:T(8,128)(2,1)S(1)}, bf16[64,32,128]{2,1,0:T(8,128)(2,1)S(1)}, u32[]{:S(2)}, u32[]{:S(2)}) collective-permute-start(bf16[64,32,128]{2,1,0:T(8,128)(2,1)S(1)} %get-tuple-element.21), channel_id=1, source_target_pairs={{0,8},{8,16},{16,24},{24,0},{1,9},{9,17},{17,25},{25,1},{2,10},{10... | collective-permute-start | bytes 1572872 | tf_op jit(solution)/shard_map/ppermute | solution.py:89
  36.2 25.3 %collective-permute-start.8 = (bf16[64,32,128]{2,1,0:T(8,128)(2,1)S(1)}, bf16[64,32,128]{2,1,0:T(8,128)(2,1)S(1)}, u32[]{:S(2)}, u32[]{:S(2)}) collective-permute-start(bf16[64,32,128]{2,1,0:T(8,128)(2,1)S(1)} %get-tuple-element.21), channel_id=1, source_target_pairs={{0,16},{8,24},{16,0},{24,8},{1,17},{9,25},{17,1},{25,9},{2,18},{10... | collective-permute-start | bytes 1572872 | tf_op jit(solution)/shard_map/ppermute | solution.py:89
  39.3 23.0 %collective-permute-start.9 = (bf16[64,32,128]{2,1,0:T(8,128)(2,1)S(1)}, bf16[64,32,128]{2,1,0:T(8,128)(2,1)S(1)}, u32[]{:S(2)}, u32[]{:S(2)}) collective-permute-start(bf16[64,32,128]{2,1,0:T(8,128)(2,1)S(1)} %get-tuple-element.21), channel_id=1, source_target_pairs={{0,24},{8,0},{16,8},{24,16},{1,25},{9,1},{17,9},{25,17},{2,26},{10... | collective-permute-start | bytes 1572872 | tf_op jit(solution)/shard_map/ppermute | solution.py:89
  66.0 7.1 %copy-start.3 = (s32[1,24,128]{2,1,0:T(8,128)S(1)}, s32[1,24,128]{2,1,0:T(8,128)}, u32[]{:S(2)}) copy-start(s32[1,24,128]{2,1,0:T(8,128)} %param.8) | copy-start | bytes 36868
  82.0 2.0 %copy-start = (f32[256,32,128]{2,1,0:T(8,128)}, f32[256,32,128]{2,1,0:T(8,128)S(1)}, u32[]{:S(2)}) copy-start(f32[256,32,128]{2,1,0:T(8,128)S(1)} %shard_map.77) | copy-start | bytes 12582916
  87.5 65.1 %copy-start.2 = (f32[1024]{0:T(1024)S(1)}, f32[1024]{0:T(1024)}, u32[]{:S(2)}) copy-start(f32[1024]{0:T(1024)} %param.11) | copy-start | bytes 12292
  87.5 8.2 %collective-permute-start.13 = (f32[8,8,8,128]{3,2,1,0:T(8,128)S(1)}, f32[8,8,8,128]{3,2,1,0:T(8,128)S(1)}, u32[]{:S(2)}, u32[]{:S(2)}) collective-permute-start(f32[8,8,8,128]{3,2,1,0:T(8,128)S(1)} %get-tuple-element.2), channel_id=1, source_target_pairs={{0,8},{8,16},{16,24},{24,0},{1,9},{9,17},{17,25},{25,1},{2,10},{10... | collective-permute-start | bytes 786440 | tf_op jit(solution)/shard_map/ppermute | solution.py:134
  88.2 14.0 %collective-permute-start.14 = (f32[8,8,8,128]{3,2,1,0:T(8,128)S(1)}, f32[8,8,8,128]{3,2,1,0:T(8,128)S(1)}, u32[]{:S(2)}, u32[]{:S(2)}) collective-permute-start(f32[8,8,8,128]{3,2,1,0:T(8,128)S(1)} %get-tuple-element.4), channel_id=1, source_target_pairs={{0,16},{8,24},{16,0},{24,8},{1,17},{9,25},{17,1},{25,9},{2,18},{10... | collective-permute-start | bytes 786440 | tf_op jit(solution)/shard_map/ppermute | solution.py:134
  90.4 11.8 %collective-permute-start.15 = (f32[8,8,8,128]{3,2,1,0:T(8,128)S(1)}, f32[8,8,8,128]{3,2,1,0:T(8,128)S(1)}, u32[]{:S(2)}, u32[]{:S(2)}) collective-permute-start(f32[8,8,8,128]{3,2,1,0:T(8,128)S(1)} %get-tuple-element.3), channel_id=1, source_target_pairs={{0,24},{8,0},{16,8},{24,16},{1,25},{9,1},{17,9},{25,17},{2,26},{10... | collective-permute-start | bytes 786440 | tf_op jit(solution)/shard_map/ppermute | solution.py:134
  102.3 10.8 %collective-permute-start.16 = (f32[8,8,128]{2,1,0:T(8,128)S(1)}, f32[8,8,128]{2,1,0:T(8,128)S(1)}, u32[]{:S(2)}, u32[]{:S(2)}) collective-permute-start(f32[8,8,128]{2,1,0:T(8,128)S(1)} %get-tuple-element.8), channel_id=1, source_target_pairs={{0,1},{1,2},{2,3},{3,4},{4,5},{5,6},{6,7},{7,0},{8,9},{9,10},{10,1... | collective-permute-start | bytes 98312 | tf_op jit(solution)/shard_map/ppermute | solution.py:139
  104.7 9.8 %collective-permute-start.17 = (f32[8,8,128]{2,1,0:T(8,128)S(1)}, f32[8,8,128]{2,1,0:T(8,128)S(1)}, u32[]{:S(2)}, u32[]{:S(2)}) collective-permute-start(f32[8,8,128]{2,1,0:T(8,128)S(1)} %get-tuple-element.14), channel_id=1, source_target_pairs={{0,2},{1,3},{2,4},{3,5},{4,6},{5,7},{6,0},{7,1},{8,10},{9,11},{10,... | collective-permute-start | bytes 98312 | tf_op jit(solution)/shard_map/ppermute | solution.py:139
  105.3 31.6 %collective-permute-start.18 = (f32[8,8,128]{2,1,0:T(8,128)S(1)}, f32[8,8,128]{2,1,0:T(8,128)S(1)}, u32[]{:S(2)}, u32[]{:S(2)}) collective-permute-start(f32[8,8,128]{2,1,0:T(8,128)S(1)} %get-tuple-element.13), channel_id=1, source_target_pairs={{0,3},{1,4},{2,5},{3,6},{4,7},{5,0},{6,1},{7,2},{8,11},{9,12},{10,... | collective-permute-start | bytes 98312 | tf_op jit(solution)/shard_map/ppermute | solution.py:139
  107.0 31.8 %collective-permute-start.19 = (f32[8,8,128]{2,1,0:T(8,128)S(1)}, f32[8,8,128]{2,1,0:T(8,128)S(1)}, u32[]{:S(2)}, u32[]{:S(2)}) collective-permute-start(f32[8,8,128]{2,1,0:T(8,128)S(1)} %get-tuple-element.12), channel_id=1, source_target_pairs={{0,4},{1,5},{2,6},{3,7},{4,0},{5,1},{6,2},{7,3},{8,12},{9,13},{10,... | collective-permute-start | bytes 98312 | tf_op jit(solution)/shard_map/ppermute | solution.py:139
  110.7 31.7 %collective-permute-start.20 = (f32[8,8,128]{2,1,0:T(8,128)S(1)}, f32[8,8,128]{2,1,0:T(8,128)S(1)}, u32[]{:S(2)}, u32[]{:S(2)}) collective-permute-start(f32[8,8,128]{2,1,0:T(8,128)S(1)} %get-tuple-element.11), channel_id=1, source_target_pairs={{0,5},{1,6},{2,7},{3,0},{4,1},{5,2},{6,3},{7,4},{8,13},{9,14},{10,... | collective-permute-start | bytes 98312 | tf_op jit(solution)/shard_map/ppermute | solution.py:139
  113.1 30.9 %collective-permute-start.21 = (f32[8,8,128]{2,1,0:T(8,128)S(1)}, f32[8,8,128]{2,1,0:T(8,128)S(1)}, u32[]{:S(2)}, u32[]{:S(2)}) collective-permute-start(f32[8,8,128]{2,1,0:T(8,128)S(1)} %get-tuple-element.10), channel_id=1, source_target_pairs={{0,6},{1,7},{2,0},{3,1},{4,2},{5,3},{6,4},{7,5},{8,14},{9,15},{10,... | collective-permute-start | bytes 98312 | tf_op jit(solution)/shard_map/ppermute | solution.py:139
  114.5 32.5 %collective-permute-start.22 = (f32[8,8,128]{2,1,0:T(8,128)S(1)}, f32[8,8,128]{2,1,0:T(8,128)S(1)}, u32[]{:S(2)}, u32[]{:S(2)}) collective-permute-start(f32[8,8,128]{2,1,0:T(8,128)S(1)} %get-tuple-element.9), channel_id=1, source_target_pairs={{0,7},{1,0},{2,1},{3,2},{4,3},{5,4},{6,5},{7,6},{8,15},{9,8},{10,9... | collective-permute-start | bytes 98312 | tf_op jit(solution)/shard_map/ppermute | solution.py:139
  136.8 15.7 %collective-permute-start.23 = (f32[1,32,1024]{2,1,0:T(8,128)S(1)}, f32[1,32,1024]{2,1,0:T(8,128)S(1)}, u32[]{:S(2)}, u32[]{:S(2)}) collective-permute-start(f32[1,32,1024]{2,1,0:T(8,128)S(1)} %get-tuple-element.17), channel_id=1, source_target_pairs={{0,32},{32,64},{64,96},{96,128},{128,160},{160,192},{192,224},{1,3... | collective-permute-start | bytes 393224 | tf_op jit(solution)/shard_map/ppermute | solution.py:25
  138.8 13.8 %collective-permute-start.24 = (f32[1,32,1024]{2,1,0:T(8,128)S(1)}, f32[1,32,1024]{2,1,0:T(8,128)S(1)}, u32[]{:S(2)}, u32[]{:S(2)}) collective-permute-start(f32[1,32,1024]{2,1,0:T(8,128)S(1)} %get-tuple-element.17), channel_id=1, source_target_pairs={{32,0},{64,32},{96,64},{128,96},{160,128},{192,160},{224,192},{33,... | collective-permute-start | bytes 393224 | tf_op jit(solution)/shard_map/ppermute | solution.py:27
  142.4 6.3 %collective-permute-start.10 = (f32[8,24,128]{2,1,0:T(8,128)S(1)}, f32[8,24,128]{2,1,0:T(8,128)S(1)}, u32[]{:S(2)}, u32[]{:S(2)}) collective-permute-start(f32[8,24,128]{2,1,0:T(8,128)S(1)} %get-tuple-element.5), channel_id=1, source_target_pairs={{0,8},{8,16},{16,24},{24,0},{1,9},{9,17},{17,25},{25,1},{2,10},{10... | collective-permute-start | bytes 294920 | tf_op jit(solution)/shard_map/ppermute | solution.py:129
  144.0 7.5 %collective-permute-start.11 = (f32[8,24,128]{2,1,0:T(8,128)S(1)}, f32[8,24,128]{2,1,0:T(8,128)S(1)}, u32[]{:S(2)}, u32[]{:S(2)}) collective-permute-start(f32[8,24,128]{2,1,0:T(8,128)S(1)} %get-tuple-element.7), channel_id=1, source_target_pairs={{0,16},{8,24},{16,0},{24,8},{1,17},{9,25},{17,1},{25,9},{2,18},{10... | collective-permute-start | bytes 294920 | tf_op jit(solution)/shard_map/ppermute | solution.py:129
  147.0 4.6 %collective-permute-start.12 = (f32[8,24,128]{2,1,0:T(8,128)S(1)}, f32[8,24,128]{2,1,0:T(8,128)S(1)}, u32[]{:S(2)}, u32[]{:S(2)}) collective-permute-start(f32[8,24,128]{2,1,0:T(8,128)S(1)} %get-tuple-element.6), channel_id=1, source_target_pairs={{0,24},{8,0},{16,8},{24,16},{1,25},{9,1},{17,9},{25,17},{2,26},{10... | collective-permute-start | bytes 294920 | tf_op jit(solution)/shard_map/ppermute | solution.py:129
Sparse Core Ops, SparseCore 0:
  86.2 49.6 reduce-scatter.1
